TPU v7x, 512 devices: a whole 4x8x8 slice. The times are simulated.
512 devices in a mesh: chan: 16 (over x, y_lo, core), tile: 32 (over y_hi, z).
Axes of the slice: x: 4, y: 8 (y_hi: 4, y_lo: 2; y = y_hi * 2 + y_lo), z: 8, core: 2. Of those that a mesh axis runs over, the one named last changes fastest.
Arguments:
- channel_data: bfloat16 [16, 4096, 2048], P(None, 'tile', 'chan'), may hold values from -6 to 6
- delay_weights: bfloat16 [32, 16, 2048, 256], P('tile', None, 'chan'), may hold values from -0.046875 to 0.046875
- peak_lags: int32 [15, 128, 512], P(None, 'chan', 'tile'), may hold values from -15 to 15
- frame_pairs: int32 [15, 2], replicated, may hold values from 0 to 15, as said below
Outputs:
- quality: float32 [15, 128, 4096], P(None, 'chan', 'tile')
- strain: float32 [15, 128, 4096], P(None, 'chan', 'tile')
Inputs may be any that keep to these rules, and one draw needn't show every extreme that they name: `frame_pairs`: the pairs follow one random order of all 16 frames: pair i holds its i-th and (i+1)-th frame, so the two frames of a pair differ and every frame occurs.
All inputs are finite; a program needn't handle non-finite values.
Results may differ from a plain program's by a relative error of at most 0.0003.
Values may be sent and summed in bfloat16 or wider, within the bound.
No kernel may reach another device: no remote copies, remote signals or barrier semaphores. Data moves between devices by JAX's collectives and lax.ppermute only.
A program may use at most 64 MiB of HBM per device.

v0:
```python
import jax
import jax.numpy as jnp
from jax import lax
from jax.sharding import PartitionSpec as P

MAXLAG = 16
WIN = 32
BLK = 8


epsilon = 1e-05


def passed_along(block, axis, distance):
    devices = range(lax.axis_size(axis))
    route = [(i - distance, i) for i in devices if i - distance in devices]
    return lax.ppermute(block, axis, route)


def extended_2(cells, sides, width):
    for axis, dim in sides:
        count = lax.axis_size(axis)
        ends = count - 1
        head = lax.slice_in_dim(cells, 0, width, axis=dim)
        tail = lax.slice_in_dim(cells, cells.shape[dim] - width, cells.shape[dim], axis=dim)
        cells = jnp.concatenate(
            [
                lax.ppermute(tail, axis, [(i, (i + 1) % count) for i in range(ends)]),
                cells,
                lax.ppermute(head, axis, [((i + 1) % count, i) for i in range(ends)]),
            ],
            axis=dim,
        )
    return cells


def beamform(extended, weights, sample_rows):
    frame_count = extended.shape[0]

    def add_tap(tap_index, running):
        window = lax.dynamic_slice_in_dim(extended, tap_index, sample_rows, 1)
        return running + jnp.einsum(
            "fzc,cm->fmz", window, weights[tap_index], preferred_element_type=jnp.float32
        )

    start_sum = jnp.zeros((frame_count, weights.shape[2], sample_rows), jnp.float32)
    return lax.fori_loop(0, weights.shape[0], add_tap, start_sum)


def window_sum(values):
    span_len = values.shape[-1]
    out_len = span_len - WIN + 1
    rows_index = lax.broadcasted_iota(jnp.int32, (span_len, out_len), 0)
    cols_index = lax.broadcasted_iota(jnp.int32, (span_len, out_len), 1)
    band = ((rows_index >= cols_index) & (rows_index < cols_index + WIN)).astype(jnp.float32)
    return jnp.einsum(
        "...j,jz->...z",
        values,
        band,
        precision=lax.Precision.HIGHEST,
        preferred_element_type=jnp.float32,
    )


def shards(channel_data, delay_weights, peak_lags, frame_pairs):
    sample_rows = channel_data.shape[1]
    tap_count = delay_weights.shape[1]
    weights = delay_weights[0]
    rim_rows = passed_along(channel_data[:, : tap_count - 1, :], "tile", -1)
    extended = jnp.concatenate([channel_data, rim_rows], axis=1)
    volume = lax.psum_scatter(
        beamform(extended, weights, sample_rows), "chan", scatter_dimension=1, tiled=True
    )
    halo_reach = MAXLAG + WIN // 2
    padded = extended_2(volume, (("tile", 2),), halo_reach)
    line_count = padded.shape[1] // 2
    pair_count = frame_pairs.shape[0]
    front = padded[frame_pairs[:, 0]].reshape(pair_count, line_count, 2, -1)
    later_frame = padded[frame_pairs[:, 1]].reshape(pair_count, line_count, 2, -1)
    span_len = sample_rows + WIN - 1
    first_part = front[..., MAXLAG : MAXLAG + span_len]
    moved = jnp.stack(
        [
            later_frame[..., shift_start : shift_start + span_len]
            for shift_start in range(2 * MAXLAG + 1)
        ]
    )
    power_a = window_sum(jnp.sum(first_part * first_part, axis=2)) / (2 * WIN)
    cross_sum = window_sum(jnp.sum(first_part[None] * moved, axis=3))
    power_b = window_sum(jnp.sum(moved * moved, axis=3)) / (2 * WIN)
    scores = cross_sum / (2 * WIN * jnp.sqrt(power_a + epsilon)[None] * jnp.sqrt(power_b + epsilon))
    quality = jnp.max(scores, axis=0)
    peak_full = jnp.repeat(peak_lags, BLK, axis=2)
    lag_values = jnp.arange(-MAXLAG, MAXLAG + 1, dtype=jnp.int32)[:, None, None, None]

    def pick_lag(delta):
        return jnp.sum(
            jnp.where(lag_values == peak_full[None] + delta, scores, jnp.zeros_like(scores)), axis=0
        )

    at_prev = pick_lag(-1)
    centre = pick_lag(0)
    at_next = pick_lag(1)
    curvature = jnp.maximum(2.0 * centre - at_prev - at_next, 0.25)
    displacement = peak_full.astype(jnp.float32) + (at_next - at_prev) / (2.0 * curvature)
    disp_padded = extended_2(displacement, (("tile", 2),), 2)
    strain = (
        disp_padded[..., 0:sample_rows]
        - 8.0 * disp_padded[..., 1 : sample_rows + 1]
        + 8.0 * disp_padded[..., 3 : sample_rows + 3]
        - disp_padded[..., 4 : sample_rows + 4]
    ) / 12.0
    return (quality, strain)


def solution(mesh):
    return jax.shard_map(
        shards,
        mesh=mesh,
        in_specs=(
            P(None, "tile", "chan"),
            P("tile", None, "chan", None),
            P(None, "chan", "tile"),
            P(),
        ),
        out_specs=(P(None, "chan", "tile"), P(None, "chan", "tile")),
        check_vma=False,
    )
```

profile of v0, /device:TPU:32, one launch (start us, length us, event | category | flops | bytes accessed | tf_op | source)
XLA Modules:
  0.0 205.5 jit_solution(2628461334921635301)
XLA Ops:
  8.1 10.7 %collective-permute-start = (bf16[16,15,128]{2,1,0:T(8,128)(2,1)S(1)}, bf16[16,15,128]{2,1,0:T(8,128)(2,1)S(1)}, u32[]{:S(2)}, u32[]{:S(2)}) collective-permute-start(bf16[16,15,128]{2,1,0:T(8,128)(2,1)S(1)} %slice.139), channel_id=1, source_target_pairs={{1,0},{2,1},{3,2},{4,3},{5,4},{6,5},{7,6},{8,7},{9,8},{10,9},{11,1... | collective-permute-start | bytes 184328 | tf_op jit(solution)/shard_map/ppermute | solution.py:17
  18.8 2.3 %copy.13 = bf16[1,16,128,256]{2,3,1,0:T(8,128)(2,1)} copy(bf16[1,16,128,256]{3,2,1,0:T(8,128)(2,1)} %param.7) | data formatting | bytes 2097152 | tf_op args[1]
  21.3 1.1 pad_maximum_fusion
  22.4 29.7 %while.14 = (s32[]{:T(128)}, f32[16,256,128]{2,1,0:T(8,128)S(1)}, bf16[16,128,256]{1,2,0:T(8,128)(2,1)}, bf16[16,143,128]{2,1,0:T(8,128)(2,1)S(1)}, s32[]{:T(128)}, /*index=5*/s32[]{:T(128)}) while((s32[]{:T(128)}, f32[16,256,128]{2,1,0:T(8,128)S(1)}, bf16[16,128,256]{1,2,0:T(8,128)(2,1)}, bf16[16,143,128]{2,1,0:T(8,128)(2,1)S(1)}, ...), condition=%wide.region_1.0_spmd.clone, body=%wide.region_0.0_spmd.clone.sunk | while | flops 135266304 | bytes 4785231 | solution.py:47
  22.4 1.8 bitcast_add_fusion.4
  24.2 1.8 bitcast_add_fusion.4
  26.1 1.8 bitcast_add_fusion.4
  28.0 1.8 bitcast_add_fusion.4
  29.8 1.8 bitcast_add_fusion.4
  31.7 1.8 bitcast_add_fusion.4
  33.5 1.8 bitcast_add_fusion.4
  35.4 1.8 bitcast_add_fusion.4
  37.2 1.8 bitcast_add_fusion.4
  39.1 1.8 bitcast_add_fusion.4
  40.9 1.8 bitcast_add_fusion.4
  42.8 1.8 bitcast_add_fusion.4
  44.7 1.8 bitcast_add_fusion.4
  46.5 1.8 bitcast_add_fusion.4
  48.4 1.8 bitcast_add_fusion.4
  50.2 1.8 bitcast_add_fusion.4
  52.1 1.3 copy-done
  53.8 69.9 %reduce-scatter.2.cloned.1.call-done = f32[16,16,128]{2,1,0:T(8,128)} async-done(((f32[16,256,128]{2,1,0:T(8,128)}), f32[16,16,128]{2,1,0:T(8,128)}) %reduce-scatter.2.cloned.1.call-update) | async-done | bytes 131088 | tf_op jit(solution)/shard_map/reduce_scatter | solution.py:71
  124.8 3.8 %collective-permute-start.1 = (f32[16,16,32]{2,1,0:T(8,128)S(1)}, f32[16,16,32]{2,1,0:T(8,128)S(1)}, u32[]{:S(2)}, u32[]{:S(2)}) collective-permute-start(f32[16,16,32]{2,1,0:T(8,128)S(1)} %get-tuple-element.115), channel_id=1, source_target_pairs={{0,1},{1,2},{2,3},{3,4},{4,5},{5,6},{6,7},{7,8},{8,9},{9,10},{10,1... | collective-permute-start | bytes 98312 | tf_op jit(solution)/shard_map/ppermute | solution.py:28
  128.6 6.3 %collective-permute-start.2 = (f32[16,16,32]{2,1,0:T(8,128)S(1)}, f32[16,16,32]{2,1,0:T(8,128)S(1)}, u32[]{:S(2)}, u32[]{:S(2)}) collective-permute-start(f32[16,16,32]{2,1,0:T(8,128)S(1)} %get-tuple-element.116), channel_id=1, source_target_pairs={{1,0},{2,1},{3,2},{4,3},{5,4},{6,5},{7,6},{8,7},{9,8},{10,9},{11,1... | collective-permute-start | bytes 98312 | tf_op jit(solution)/shard_map/ppermute | solution.py:30
  135.9 1.5 collective-permute-done.2
  151.2 3.1 %copy-done.1 = f32[33,15,8,2,159]{4,3,2,1,0:T(2,128)} copy-done((f32[33,15,8,2,159]{4,3,2,1,0:T(2,128)}, f32[33,15,8,2,159]{4,3,2,1,0:T(2,128)S(1)}, u32[]{:S(2)}) %copy-start.1) | copy-done | bytes 5037144
  155.4 23.7 %multiply_reduce_fusion = (f32[33,15,8,159]{3,2,1,0:T(8,128)S(1)}, f32[33,15,8,159]{3,2,1,0:T(8,128)S(1)}) fusion(f32[33,15,8,2,159]{4,3,2,1,0:T(2,128)} %copy-done.1, f32[15,8,2,159]{3,2,1,0:T(2,128)S(1)} %get-tuple-element.114), kind=kLoop, calls=%fused_computation.7 | loop fusion | flops 3777840 | bytes 10226880 | tf_op jit(solution)/shard_map/reduce_sum | solution.py:90
  179.1 2.1 %fusion.42 = f32[33,15,8,128]{3,2,1,0:T(8,128)S(1)} fusion(f32[33,15,8,159]{3,2,1,0:T(8,128)S(1)} %get-tuple-element.100, s32[128]{0:T(128)S(1)} %iota_add_fusion.1), kind=kOutput, calls=%fused_computation.97 | convolution fusion | flops 967188096 | bytes 4546592 | tf_op jit(solution)/shard_map/...j,jz->...z/dot_general | solution.py:56
  181.5 3.9 %select_reduce_fusion = (f32[15,8,128]{2,1,0:T(8,128)S(1)}, f32[15,8,128]{2,1,0:T(8,128)S(1)}, f32[15,8,128]{2,1,0:T(8,128)S(1)}, f32[15,8,128]{2,1,0:T(8,128)}) fusion(s32[15,8,128]{2,1,0:T(8,128)S(1)} %copy.15, s32[33]{0:T(128)S(1)} %iota_add_fusion, s32[15,8,128]{2,1,0:T(8,128)S(1)} %copy.17, s32[15,8,128]{2,1,0:T(8,128)S(1)} %copy.16, ...), kind=kOutput, calls=%fused_computation.9 | convolution fusion | flops 974222976 | bytes 5038244 | tf_op jit(solution)/shard_map/...j,jz->...z/dot_general | solution.py:56
  185.5 1.9 collective-permute-start.3
  187.4 8.6 %collective-permute-start.4 = (f32[15,8,2]{2,1,0:T(8,128)S(1)}, f32[15,8,2]{2,1,0:T(8,128)S(1)}, u32[]{:S(2)}, u32[]{:S(2)}) collective-permute-start(f32[15,8,2]{2,1,0:T(8,128)S(1)} %get-tuple-element.120), channel_id=1, source_target_pairs={{1,0},{2,1},{3,2},{4,3},{5,4},{6,5},{7,6},{8,7},{9,8},{10,9},{11,1... | collective-permute-start | bytes 2888 | tf_op jit(solution)/shard_map/ppermute | solution.py:30
  196.2 1.6 collective-permute-done.4
  (67 shorter events, 19.7 us)
Async XLA Ops:
  7.2 116.5 %reduce-scatter.2.cloned.1.call-start = ((), (), s32[]{:S(2)}) async-start(), calls=%async_computation.1 | async-start | bytes 2228224 | tf_op jit(solution)/shard_map/reduce_scatter | solution.py:71
  8.1 13.2 %collective-permute-start = (bf16[16,15,128]{2,1,0:T(8,128)(2,1)S(1)}, bf16[16,15,128]{2,1,0:T(8,128)(2,1)S(1)}, u32[]{:S(2)}, u32[]{:S(2)}) collective-permute-start(bf16[16,15,128]{2,1,0:T(8,128)(2,1)S(1)} %slice.139), channel_id=1, source_target_pairs={{1,0},{2,1},{3,2},{4,3},{5,4},{6,5},{7,6},{8,7},{9,8},{10,9},{11,1... | collective-permute-start | bytes 184328 | tf_op jit(solution)/shard_map/ppermute | solution.py:17
  22.3 31.1 %copy-start.2 = (s32[15,8,16]{2,1,0:T(8,128)S(1)}, s32[15,8,16]{2,1,0:T(8,128)}, u32[]{:S(2)}) copy-start(s32[15,8,16]{2,1,0:T(8,128)} %param.8) | copy-start | bytes 23044
  22.4 31.2 %copy-start.3 = (s32[15,2]{0,1:T(2,128)S(1)}, s32[15,2]{0,1:T(2,128)}, u32[]{:S(2)}) copy-start(s32[15,2]{0,1:T(2,128)} %param.9) | copy-start | bytes 364
  52.1 1.4 copy-start
  124.8 11.1 %collective-permute-start.1 = (f32[16,16,32]{2,1,0:T(8,128)S(1)}, f32[16,16,32]{2,1,0:T(8,128)S(1)}, u32[]{:S(2)}, u32[]{:S(2)}) collective-permute-start(f32[16,16,32]{2,1,0:T(8,128)S(1)} %get-tuple-element.115), channel_id=1, source_target_pairs={{0,1},{1,2},{2,3},{3,4},{4,5},{5,6},{6,7},{7,8},{8,9},{9,10},{10,1... | collective-permute-start | bytes 98312 | tf_op jit(solution)/shard_map/ppermute | solution.py:28
  128.6 8.8 %collective-permute-start.2 = (f32[16,16,32]{2,1,0:T(8,128)S(1)}, f32[16,16,32]{2,1,0:T(8,128)S(1)}, u32[]{:S(2)}, u32[]{:S(2)}) collective-permute-start(f32[16,16,32]{2,1,0:T(8,128)S(1)} %get-tuple-element.116), channel_id=1, source_target_pairs={{1,0},{2,1},{3,2},{4,3},{5,4},{6,5},{7,6},{8,7},{9,8},{10,9},{11,1... | collective-permute-start | bytes 98312 | tf_op jit(solution)/shard_map/ppermute | solution.py:30
  151.2 3.1 %copy-start.1 = (f32[33,15,8,2,159]{4,3,2,1,0:T(2,128)}, f32[33,15,8,2,159]{4,3,2,1,0:T(2,128)S(1)}, u32[]{:S(2)}) copy-start(f32[33,15,8,2,159]{4,3,2,1,0:T(2,128)S(1)} %fusion.7) | copy-start | bytes 15111364
  185.5 10.8 %collective-permute-start.3 = (f32[15,8,2]{2,1,0:T(8,128)S(1)}, f32[15,8,2]{2,1,0:T(8,128)S(1)}, u32[]{:S(2)}, u32[]{:S(2)}) collective-permute-start(f32[15,8,2]{2,1,0:T(8,128)S(1)} %get-tuple-element.119), channel_id=1, source_target_pairs={{0,1},{1,2},{2,3},{3,4},{4,5},{5,6},{6,7},{7,8},{8,9},{9,10},{10,1... | collective-permute-start | bytes 2888 | tf_op jit(solution)/shard_map/ppermute | solution.py:28
  187.4 10.4 %collective-permute-start.4 = (f32[15,8,2]{2,1,0:T(8,128)S(1)}, f32[15,8,2]{2,1,0:T(8,128)S(1)}, u32[]{:S(2)}, u32[]{:S(2)}) collective-permute-start(f32[15,8,2]{2,1,0:T(8,128)S(1)} %get-tuple-element.120), channel_id=1, source_target_pairs={{1,0},{2,1},{3,2},{4,3},{5,4},{6,5},{7,6},{8,7},{9,8},{10,9},{11,1... | collective-permute-start | bytes 2888 | tf_op jit(solution)/shard_map/ppermute | solution.py:30
Sparse Core Ops, SparseCore 0:
  53.6 70.0 reduce-scatter.1
where the time goes:
time: 207 us; the launch traced here: 205 us
  waiting for transfers between devices  73.9 us (36%)
  matrix products  35.5 us (17%)
  starting transfers between devices  31.3 us (15%)
  other arithmetic  27.2 us (13%)
  local copies, waits for them, and re-layouts  22.9 us (11%)
  between operations  14.3 us (7%)
    reduce_scatter x1, waiting for transfers between devices, shards(): lax.psum_scatter(beamform(extended, weights, sample_rows), 'chan', scatte...  69.9 us
    dot_general x16, matrix products, add_tap(): jnp.einsum('fzc,cm->fmz', window, weights[tap_index], preferred_element_t...  29.3 us
    reduce_sum x1, other arithmetic, shards(): power_b = window_sum(jnp.sum(moved * moved, axis=3)) / (2 * WIN)  23.7 us
    unnamed x42, local copies, waits for them, and re-layouts  18.5 us
    ppermute x2, starting transfers between devices, extended_2(): lax.ppermute(head, axis, [((i + 1) % count, i) for i in range(ends)])  14.9 us
    ppermute x1, starting transfers between devices, passed_along(): return lax.ppermute(block, axis, route)  10.7 us
    dot_general x3, matrix products, window_sum(): jnp.einsum('...j,jz->...z', values, band, precision=lax.Precision.HIGHEST...  6.18 us
    ppermute x2, starting transfers between devices, extended_2(): lax.ppermute(tail, axis, [(i, (i + 1) % count) for i in range(ends)])  5.69 us
  transfers between devices with their start and end apart: 6, of which 6 were waited for; matrix products, arithmetic and copies ran while one was open for 2% of the time, Pallas kernels for 0%

commit v1 on v0

v1 whole, which is shorter than its diff:
```python
import jax
import jax.numpy as jnp
from jax import lax
from jax.sharding import Mesh, PartitionSpec as P

MAXLAG = 16
WIN = 32
BLK = 8
HALO = MAXLAG + WIN // 2 + 2

epsilon = 1e-05

CHAN = ("cx", "cy", "cc")


def window_sum(values):
    width = 1
    while width < WIN:
        n = values.shape[-1] - width
        values = values[..., :n] + values[..., width : width + n]
        width *= 2
    return values


def from_left(block, axis):
    count = lax.axis_size(axis)
    return lax.ppermute(block, axis, [(i, i + 1) for i in range(count - 1)])


def from_right(block, axis):
    count = lax.axis_size(axis)
    return lax.ppermute(block, axis, [(i + 1, i) for i in range(count - 1)])


def beamform(extended, weights):
    return lax.conv_general_dilated(
        extended,
        weights,
        window_strides=(1,),
        padding="VALID",
        dimension_numbers=("NWC", "WIO", "NCW"),
        preferred_element_type=jnp.float32,
    )


def shards(channel_data, delay_weights, peak_lags, frame_pairs):
    frames, sample_rows, _ = channel_data.shape
    tap_count = delay_weights.shape[1]
    nx, ny, nc = (lax.axis_size(a) for a in CHAN)
    tile = lax.axis_index("tile")
    tiles = lax.axis_size("tile")

    lag_f = peak_lags.astype(jnp.float32)
    lag_prev = from_left(lag_f[:, :, -1:], "tile")
    lag_next = from_right(lag_f[:, :, :1], "tile")

    rim_rows = from_right(channel_data[:, : tap_count - 1, :], "tile")
    extended = jnp.concatenate([channel_data, rim_rows], axis=1)

    weights = delay_weights[0]
    taps, cin, cols = weights.shape
    per_dev = cols // (nx * ny * nc)
    w6 = weights.reshape(taps, cin, nx, ny, nc, per_dev)
    core = lax.axis_index("cc")
    w_mine = lax.dynamic_index_in_dim(w6, core, 4, keepdims=False).reshape(taps, cin, -1)
    w_other = lax.dynamic_index_in_dim(w6, 1 - core, 4, keepdims=False).reshape(taps, cin, -1)
    vol_other = beamform(extended, w_other)
    vol_mine = beamform(extended, w_mine)
    vol = vol_mine + lax.ppermute(vol_other, "cc", [(0, 1), (1, 0)])
    vol = vol.reshape(frames, nx * ny, per_dev, sample_rows)
    vol = lax.all_to_all(vol, ("cx", "cy"), 1, 1, tiled=True).sum(axis=1)

    head = vol[..., :HALO]
    tail = vol[..., sample_rows - HALO :]
    padded = jnp.concatenate([from_left(tail, "tile"), vol, from_right(head, "tile")], axis=2)

    line_count = per_dev // 2
    pair_count = frame_pairs.shape[0]
    front = padded[frame_pairs[:, 0]].reshape(pair_count, line_count, 2, -1)
    later = padded[frame_pairs[:, 1]].reshape(pair_count, line_count, 2, -1)
    out_len = sample_rows + 4
    prod_len = out_len + WIN - 1
    xr = front[:, :, 0, WIN // 2 : WIN // 2 + prod_len]
    xi = front[:, :, 1, WIN // 2 : WIN // 2 + prod_len]
    yr = later[:, :, 0]
    yi = later[:, :, 1]
    nlag = 2 * MAXLAG + 1
    prods = jnp.stack(
        [xr * yr[..., j : j + prod_len] + xi * yi[..., j : j + prod_len] for j in range(nlag)]
    )
    cross_sum = window_sum(prods)
    power_a = window_sum(xr * xr + xi * xi) / (2 * WIN)
    ey = yr * yr + yi * yi
    power_full = window_sum(ey[..., : out_len + nlag - 1 + WIN - 1]) / (2 * WIN)
    root_b = jnp.sqrt(power_full + epsilon)
    root_b = jnp.stack([root_b[..., j : j + out_len] for j in range(nlag)])
    scores = cross_sum / (2 * WIN * jnp.sqrt(power_a + epsilon)[None] * root_b)
    quality = jnp.max(scores[..., 2 : 2 + sample_rows], axis=0)

    own = jnp.repeat(lag_f, BLK, axis=2)
    peak_full = jnp.concatenate(
        [jnp.repeat(lag_prev, 2, axis=2), own, jnp.repeat(lag_next, 2, axis=2)], axis=2
    ).astype(jnp.int32)
    lag_values = jnp.arange(-MAXLAG, MAXLAG + 1, dtype=jnp.int32)[:, None, None, None]

    def pick_lag(delta):
        return jnp.sum(
            jnp.where(lag_values == peak_full[None] + delta, scores, jnp.zeros_like(scores)), axis=0
        )

    at_prev = pick_lag(-1)
    centre = pick_lag(0)
    at_next = pick_lag(1)
    curvature = jnp.maximum(2.0 * centre - at_prev - at_next, 0.25)
    displacement = peak_full.astype(jnp.float32) + (at_next - at_prev) / (2.0 * curvature)
    zo = lax.broadcasted_iota(jnp.int32, displacement.shape, 2)
    outside = ((tile == 0) & (zo < 2)) | ((tile == tiles - 1) & (zo >= sample_rows + 2))
    dz = jnp.where(outside, 0.0, displacement)
    strain = (
        dz[..., 0:sample_rows]
        - 8.0 * dz[..., 1 : sample_rows + 1]
        + 8.0 * dz[..., 3 : sample_rows + 3]
        - dz[..., 4 : sample_rows + 4]
    ) / 12.0
    return (quality, strain)


def solution(mesh):
    chan = mesh.shape["chan"]
    tile = mesh.shape["tile"]
    devices = mesh.devices.reshape(chan // 4, 2, 2, tile)
    fine = Mesh(devices, CHAN + ("tile",))
    return jax.shard_map(
        shards,
        mesh=fine,
        in_specs=(
            P(None, "tile", CHAN),
            P("tile", None, CHAN, None),
            P(None, CHAN, "tile"),
            P(),
        ),
        out_specs=(P(None, CHAN, "tile"), P(None, CHAN, "tile")),
        check_vma=False,
    )
```

time: 207 us -> 86.4 us (0.42)
  the two profiles are of different devices: /device:TPU:32 before, /device:TPU:36 now
where the time goes in v1:
time: 86.4 us; the launch traced here: 86 us
  starting transfers between devices  38.8 us (45%)
  other arithmetic  15.1 us (17%)
  waiting for transfers between devices  14.1 us (16%)
  local copies, waits for them, and re-layouts  11.8 us (14%)
  matrix products  4.69 us (5%)
  between operations  1.52 us (2%)
    ppermute x3, starting transfers between devices, from_right(): return lax.ppermute(block, axis, [(i + 1, i) for i in range(count - 1)])  27.2 us
    ppermute x2, waiting for transfers between devices, from_left(): return lax.ppermute(block, axis, [(i, i + 1) for i in range(count - 1)])  9.97 us
    unnamed x41, local copies, waits for them, and re-layouts  5.96 us
    all_to_all x1, starting transfers between devices, shards(): vol = lax.all_to_all(vol, ('cx', 'cy'), 1, 1, tiled=True).sum(axis=1)  5.82 us
    add x12, other arithmetic, window_sum(): values = values[..., :n] + values[..., width:width + n]  5.24 us
    conv_general_dilated x2, matrix products, beamform(): lax.conv_general_dilated(extended, weights, window_strides=(1,), padding=...  4.69 us
    unnamed x32, other arithmetic  4.24 us
    ppermute x2, starting transfers between devices, from_left(): return lax.ppermute(block, axis, [(i, i + 1) for i in range(count - 1)])  3.84 us
  transfers between devices with their start and end apart: 7, of which 4 were waited for; matrix products, arithmetic and copies ran while one was open for 5% of the time, Pallas kernels for 0%

profile of v1, /device:TPU:36, one launch (start us, length us, event | category | flops | bytes accessed | tf_op | source)
XLA Modules:
  0.0 86.0 jit_solution(5989407166368859803)
XLA Ops:
  0.6 0.9 slice.587
  1.5 10.7 %collective-permute-start = (bf16[16,15,128]{2,0,1:T(8,128)(2,1)S(1)}, bf16[16,15,128]{2,0,1:T(8,128)(2,1)S(1)}, u32[]{:S(2)}, u32[]{:S(2)}) collective-permute-start(bf16[16,15,128]{2,0,1:T(8,128)(2,1)S(1)} %copy.196), channel_id=1, source_target_pairs={{1,0},{2,1},{3,2},{4,3},{5,4},{6,5},{7,6},{8,7},{9,8},{10,9},{11,1... | collective-permute-start | bytes 184328 | tf_op jit(solution)/shard_map/ppermute | solution.py:32
  12.2 1.4 %constant_dynamic-update-slice_fusion.1 = bf16[16,143,128]{2,0,1:T(8,128)(2,1)S(1)} fusion(bf16[16,128,128]{2,1,0:T(8,128)(2,1)} %param.4), kind=kLoop, calls=%fused_computation.16 | loop fusion | bytes 1048576
  13.6 1.6 %copy.68 = bf16[1,16,128,256]{2,3,1,0:T(8,128)(2,1)S(1)} copy(bf16[1,16,128,256]{3,2,1,0:T(8,128)(2,1)} %param.5) | data formatting | bytes 2097152 | tf_op args[1]
  15.3 0.2 constant_dynamic-slice_fusion.1
  15.5 2.3 %fusion.85 = f32[16,128,128]{1,0,2:T(8,128)S(1)} fusion(bf16[16,143,128]{2,0,1:T(8,128)(2,1)S(1)} %constant_dynamic-update-slice_fusion, bf16[16,128,128]{1,2,0:T(8,128)(2,1)S(1)} %bitcast.468), kind=kOutput, calls=%fused_computation.295 | convolution fusion | flops 1073741824 | bytes 2158592 | tf_op jit(solution)/shard_map/conv_general_dilated | solution.py:36
  17.9 1.9 %collective-permute-start.1 = (f32[16,128,128]{1,0,2:T(8,128)S(1)}, f32[16,128,128]{1,0,2:T(8,128)S(1)}, u32[]{:S(2)}, u32[]{:S(2)}) collective-permute-start(f32[16,128,128]{1,0,2:T(8,128)S(1)} %fusion.85), channel_id=1, source_target_pairs={{0,32},{32,0},{1,33},{33,1},{2,34},{34,2},{3,35},{35,3},{4,36},{36... | collective-permute-start | bytes 3145736 | tf_op jit(solution)/shard_map/ppermute | solution.py:69
  19.8 2.6 %collective-permute-done.1 = f32[16,128,128]{1,0,2:T(8,128)S(1)} collective-permute-done((f32[16,128,128]{1,0,2:T(8,128)S(1)}, f32[16,128,128]{1,0,2:T(8,128)S(1)}, u32[]{:S(2)}, u32[]{:S(2)}) %collective-permute-start.1) | collective-permute-done | bytes 1048608 | tf_op jit(solution)/shard_map/ppermute | solution.py:69
  22.4 2.3 %convolution_add_fusion = f32[16,128,128]{1,0,2:T(8,128)S(1)} fusion(f32[16,128,128]{1,0,2:T(8,128)S(1)} %collective-permute-done.1, bf16[16,143,128]{2,0,1:T(8,128)(2,1)S(1)} %constant_dynamic-update-slice_fusion, bf16[16,128,128]{1,2,0:T(8,128)(2,1)S(1)} %bitcast.467), kind=kOutput, calls=%fused_computation.12 | convolution fusion | flops 1074003968 | bytes 3207168 | tf_op jit(solution)/shard_map/conv_general_dilated | solution.py:36
  24.8 0.4 copy.69
  25.2 1.1 %copy.70 = f32[16,8,16,128]{3,2,0,1:T(8,128)} copy(f32[16,8,16,128]{3,2,1,0:T(8,128)S(1)} %bitcast.465) | data formatting | bytes 2097152 | tf_op jit(solution)/shard_map/reshape | solution.py:70
  26.3 5.8 %all-to-all-start = ((f32[16,8,16,128]{3,2,0,1:T(8,128)}), f32[16,8,16,128]{3,2,0,1:T(8,128)S(1)}, u32[]{:S(2)}, u32[]{:S(2)}) async-start(f32[16,8,16,128]{3,2,0,1:T(8,128)} %copy.70), calls=%async_computation | async-start | bytes 2097152 | tf_op jit(solution)/shard_map/all_to_all | solution.py:71
  32.2 1.9 %collective-permute-start.4 = (f32[15,8,1]{2,1,0:T(8,128)S(1)}, f32[15,8,1]{2,1,0:T(8,128)S(1)}, u32[]{:S(2)}, u32[]{:S(2)}) collective-permute-start(f32[15,8,1]{2,1,0:T(8,128)S(1)} %get-tuple-element.18), channel_id=1, source_target_pairs={{0,1},{1,2},{2,3},{3,4},{4,5},{5,6},{6,7},{7,8},{8,9},{9,10},{10,1... | collective-permute-start | bytes 1448 | tf_op jit(solution)/shard_map/ppermute | solution.py:27
  34.1 8.1 %collective-permute-start.5 = (f32[15,8,1]{2,1,0:T(8,128)S(1)}, f32[15,8,1]{2,1,0:T(8,128)S(1)}, u32[]{:S(2)}, u32[]{:S(2)}) collective-permute-start(f32[15,8,1]{2,1,0:T(8,128)S(1)} %get-tuple-element.19), channel_id=1, source_target_pairs={{1,0},{2,1},{3,2},{4,3},{5,4},{6,5},{7,6},{8,7},{9,8},{10,9},{11,1... | collective-permute-start | bytes 1448 | tf_op jit(solution)/shard_map/ppermute | solution.py:32
  42.5 0.2 copy.79
  42.7 9.3 %collective-permute-done.4 = f32[15,8,1]{2,1,0:T(8,128)S(1)} collective-permute-done((f32[15,8,1]{2,1,0:T(8,128)S(1)}, f32[15,8,1]{2,1,0:T(8,128)S(1)}, u32[]{:S(2)}, u32[]{:S(2)}) %collective-permute-start.4) | collective-permute-done | bytes 512 | tf_op jit(solution)/shard_map/ppermute | solution.py:27
  52.8 1.9 %collective-permute-start.2 = (f32[16,16,34]{2,1,0:T(8,128)S(1)}, f32[16,16,34]{2,1,0:T(8,128)S(1)}, u32[]{:S(2)}, u32[]{:S(2)}) collective-permute-start(f32[16,16,34]{2,1,0:T(8,128)S(1)} %get-tuple-element.16), channel_id=1, source_target_pairs={{0,1},{1,2},{2,3},{3,4},{4,5},{5,6},{6,7},{7,8},{8,9},{9,10},{10,1... | collective-permute-start | bytes 104456 | tf_op jit(solution)/shard_map/ppermute | solution.py:27
  54.7 8.3 %collective-permute-start.3 = (f32[16,16,34]{2,1,0:T(8,128)S(1)}, f32[16,16,34]{2,1,0:T(8,128)S(1)}, u32[]{:S(2)}, u32[]{:S(2)}) collective-permute-start(f32[16,16,34]{2,1,0:T(8,128)S(1)} %get-tuple-element.17), channel_id=1, source_target_pairs={{1,0},{2,1},{3,2},{4,3},{5,4},{6,5},{7,6},{8,7},{9,8},{10,9},{11,1... | collective-permute-start | bytes 104456 | tf_op jit(solution)/shard_map/ppermute | solution.py:32
  63.2 0.7 collective-permute-done.2
  63.9 1.5 %collective-permute-done.3 = f32[16,16,34]{2,1,0:T(8,128)S(1)} collective-permute-done((f32[16,16,34]{2,1,0:T(8,128)S(1)}, f32[16,16,34]{2,1,0:T(8,128)S(1)}, u32[]{:S(2)}, u32[]{:S(2)}) %collective-permute-start.3) | collective-permute-done | bytes 34848 | tf_op jit(solution)/shard_map/ppermute | solution.py:32
  65.4 0.2 pad_maximum_fusion
  65.5 0.6 gather_fusion.1
  66.3 0.2 fusion.82
  66.5 0.6 gather_fusion
  67.2 0.6 fusion.81
  72.5 1.1 %slice_add_fusion.4 = f32[33,15,8,162]{3,2,1,0:T(8,128)S(1)} fusion(f32[33,15,8,163]{3,2,1,0:T(8,128)S(1)} %constant_dynamic-update-slice_fusion.2), kind=kLoop, calls=%fused_computation.7 | loop fusion | flops 641520 | bytes 7698240 | tf_op jit(solution)/shard_map/add | solution.py:20
  73.6 1.1 %slice_add_fusion.3 = f32[33,15,8,160]{3,2,1,0:T(8,128)S(1)} fusion(f32[33,15,8,162]{3,2,1,0:T(8,128)S(1)} %slice_add_fusion.4), kind=kLoop, calls=%fused_computation.6 | loop fusion | flops 633600 | bytes 7603200 | tf_op jit(solution)/shard_map/add | solution.py:20
  74.7 1.1 %slice_add_fusion.2 = f32[33,15,8,156]{3,2,1,0:T(8,128)S(1)} fusion(f32[33,15,8,160]{3,2,1,0:T(8,128)S(1)} %slice_add_fusion.3), kind=kLoop, calls=%fused_computation.5 | loop fusion | flops 617760 | bytes 7413120 | tf_op jit(solution)/shard_map/add | solution.py:20
  75.8 1.1 %slice_add_fusion.1 = f32[33,15,8,148]{3,2,1,0:T(8,128)S(1)} fusion(f32[33,15,8,156]{3,2,1,0:T(8,128)S(1)} %slice_add_fusion.2), kind=kLoop, calls=%fused_computation.4 | loop fusion | flops 586080 | bytes 7032960 | tf_op jit(solution)/shard_map/add | solution.py:20
  81.3 2.6 %select_reduce_fusion = (f32[15,8,132]{2,1,0:T(8,128)S(1)}, f32[15,8,132]{2,1,0:T(8,128)S(1)}, f32[15,8,132]{2,1,0:T(8,128)S(1)}, f32[33,15,8,132]{3,2,1,0:T(8,128)S(1)}) fusion(s32[15,8,132]{2,1,0:T(8,128)S(1)} %maximum_convert_fusion, s32[33]{0:T(128)S(1)} %iota_add_fusion, s32[15,8,132]{2,1,0:T(8,128)S(1)} %get-tuple-element.15, ...), kind=kLoop, calls=%fused_computation.8 | loop fusion | flops 6225120 | bytes 8807172 | tf_op jit(solution)/shard_map/reduce_sum | solution.py:107
  84.0 0.7 fusion.75
  84.7 1.2 %slice_reduce_fusion = f32[15,8,128]{2,1,0:T(8,128)} fusion(f32[33,15,8,132]{3,2,1,0:T(8,128)S(1)} %get-tuple-element.7), kind=kLoop, calls=%fused_computation.11 | loop fusion | flops 491520 | bytes 2088960 | tf_op jit(solution)/shard_map/reduce_max | solution.py:98
  (108 shorter events, 10.1 us)
Async XLA Ops:
  1.5 14.0 %collective-permute-start = (bf16[16,15,128]{2,0,1:T(8,128)(2,1)S(1)}, bf16[16,15,128]{2,0,1:T(8,128)(2,1)S(1)}, u32[]{:S(2)}, u32[]{:S(2)}) collective-permute-start(bf16[16,15,128]{2,0,1:T(8,128)(2,1)S(1)} %copy.196), channel_id=1, source_target_pairs={{1,0},{2,1},{3,2},{4,3},{5,4},{6,5},{7,6},{8,7},{9,8},{10,9},{11,1... | collective-permute-start | bytes 184328 | tf_op jit(solution)/shard_map/ppermute | solution.py:32
  17.9 4.6 %collective-permute-start.1 = (f32[16,128,128]{1,0,2:T(8,128)S(1)}, f32[16,128,128]{1,0,2:T(8,128)S(1)}, u32[]{:S(2)}, u32[]{:S(2)}) collective-permute-start(f32[16,128,128]{1,0,2:T(8,128)S(1)} %fusion.85), channel_id=1, source_target_pairs={{0,32},{32,0},{1,33},{33,1},{2,34},{34,2},{3,35},{35,3},{4,36},{36... | collective-permute-start | bytes 3145736 | tf_op jit(solution)/shard_map/ppermute | solution.py:69
  24.8 7.3 %copy-start = (s32[15,8,16]{2,1,0:T(8,128)S(1)}, s32[15,8,16]{2,1,0:T(8,128)}, u32[]{:S(2)}) copy-start(s32[15,8,16]{2,1,0:T(8,128)} %param.6) | copy-start | bytes 23044
  24.8 17.6 %copy-start.1 = (s32[15,2]{0,1:T(2,128)S(1)}, s32[15,2]{0,1:T(2,128)}, u32[]{:S(2)}) copy-start(s32[15,2]{0,1:T(2,128)} %param.7) | copy-start | bytes 364
  26.3 26.3 %all-to-all-start = ((f32[16,8,16,128]{3,2,0,1:T(8,128)}), f32[16,8,16,128]{3,2,0,1:T(8,128)S(1)}, u32[]{:S(2)}, u32[]{:S(2)}) async-start(f32[16,8,16,128]{3,2,0,1:T(8,128)} %copy.70), calls=%async_computation | async-start | bytes 2097152 | tf_op jit(solution)/shard_map/all_to_all | solution.py:71
  32.2 19.8 %collective-permute-start.4 = (f32[15,8,1]{2,1,0:T(8,128)S(1)}, f32[15,8,1]{2,1,0:T(8,128)S(1)}, u32[]{:S(2)}, u32[]{:S(2)}) collective-permute-start(f32[15,8,1]{2,1,0:T(8,128)S(1)} %get-tuple-element.18), channel_id=1, source_target_pairs={{0,1},{1,2},{2,3},{3,4},{4,5},{5,6},{6,7},{7,8},{8,9},{9,10},{10,1... | collective-permute-start | bytes 1448 | tf_op jit(solution)/shard_map/ppermute | solution.py:27
  34.1 18.0 %collective-permute-start.5 = (f32[15,8,1]{2,1,0:T(8,128)S(1)}, f32[15,8,1]{2,1,0:T(8,128)S(1)}, u32[]{:S(2)}, u32[]{:S(2)}) collective-permute-start(f32[15,8,1]{2,1,0:T(8,128)S(1)} %get-tuple-element.19), channel_id=1, source_target_pairs={{1,0},{2,1},{3,2},{4,3},{5,4},{6,5},{7,6},{8,7},{9,8},{10,9},{11,1... | collective-permute-start | bytes 1448 | tf_op jit(solution)/shard_map/ppermute | solution.py:32
  52.8 11.1 %collective-permute-start.2 = (f32[16,16,34]{2,1,0:T(8,128)S(1)}, f32[16,16,34]{2,1,0:T(8,128)S(1)}, u32[]{:S(2)}, u32[]{:S(2)}) collective-permute-start(f32[16,16,34]{2,1,0:T(8,128)S(1)} %get-tuple-element.16), channel_id=1, source_target_pairs={{0,1},{1,2},{2,3},{3,4},{4,5},{5,6},{6,7},{7,8},{8,9},{9,10},{10,1... | collective-permute-start | bytes 104456 | tf_op jit(solution)/shard_map/ppermute | solution.py:27
  54.7 10.6 %collective-permute-start.3 = (f32[16,16,34]{2,1,0:T(8,128)S(1)}, f32[16,16,34]{2,1,0:T(8,128)S(1)}, u32[]{:S(2)}, u32[]{:S(2)}) collective-permute-start(f32[16,16,34]{2,1,0:T(8,128)S(1)} %get-tuple-element.17), channel_id=1, source_target_pairs={{1,0},{2,1},{3,2},{4,3},{5,4},{6,5},{7,6},{8,7},{9,8},{10,9},{11,1... | collective-permute-start | bytes 104456 | tf_op jit(solution)/shard_map/ppermute | solution.py:32

commit v2 on v1

--- a/solution.py
+++ b/solution.py
@@ -1,25 +1,76 @@
 import jax
 import jax.numpy as jnp
 from jax import lax
+from jax.experimental import pallas as pl
+from jax.experimental.pallas import tpu as pltpu
 from jax.sharding import Mesh, PartitionSpec as P
 
 MAXLAG = 16
 WIN = 32
 BLK = 8
 HALO = MAXLAG + WIN // 2 + 2
+LANES = 256
 
 epsilon = 1e-05
 
 CHAN = ("cx", "cy", "cc")
 
 
-def window_sum(values):
+def _wsum(a):
     width = 1
     while width < WIN:
-        n = values.shape[-1] - width
-        values = values[..., :n] + values[..., width : width + n]
+        a = a + pltpu.roll(a, LANES - width, 1)
         width *= 2
-    return values
+    return a
+
+
+def corr_kernel(fp_ref, v_ref, peak_ref, q_ref, d_ref):
+    def pair(p, carry):
+        fa = fp_ref[p, 0]
+        fb = fp_ref[p, 1]
+        xr = pltpu.roll(v_ref[fa, 0], LANES - WIN // 2, 1)
+        xi = pltpu.roll(v_ref[fa, 1], LANES - WIN // 2, 1)
+        yr = v_ref[fb, 0]
+        yi = v_ref[fb, 1]
+        root_a = jnp.sqrt(_wsum(xr * xr + xi * xi) / (2 * WIN) + epsilon)
+        root_full = jnp.sqrt(_wsum(yr * yr + yi * yi) / (2 * WIN) + epsilon)
+        scale_a = 2 * WIN * root_a
+        want = peak_ref[p] + MAXLAG
+        best = None
+        prv = jnp.zeros_like(xr)
+        cen = jnp.zeros_like(xr)
+        nxt = jnp.zeros_like(xr)
+        for j in range(2 * MAXLAG + 1):
+            sh = (LANES - j) % LANES
+            yrj = pltpu.roll(yr, sh, 1) if sh else yr
+            yij = pltpu.roll(yi, sh, 1) if sh else yi
+            rbj = pltpu.roll(root_full, sh, 1) if sh else root_full
+            cross = _wsum(xr * yrj + xi * yij)
+            ncc = cross / (scale_a * rbj)
+            best = ncc if best is None else jnp.maximum(best, ncc)
+            prv = jnp.where(want == j + 1, ncc, prv)
+            cen = jnp.where(want == j, ncc, cen)
+            nxt = jnp.where(want == j - 1, ncc, nxt)
+        q_ref[p] = best
+        curvature = jnp.maximum(2.0 * cen - prv - nxt, 0.25)
+        d_ref[p] = peak_ref[p].astype(jnp.float32) + (nxt - prv) / (2.0 * curvature)
+        return carry
+
+    lax.fori_loop(0, fp_ref.shape[0], pair, 0)
+
+
+def correlate(frame_pairs, v, peak):
+    pairs = frame_pairs.shape[0]
+    lines = v.shape[2]
+    out = jax.ShapeDtypeStruct((pairs, lines, LANES), jnp.float32)
+    vmem = pltpu.MemorySpace.VMEM
+    smem = pltpu.MemorySpace.SMEM
+    return pl.pallas_call(
+        corr_kernel,
+        out_shape=(out, out),
+        in_specs=[pl.BlockSpec(memory_space=smem), pl.BlockSpec(memory_space=vmem), pl.BlockSpec(memory_space=vmem)],
+        out_specs=(pl.BlockSpec(memory_space=vmem), pl.BlockSpec(memory_space=vmem)),
+    )(frame_pairs, v, peak)
 
 
 def from_left(block, axis):
@@ -75,44 +126,17 @@
     padded = jnp.concatenate([from_left(tail, "tile"), vol, from_right(head, "tile")], axis=2)
 
     line_count = per_dev // 2
-    pair_count = frame_pairs.shape[0]
-    front = padded[frame_pairs[:, 0]].reshape(pair_count, line_count, 2, -1)
-    later = padded[frame_pairs[:, 1]].reshape(pair_count, line_count, 2, -1)
-    out_len = sample_rows + 4
-    prod_len = out_len + WIN - 1
-    xr = front[:, :, 0, WIN // 2 : WIN // 2 + prod_len]
-    xi = front[:, :, 1, WIN // 2 : WIN // 2 + prod_len]
-    yr = later[:, :, 0]
-    yi = later[:, :, 1]
-    nlag = 2 * MAXLAG + 1
-    prods = jnp.stack(
-        [xr * yr[..., j : j + prod_len] + xi * yi[..., j : j + prod_len] for j in range(nlag)]
-    )
-    cross_sum = window_sum(prods)
-    power_a = window_sum(xr * xr + xi * xi) / (2 * WIN)
-    ey = yr * yr + yi * yi
-    power_full = window_sum(ey[..., : out_len + nlag - 1 + WIN - 1]) / (2 * WIN)
-    root_b = jnp.sqrt(power_full + epsilon)
-    root_b = jnp.stack([root_b[..., j : j + out_len] for j in range(nlag)])
-    scores = cross_sum / (2 * WIN * jnp.sqrt(power_a + epsilon)[None] * root_b)
-    quality = jnp.max(scores[..., 2 : 2 + sample_rows], axis=0)
-
+    span = padded.shape[2]
+    padded = jnp.pad(padded, ((0, 0), (0, 0), (0, LANES - span)))
+    v = padded.reshape(frames, line_count, 2, LANES).transpose(0, 2, 1, 3)
     own = jnp.repeat(lag_f, BLK, axis=2)
     peak_full = jnp.concatenate(
         [jnp.repeat(lag_prev, 2, axis=2), own, jnp.repeat(lag_next, 2, axis=2)], axis=2
     ).astype(jnp.int32)
-    lag_values = jnp.arange(-MAXLAG, MAXLAG + 1, dtype=jnp.int32)[:, None, None, None]
-
-    def pick_lag(delta):
-        return jnp.sum(
-            jnp.where(lag_values == peak_full[None] + delta, scores, jnp.zeros_like(scores)), axis=0
-        )
-
-    at_prev = pick_lag(-1)
-    centre = pick_lag(0)
-    at_next = pick_lag(1)
-    curvature = jnp.maximum(2.0 * centre - at_prev - at_next, 0.25)
-    displacement = peak_full.astype(jnp.float32) + (at_next - at_prev) / (2.0 * curvature)
+    peak_full = jnp.pad(peak_full, ((0, 0), (0, 0), (0, LANES - peak_full.shape[2])))
+    best, displacement = correlate(frame_pairs, v, peak_full)
+    quality = best[..., 2 : 2 + sample_rows]
+    displacement = displacement[..., : sample_rows + 4]
     zo = lax.broadcasted_iota(jnp.int32, displacement.shape, 2)
     outside = ((tile == 0) & (zo < 2)) | ((tile == tiles - 1) & (zo >= sample_rows + 2))
     dz = jnp.where(outside, 0.0, displacement)

time: 86.4 us -> 97.4 us (1.13)
  Pallas kernels: 0 us -> 26.5 us
  other arithmetic: 15.1 us -> 2.05 us
  local copies, waits for them, and re-layouts: 11.8 us -> 9.37 us
    pallas_call x0 -> x1, Pallas kernels: none -> 26.5 us  [correlate(): pl.pallas_call(corr_kernel, out_shape=(out, out), in_specs=[pl.BlockSpec(...]
    add x16 -> x0, other arithmetic: 5.43 us -> none  [the longest x12 5.24 us: window_sum(): values = values[..., :n] + values[..., width:width + n]]
    unnamed x32 -> x0, other arithmetic: 4.24 us -> none
    reduce_sum x1 -> x0, other arithmetic: 2.56 us -> none  [pick_lag(): jnp.sum(jnp.where(lag_values == peak_full[None] + delta, scores, jnp.zero...]
    unnamed x41 -> x13, local copies, waits for them, and re-layouts: 5.96 us -> 3.55 us
    reduce_max x1 -> x0, other arithmetic: 1.21 us -> none  [shards(): quality = jnp.max(scores[..., 2:2 + sample_rows], axis=0)]
    gather x2 -> x0, local copies, waits for them, and re-layouts: 1.13 us -> none  [the longest x1 0.57 us: shards(): later = padded[frame_pairs[:, 1]].reshape(pair_count, line_count, 2, -1)]
where the time goes in v2:
time: 97.4 us; the launch traced here: 96.9 us
  starting transfers between devices  38.7 us (40%)
  Pallas kernels  26.5 us (27%)
  waiting for transfers between devices  14.7 us (15%)
  local copies, waits for them, and re-layouts  9.37 us (10%)
  matrix products  4.69 us (5%)
  other arithmetic  2.05 us (2%)
    ppermute x3, starting transfers between devices, from_right(): return lax.ppermute(block, axis, [(i + 1, i) for i in range(count - 1)])  27 us
    pallas_call x1, Pallas kernels, correlate(): pl.pallas_call(corr_kernel, out_shape=(out, out), in_specs=[pl.BlockSpec(...  26.5 us
    ppermute x2, waiting for transfers between devices, from_left(): return lax.ppermute(block, axis, [(i, i + 1) for i in range(count - 1)])  10.6 us
    all_to_all x1, starting transfers between devices, shards(): vol = lax.all_to_all(vol, ('cx', 'cy'), 1, 1, tiled=True).sum(axis=1)  5.95 us
    conv_general_dilated x2, matrix products, beamform(): lax.conv_general_dilated(extended, weights, window_strides=(1,), padding=...  4.69 us
    ppermute x2, starting transfers between devices, from_left(): return lax.ppermute(block, axis, [(i, i + 1) for i in range(count - 1)])  3.84 us
    unnamed x13, local copies, waits for them, and re-layouts  3.55 us
    ppermute x1, waiting for transfers between devices, shards(): vol = vol_mine + lax.ppermute(vol_other, 'cc', [(0, 1), (1, 0)])  2.63 us
  transfers between devices with their start and end apart: 7, of which 4 were waited for; matrix products, arithmetic and copies ran while one was open for 5% of the time, Pallas kernels for 0%

profile of v2, /device:TPU:36, one launch (start us, length us, event | category | flops | bytes accessed | tf_op | source)
XLA Modules:
  0.0 96.9 jit_solution(13121874787560434802)
XLA Ops:
  0.7 0.8 slice-done
  1.5 10.7 %collective-permute-start = (bf16[16,15,128]{2,0,1:T(8,128)(2,1)S(1)}, bf16[16,15,128]{2,0,1:T(8,128)(2,1)S(1)}, u32[]{:S(2)}, u32[]{:S(2)}) collective-permute-start(bf16[16,15,128]{2,0,1:T(8,128)(2,1)S(1)} %copy.61), channel_id=1, source_target_pairs={{1,0},{2,1},{3,2},{4,3},{5,4},{6,5},{7,6},{8,7},{9,8},{10,9},{11,1... | collective-permute-start | bytes 184328 | tf_op jit(solution)/shard_map/ppermute | solution.py:83
  12.2 1.4 %constant_dynamic-update-slice_fusion.1 = bf16[16,143,128]{2,0,1:T(8,128)(2,1)S(1)} fusion(bf16[16,128,128]{2,1,0:T(8,128)(2,1)} %param.4), kind=kLoop, calls=%fused_computation.13 | loop fusion | bytes 1048576
  13.6 0.7 copy.42
  14.3 0.2 constant_dynamic-slice_fusion.1
  14.6 2.3 %fusion.5 = f32[16,128,128]{1,0,2:T(8,128)S(1)} fusion(bf16[16,143,128]{2,0,1:T(8,128)(2,1)S(1)} %constant_dynamic-update-slice_fusion, bf16[16,128,128]{1,2,0:T(8,128)(2,1)S(1)} %bitcast.23), kind=kOutput, calls=%fused_computation.19 | convolution fusion | flops 1073741824 | bytes 2158592 | tf_op jit(solution)/shard_map/conv_general_dilated | solution.py:87
  16.9 1.9 %collective-permute-start.1 = (f32[16,128,128]{1,0,2:T(8,128)S(1)}, f32[16,128,128]{1,0,2:T(8,128)S(1)}, u32[]{:S(2)}, u32[]{:S(2)}) collective-permute-start(f32[16,128,128]{1,0,2:T(8,128)S(1)} %fusion.5), channel_id=1, source_target_pairs={{0,32},{32,0},{1,33},{33,1},{2,34},{34,2},{3,35},{35,3},{4,36},{36... | collective-permute-start | bytes 3145736 | tf_op jit(solution)/shard_map/ppermute | solution.py:120
  18.9 2.6 %collective-permute-done.1 = f32[16,128,128]{1,0,2:T(8,128)S(1)} collective-permute-done((f32[16,128,128]{1,0,2:T(8,128)S(1)}, f32[16,128,128]{1,0,2:T(8,128)S(1)}, u32[]{:S(2)}, u32[]{:S(2)}) %collective-permute-start.1) | collective-permute-done | bytes 1048608 | tf_op jit(solution)/shard_map/ppermute | solution.py:120
  21.5 2.3 %convolution_add_fusion = f32[16,128,128]{1,0,2:T(8,128)S(1)} fusion(f32[16,128,128]{1,0,2:T(8,128)S(1)} %collective-permute-done.1, bf16[16,143,128]{2,0,1:T(8,128)(2,1)S(1)} %constant_dynamic-update-slice_fusion, bf16[16,128,128]{1,2,0:T(8,128)(2,1)S(1)} %bitcast.22), kind=kOutput, calls=%fused_computation | convolution fusion | flops 1074003968 | bytes 3207168 | tf_op jit(solution)/shard_map/conv_general_dilated | solution.py:87
  23.8 0.4 copy.43
  24.3 1.1 %copy.44 = f32[16,8,16,128]{3,2,0,1:T(8,128)} copy(f32[16,8,16,128]{3,2,1,0:T(8,128)S(1)} %bitcast.18) | data formatting | bytes 2097152 | tf_op jit(solution)/shard_map/reshape | solution.py:121
  25.3 5.9 %all-to-all-start = ((f32[16,8,16,128]{3,2,0,1:T(8,128)}), f32[16,8,16,128]{3,2,0,1:T(8,128)S(1)}, u32[]{:S(2)}, u32[]{:S(2)}) async-start(f32[16,8,16,128]{3,2,0,1:T(8,128)} %copy.44), calls=%async_computation | async-start | bytes 2097152 | tf_op jit(solution)/shard_map/all_to_all | solution.py:122
  31.4 1.9 %collective-permute-start.4 = (f32[15,8,1]{2,1,0:T(8,128)S(1)}, f32[15,8,1]{2,1,0:T(8,128)S(1)}, u32[]{:S(2)}, u32[]{:S(2)}) collective-permute-start(f32[15,8,1]{2,1,0:T(8,128)S(1)} %get-tuple-element.10), channel_id=1, source_target_pairs={{0,1},{1,2},{2,3},{3,4},{4,5},{5,6},{6,7},{7,8},{8,9},{9,10},{10,1... | collective-permute-start | bytes 1448 | tf_op jit(solution)/shard_map/ppermute | solution.py:78
  33.3 8.2 %collective-permute-start.5 = (f32[15,8,1]{2,1,0:T(8,128)S(1)}, f32[15,8,1]{2,1,0:T(8,128)S(1)}, u32[]{:S(2)}, u32[]{:S(2)}) collective-permute-start(f32[15,8,1]{2,1,0:T(8,128)S(1)} %get-tuple-element.11), channel_id=1, source_target_pairs={{1,0},{2,1},{3,2},{4,3},{5,4},{6,5},{7,6},{8,7},{9,8},{10,9},{11,1... | collective-permute-start | bytes 1448 | tf_op jit(solution)/shard_map/ppermute | solution.py:83
  41.7 0.2 copy.53
  41.9 0.5 copy-done.3
  42.3 0.7 copy.54.fp_ref
  43.0 10.5 %collective-permute-done.4 = f32[15,8,1]{2,1,0:T(8,128)S(1)} collective-permute-done((f32[15,8,1]{2,1,0:T(8,128)S(1)}, f32[15,8,1]{2,1,0:T(8,128)S(1)}, u32[]{:S(2)}, u32[]{:S(2)}) %collective-permute-start.4) | collective-permute-done | bytes 512 | tf_op jit(solution)/shard_map/ppermute | solution.py:78
  53.5 0.2 copy.55
  53.7 0.2 copy.56
  54.1 1.9 %collective-permute-start.2 = (f32[16,16,34]{2,1,0:T(8,128)S(1)}, f32[16,16,34]{2,1,0:T(8,128)S(1)}, u32[]{:S(2)}, u32[]{:S(2)}) collective-permute-start(f32[16,16,34]{2,1,0:T(8,128)S(1)} %get-tuple-element.8), channel_id=1, source_target_pairs={{0,1},{1,2},{2,3},{3,4},{4,5},{5,6},{6,7},{7,8},{8,9},{9,10},{10,1... | collective-permute-start | bytes 104456 | tf_op jit(solution)/shard_map/ppermute | solution.py:78
  56.0 8.1 %collective-permute-start.3 = (f32[16,16,34]{2,1,0:T(8,128)S(1)}, f32[16,16,34]{2,1,0:T(8,128)S(1)}, u32[]{:S(2)}, u32[]{:S(2)}) collective-permute-start(f32[16,16,34]{2,1,0:T(8,128)S(1)} %get-tuple-element.9), channel_id=1, source_target_pairs={{1,0},{2,1},{3,2},{4,3},{5,4},{6,5},{7,6},{8,7},{9,8},{10,9},{11,1... | collective-permute-start | bytes 104456 | tf_op jit(solution)/shard_map/ppermute | solution.py:83
  64.4 0.7 pad.9.peak_ref
  65.2 1.4 %collective-permute-done.3 = f32[16,16,34]{2,1,0:T(8,128)S(1)} collective-permute-done((f32[16,16,34]{2,1,0:T(8,128)S(1)}, f32[16,16,34]{2,1,0:T(8,128)S(1)}, u32[]{:S(2)}, u32[]{:S(2)}) %collective-permute-start.3) | collective-permute-done | bytes 34848 | tf_op jit(solution)/shard_map/ppermute | solution.py:83
  66.6 0.2 pad_maximum_fusion
  66.8 0.2 copy.58
  67.0 0.9 copy.62
  67.9 26.5 %shard_map.59 = (f32[15,8,256]{2,1,0:T(8,128)}, f32[15,8,256]{2,1,0:T(8,128)}) custom-call(s32[15,2]{1,0:T(8,128)} %copy.54.fp_ref, f32[16,2,8,256]{3,2,1,0:T(8,128)} %bitcast.21, s32[15,8,256]{2,1,0:T(8,128)} %pad.9.peak_ref), custom_call_target="tpu_custom_call" | custom-call | tf_op jit(solution)/shard_map/pallas_call | solution.py:68
  94.4 0.9 slice_select_fusion
  95.3 0.7 fusion
  96.1 0.1 copy-done.2
  96.2 0.7 slice.38
  (24 shorter events, 0.9 us)
Async XLA Ops:
  0.6 0.8 slice-start
  0.6 13.0 %copy-start = (bf16[1,16,128,256]{3,2,1,0:T(8,128)(2,1)S(1)}, bf16[1,16,128,256]{3,2,1,0:T(8,128)(2,1)}, u32[]{:S(2)}) copy-start(bf16[1,16,128,256]{3,2,1,0:T(8,128)(2,1)} %param.5) | copy-start | bytes 3145732
  1.5 13.1 %collective-permute-start = (bf16[16,15,128]{2,0,1:T(8,128)(2,1)S(1)}, bf16[16,15,128]{2,0,1:T(8,128)(2,1)S(1)}, u32[]{:S(2)}, u32[]{:S(2)}) collective-permute-start(bf16[16,15,128]{2,0,1:T(8,128)(2,1)S(1)} %copy.61), channel_id=1, source_target_pairs={{1,0},{2,1},{3,2},{4,3},{5,4},{6,5},{7,6},{8,7},{9,8},{10,9},{11,1... | collective-permute-start | bytes 184328 | tf_op jit(solution)/shard_map/ppermute | solution.py:83
  16.9 4.6 %collective-permute-start.1 = (f32[16,128,128]{1,0,2:T(8,128)S(1)}, f32[16,128,128]{1,0,2:T(8,128)S(1)}, u32[]{:S(2)}, u32[]{:S(2)}) collective-permute-start(f32[16,128,128]{1,0,2:T(8,128)S(1)} %fusion.5), channel_id=1, source_target_pairs={{0,32},{32,0},{1,33},{33,1},{2,34},{34,2},{3,35},{35,3},{4,36},{36... | collective-permute-start | bytes 3145736 | tf_op jit(solution)/shard_map/ppermute | solution.py:120
  25.3 6.0 %copy-start.1 = (s32[15,8,16]{2,1,0:T(8,128)S(1)}, s32[15,8,16]{2,1,0:T(8,128)}, u32[]{:S(2)}) copy-start(s32[15,8,16]{2,1,0:T(8,128)} %param.6) | copy-start | bytes 23044
  25.3 28.5 %all-to-all-start = ((f32[16,8,16,128]{3,2,0,1:T(8,128)}), f32[16,8,16,128]{3,2,0,1:T(8,128)S(1)}, u32[]{:S(2)}, u32[]{:S(2)}) async-start(f32[16,8,16,128]{3,2,0,1:T(8,128)} %copy.44), calls=%async_computation | async-start | bytes 2097152 | tf_op jit(solution)/shard_map/all_to_all | solution.py:122
  31.4 22.2 %collective-permute-start.4 = (f32[15,8,1]{2,1,0:T(8,128)S(1)}, f32[15,8,1]{2,1,0:T(8,128)S(1)}, u32[]{:S(2)}, u32[]{:S(2)}) collective-permute-start(f32[15,8,1]{2,1,0:T(8,128)S(1)} %get-tuple-element.10), channel_id=1, source_target_pairs={{0,1},{1,2},{2,3},{3,4},{4,5},{5,6},{6,7},{7,8},{8,9},{9,10},{10,1... | collective-permute-start | bytes 1448 | tf_op jit(solution)/shard_map/ppermute | solution.py:78
  33.3 20.4 %collective-permute-start.5 = (f32[15,8,1]{2,1,0:T(8,128)S(1)}, f32[15,8,1]{2,1,0:T(8,128)S(1)}, u32[]{:S(2)}, u32[]{:S(2)}) collective-permute-start(f32[15,8,1]{2,1,0:T(8,128)S(1)} %get-tuple-element.11), channel_id=1, source_target_pairs={{1,0},{2,1},{3,2},{4,3},{5,4},{6,5},{7,6},{8,7},{9,8},{10,9},{11,1... | collective-permute-start | bytes 1448 | tf_op jit(solution)/shard_map/ppermute | solution.py:83
  41.7 0.7 copy-start.3
  54.1 11.2 %collective-permute-start.2 = (f32[16,16,34]{2,1,0:T(8,128)S(1)}, f32[16,16,34]{2,1,0:T(8,128)S(1)}, u32[]{:S(2)}, u32[]{:S(2)}) collective-permute-start(f32[16,16,34]{2,1,0:T(8,128)S(1)} %get-tuple-element.8), channel_id=1, source_target_pairs={{0,1},{1,2},{2,3},{3,4},{4,5},{5,6},{6,7},{7,8},{8,9},{9,10},{10,1... | collective-permute-start | bytes 104456 | tf_op jit(solution)/shard_map/ppermute | solution.py:78
  56.0 10.6 %collective-permute-start.3 = (f32[16,16,34]{2,1,0:T(8,128)S(1)}, f32[16,16,34]{2,1,0:T(8,128)S(1)}, u32[]{:S(2)}, u32[]{:S(2)}) collective-permute-start(f32[16,16,34]{2,1,0:T(8,128)S(1)} %get-tuple-element.9), channel_id=1, source_target_pairs={{1,0},{2,1},{3,2},{4,3},{5,4},{6,5},{7,6},{8,7},{9,8},{10,9},{11,1... | collective-permute-start | bytes 104456 | tf_op jit(solution)/shard_map/ppermute | solution.py:83
  95.3 0.9 copy-start.2

commit v3 on v1

--- a/solution.py
+++ b/solution.py
@@ -54,9 +54,6 @@
     lag_prev = from_left(lag_f[:, :, -1:], "tile")
     lag_next = from_right(lag_f[:, :, :1], "tile")
 
-    rim_rows = from_right(channel_data[:, : tap_count - 1, :], "tile")
-    extended = jnp.concatenate([channel_data, rim_rows], axis=1)
-
     weights = delay_weights[0]
     taps, cin, cols = weights.shape
     per_dev = cols // (nx * ny * nc)
@@ -64,15 +61,34 @@
     core = lax.axis_index("cc")
     w_mine = lax.dynamic_index_in_dim(w6, core, 4, keepdims=False).reshape(taps, cin, -1)
     w_other = lax.dynamic_index_in_dim(w6, 1 - core, 4, keepdims=False).reshape(taps, cin, -1)
-    vol_other = beamform(extended, w_other)
-    vol_mine = beamform(extended, w_mine)
-    vol = vol_mine + lax.ppermute(vol_other, "cc", [(0, 1), (1, 0)])
+    swap = [(0, 1), (1, 0)]
+    w_partner = lax.ppermute(w_other, "cc", swap)
+    data_partner = lax.ppermute(channel_data, "cc", swap)
+    rim = channel_data[:, : tap_count - 1, :]
+    rim_rows = from_right(rim, "tile")
+    diag = [
+        (c * tiles + t + 1, (1 - c) * tiles + t) for c in range(nc) for t in range(tiles - 1)
+    ]
+    rim_partner = lax.ppermute(rim, ("cc", "tile"), diag)
+    extended = jnp.concatenate(
+        [
+            jnp.concatenate([channel_data, rim_rows], axis=1),
+            jnp.concatenate([data_partner, rim_partner], axis=1),
+        ],
+        axis=2,
+    )
+    vol = beamform(extended, jnp.concatenate([w_mine, w_partner], axis=1))
     vol = vol.reshape(frames, nx * ny, per_dev, sample_rows)
-    vol = lax.all_to_all(vol, ("cx", "cy"), 1, 1, tiled=True).sum(axis=1)
-
-    head = vol[..., :HALO]
-    tail = vol[..., sample_rows - HALO :]
-    padded = jnp.concatenate([from_left(tail, "tile"), vol, from_right(head, "tile")], axis=2)
+    edges = jnp.concatenate([vol[..., :HALO], vol[..., sample_rows - HALO :]], axis=3)
+    edges = lax.all_to_all(edges, ("cx", "cy"), 1, 1, tiled=True).sum(axis=1)
+    inner = vol[..., HALO : sample_rows - HALO]
+    edges, inner = lax.optimization_barrier((edges, inner))
+    head = edges[..., :HALO]
+    tail = edges[..., HALO:]
+    left = from_left(tail, "tile")
+    right = from_right(head, "tile")
+    inner = lax.all_to_all(inner, ("cx", "cy"), 1, 1, tiled=True).sum(axis=1)
+    padded = jnp.concatenate([left, head, inner, tail, right], axis=2)
 
     line_count = per_dev // 2
     pair_count = frame_pairs.shape[0]

time: 86.4 us -> 99.6 us (1.15)
  the two profiles are of different devices: /device:TPU:36 before, /device:TPU:40 now
where the time goes in v3:
time: 99.6 us; the launch traced here: 99.1 us
  starting transfers between devices  50.5 us (51%)
  other arithmetic  17.1 us (17%)
  local copies, waits for them, and re-layouts  16.9 us (17%)
  waiting for transfers between devices  7.47 us (8%)
  matrix products  5.57 us (6%)
  between operations  1.6 us (2%)
    ppermute x3, starting transfers between devices, from_right(): return lax.ppermute(block, axis, [(i + 1, i) for i in range(count - 1)])  28.1 us
    unnamed x44, local copies, waits for them, and re-layouts  9.15 us
    all_to_all x1, starting transfers between devices, shards(): inner = lax.all_to_all(inner, ('cx', 'cy'), 1, 1, tiled=True).sum(axis=1)  6.57 us
    all_to_all x1, starting transfers between devices, shards(): edges = lax.all_to_all(edges, ('cx', 'cy'), 1, 1, tiled=True).sum(axis=1)  5.75 us
    conv_general_dilated x1, matrix products, beamform(): lax.conv_general_dilated(extended, weights, window_strides=(1,), padding=...  5.57 us
    add x12, other arithmetic, window_sum(): values = values[..., :n] + values[..., width:width + n]  5.24 us
    unnamed x32, other arithmetic  4.24 us
    ppermute x1, waiting for transfers between devices, shards(): rim_partner = lax.ppermute(rim, ('cc', 'tile'), diag)  3.89 us
  transfers between devices with their start and end apart: 10, of which 2 were waited for; matrix products, arithmetic and copies ran while one was open for 10% of the time, Pallas kernels for 0%

profile of v3, /device:TPU:40, one launch (start us, length us, event | category | flops | bytes accessed | tf_op | source)
XLA Modules:
  0.0 99.1 jit_solution(6033766857696849926)
XLA Ops:
  0.6 1.7 %copy.85 = bf16[1,16,128,256]{2,3,1,0:T(8,128)(2,1)S(1)} copy(bf16[1,16,128,256]{3,2,1,0:T(8,128)(2,1)} %param.5) | data formatting | bytes 2097152 | tf_op args[1]
  2.9 1.9 %collective-permute-start.3 = (bf16[16,128,128]{2,1,0:T(8,128)(2,1)S(1)}, bf16[16,128,128]{2,1,0:T(8,128)(2,1)S(1)}, u32[]{:S(2)}, u32[]{:S(2)}) collective-permute-start(bf16[16,128,128]{2,1,0:T(8,128)(2,1)S(1)} %copy.86), channel_id=1, source_target_pairs={{0,32},{32,0},{1,33},{33,1},{2,34},{34,2},{3,35},{35,3},{4,36},{36... | collective-permute-start | bytes 1572872 | tf_op jit(solution)/shard_map/ppermute | solution.py:65
  5.1 2.4 %collective-permute-start.1 = (bf16[16,128,128]{2,0,1:T(8,128)(2,1)S(1)}, bf16[16,128,128]{2,0,1:T(8,128)(2,1)}, u32[]{:S(2)}, u32[]{:S(2)}) collective-permute-start(bf16[16,128,128]{2,0,1:T(8,128)(2,1)S(1)} %copy.83), channel_id=1, source_target_pairs={{0,32},{32,0},{1,33},{33,1},{2,34},{34,2},{3,35},{35,3},{4,36},{36... | collective-permute-start | bytes 1572872 | tf_op jit(solution)/shard_map/ppermute | solution.py:66
  7.6 11.6 %collective-permute-start = (bf16[16,15,128]{2,0,1:T(8,128)(2,1)S(1)}, bf16[16,15,128]{2,0,1:T(8,128)(2,1)S(1)}, u32[]{:S(2)}, u32[]{:S(2)}) collective-permute-start(bf16[16,15,128]{2,0,1:T(8,128)(2,1)S(1)} %slice.599), channel_id=1, source_target_pairs={{1,0},{2,1},{3,2},{4,3},{5,4},{6,5},{7,6},{8,7},{9,8},{10,9},{11,1... | collective-permute-start | bytes 184328 | tf_op jit(solution)/shard_map/ppermute | solution.py:32
  19.2 1.9 %collective-permute-start.2 = (bf16[16,15,128]{2,0,1:T(8,128)(2,1)S(1)}, bf16[16,15,128]{2,0,1:T(8,128)(2,1)S(1)}, u32[]{:S(2)}, u32[]{:S(2)}) collective-permute-start(bf16[16,15,128]{2,0,1:T(8,128)(2,1)S(1)} %slice.599), channel_id=1, source_target_pairs={{1,32},{2,33},{3,34},{4,35},{5,36},{6,37},{7,38},{8,39},{9,40},{10... | collective-permute-start | bytes 184328 | tf_op jit(solution)/shard_map/ppermute | solution.py:72
  21.4 3.9 %collective-permute-done.2 = bf16[16,15,128]{2,0,1:T(8,128)(2,1)S(1)} collective-permute-done((bf16[16,15,128]{2,0,1:T(8,128)(2,1)S(1)}, bf16[16,15,128]{2,0,1:T(8,128)(2,1)S(1)}, u32[]{:S(2)}, u32[]{:S(2)}) %collective-permute-start.2) | collective-permute-done | bytes 61472 | tf_op jit(solution)/shard_map/ppermute | solution.py:72
  25.3 5.6 %fusion.1 = f32[16,128,128]{1,0,2:T(8,128)S(1)} fusion(bf16[16,15,128]{2,0,1:T(8,128)(2,1)S(1)} %collective-permute-done.2, bf16[16,128,128]{2,0,1:T(8,128)(2,1)} %collective-permute-done.1, bf16[16,15,128]{2,0,1:T(8,128)(2,1)S(1)} %collective-permute-done, bf16[16,128,128]{2,0,1:T(8,128)(2,1)S(1)} %copy.83, ...), kind=kOutput, calls=%fused_computation.12 | convolution fusion | flops 2154266624 | bytes 3268608 | tf_op jit(solution)/shard_map/conv_general_dilated | solution.py:36
  30.9 0.4 copy.88
  31.3 0.4 fusion.93
  32.0 1.1 %copy.89 = f32[16,8,16,68]{3,2,0,1:T(8,128)} copy(f32[16,8,16,68]{3,2,1,0:T(8,128)S(1)} %pad_maximum_fusion) | data formatting | bytes 1114112 | tf_op jit(solution)/shard_map/concatenate | solution.py:82
  33.1 5.8 %all-to-all-start = ((f32[16,8,16,68]{3,2,0,1:T(8,128)}), f32[16,8,16,68]{3,2,0,1:T(8,128)S(1)}, u32[]{:S(2)}, u32[]{:S(2)}) async-start(f32[16,8,16,68]{3,2,0,1:T(8,128)} %copy.89), calls=%async_computation | async-start | bytes 2097152 | tf_op jit(solution)/shard_map/all_to_all | solution.py:83
  38.9 0.7 fusion.97
  39.6 1.9 %collective-permute-start.6 = (f32[15,8,1]{2,1,0:T(8,128)}, f32[15,8,1]{2,1,0:T(8,128)S(1)}, u32[]{:S(2)}, u32[]{:S(2)}) collective-permute-start(f32[15,8,1]{2,1,0:T(8,128)} %get-tuple-element.24), channel_id=1, source_target_pairs={{0,1},{1,2},{2,3},{3,4},{4,5},{5,6},{6,7},{7,8},{8,9},{9,10},{10,1... | collective-permute-start | bytes 1448 | tf_op jit(solution)/shard_map/ppermute | solution.py:27
  41.5 8.1 %collective-permute-start.7 = (f32[15,8,1]{2,1,0:T(8,128)S(1)}, f32[15,8,1]{2,1,0:T(8,128)S(1)}, u32[]{:S(2)}, u32[]{:S(2)}) collective-permute-start(f32[15,8,1]{2,1,0:T(8,128)S(1)} %get-tuple-element.25), channel_id=1, source_target_pairs={{1,0},{2,1},{3,2},{4,3},{5,4},{6,5},{7,6},{8,7},{9,8},{10,9},{11,1... | collective-permute-start | bytes 1448 | tf_op jit(solution)/shard_map/ppermute | solution.py:32
  50.0 3.6 %all-to-all-done = f32[16,8,16,68]{3,2,0,1:T(8,128)S(1)} async-done(((f32[16,8,16,68]{3,2,0,1:T(8,128)}), f32[16,8,16,68]{3,2,0,1:T(8,128)S(1)}, u32[]{:S(2)}, u32[]{:S(2)}) %all-to-all-start) | async-done | bytes 557088 | tf_op jit(solution)/shard_map/all_to_all | solution.py:83
  53.8 2.4 %reshape.107 = f32[8,1,15360]{2,1,0:T(1,128)} reshape(f32[8,16,16,60]{3,2,1,0:T(8,128)S(1)} %bitcast.468) | data formatting | bytes 983040
  56.2 6.6 %all-to-all-start.1 = ((f32[8,1,15360]{2,1,0:T(1,128)}), f32[8,1,15360]{2,1,0:T(1,128)S(1)}, u32[]{:S(2)}, u32[]{:S(2)}) async-start(f32[8,1,15360]{2,1,0:T(1,128)} %reshape.107), calls=%async_computation.1 | async-start | bytes 983040 | tf_op jit(solution)/shard_map/all_to_all | solution.py:90
  64.0 1.9 %collective-permute-start.4 = (f32[16,16,34]{2,1,0:T(8,128)S(1)}, f32[16,16,34]{2,1,0:T(8,128)S(1)}, u32[]{:S(2)}, u32[]{:S(2)}) collective-permute-start(f32[16,16,34]{2,1,0:T(8,128)S(1)} %get-tuple-element.23), channel_id=1, source_target_pairs={{0,1},{1,2},{2,3},{3,4},{4,5},{5,6},{6,7},{7,8},{8,9},{9,10},{10,1... | collective-permute-start | bytes 104456 | tf_op jit(solution)/shard_map/ppermute | solution.py:27
  66.0 8.3 %collective-permute-start.5 = (f32[16,16,34]{2,1,0:T(8,128)S(1)}, f32[16,16,34]{2,1,0:T(8,128)S(1)}, u32[]{:S(2)}, u32[]{:S(2)}) collective-permute-start(f32[16,16,34]{2,1,0:T(8,128)S(1)} %get-tuple-element.22), channel_id=1, source_target_pairs={{1,0},{2,1},{3,2},{4,3},{5,4},{6,5},{7,6},{8,7},{9,8},{10,9},{11,1... | collective-permute-start | bytes 104456 | tf_op jit(solution)/shard_map/ppermute | solution.py:32
  74.3 0.5 broadcast.93
  74.8 1.8 %reduce = f32[8,15360]{1,0:T(8,128)S(1)} reduce(f32[8,1,15360]{2,1,0:T(1,128)S(1)} %all-to-all-done.1, f32[]{:T(128)} %broadcast.93), dimensions={1}, to_apply=%all_to_all.7.reduce_sub_computation | reduce | bytes 983044 | tf_op jit(solution)/shard_map/all_to_all | solution.py:90
  76.6 1.5 %reshape.108 = f32[8,16,16,60]{3,2,1,0:T(8,128)S(1)} reshape(f32[8,15360]{1,0:T(8,128)S(1)} %reduce) | data formatting | bytes 983040
  78.5 0.6 gather_fusion.1
  79.5 0.6 gather_fusion
  80.2 0.6 fusion.94
  85.4 1.1 %slice_add_fusion.4 = f32[33,15,8,162]{3,2,1,0:T(8,128)S(1)} fusion(f32[33,15,8,163]{3,2,1,0:T(8,128)S(1)} %constant_dynamic-update-slice_fusion), kind=kLoop, calls=%fused_computation.7 | loop fusion | flops 641520 | bytes 7698240 | tf_op jit(solution)/shard_map/add | solution.py:20
  86.5 1.1 %slice_add_fusion.3 = f32[33,15,8,160]{3,2,1,0:T(8,128)S(1)} fusion(f32[33,15,8,162]{3,2,1,0:T(8,128)S(1)} %slice_add_fusion.4), kind=kLoop, calls=%fused_computation.6 | loop fusion | flops 633600 | bytes 7603200 | tf_op jit(solution)/shard_map/add | solution.py:20
  87.7 1.1 %slice_add_fusion.2 = f32[33,15,8,156]{3,2,1,0:T(8,128)S(1)} fusion(f32[33,15,8,160]{3,2,1,0:T(8,128)S(1)} %slice_add_fusion.3), kind=kLoop, calls=%fused_computation.5 | loop fusion | flops 617760 | bytes 7413120 | tf_op jit(solution)/shard_map/add | solution.py:20
  88.8 1.1 %slice_add_fusion.1 = f32[33,15,8,148]{3,2,1,0:T(8,128)S(1)} fusion(f32[33,15,8,156]{3,2,1,0:T(8,128)S(1)} %slice_add_fusion.2), kind=kLoop, calls=%fused_computation.4 | loop fusion | flops 586080 | bytes 7032960 | tf_op jit(solution)/shard_map/add | solution.py:20
  94.4 2.6 %select_reduce_fusion = (f32[15,8,132]{2,1,0:T(8,128)S(1)}, f32[15,8,132]{2,1,0:T(8,128)S(1)}, f32[15,8,132]{2,1,0:T(8,128)S(1)}, f32[33,15,8,132]{3,2,1,0:T(8,128)S(1)}) fusion(s32[15,8,132]{2,1,0:T(8,128)S(1)} %maximum_convert_fusion, s32[33]{0:T(128)S(1)} %iota_add_fusion, s32[15,8,132]{2,1,0:T(8,128)S(1)} %get-tuple-element.21, ...), kind=kLoop, calls=%fused_computation.8 | loop fusion | flops 6225120 | bytes 8807172 | tf_op jit(solution)/shard_map/reduce_sum | solution.py:123
  97.1 0.7 fusion.86
  97.9 1.2 %slice_reduce_fusion = f32[15,8,128]{2,1,0:T(8,128)} fusion(f32[33,15,8,132]{3,2,1,0:T(8,128)S(1)} %get-tuple-element.11), kind=kLoop, calls=%fused_computation.11 | loop fusion | flops 491520 | bytes 2088960 | tf_op jit(solution)/shard_map/reduce_max | solution.py:114
  (124 shorter events, 12.8 us)
Async XLA Ops:
  0.6 4.2 %copy-start = (bf16[16,128,128]{2,1,0:T(8,128)(2,1)S(1)}, bf16[16,128,128]{2,1,0:T(8,128)(2,1)}, u32[]{:S(2)}) copy-start(bf16[16,128,128]{2,1,0:T(8,128)(2,1)} %param.4) | copy-start | bytes 1572868
  2.9 22.5 %collective-permute-start.3 = (bf16[16,128,128]{2,1,0:T(8,128)(2,1)S(1)}, bf16[16,128,128]{2,1,0:T(8,128)(2,1)S(1)}, u32[]{:S(2)}, u32[]{:S(2)}) collective-permute-start(bf16[16,128,128]{2,1,0:T(8,128)(2,1)S(1)} %copy.86), channel_id=1, source_target_pairs={{0,32},{32,0},{1,33},{33,1},{2,34},{34,2},{3,35},{35,3},{4,36},{36... | collective-permute-start | bytes 1572872 | tf_op jit(solution)/shard_map/ppermute | solution.py:65
  5.1 20.2 %collective-permute-start.1 = (bf16[16,128,128]{2,0,1:T(8,128)(2,1)S(1)}, bf16[16,128,128]{2,0,1:T(8,128)(2,1)}, u32[]{:S(2)}, u32[]{:S(2)}) collective-permute-start(bf16[16,128,128]{2,0,1:T(8,128)(2,1)S(1)} %copy.83), channel_id=1, source_target_pairs={{0,32},{32,0},{1,33},{33,1},{2,34},{34,2},{3,35},{35,3},{4,36},{36... | collective-permute-start | bytes 1572872 | tf_op jit(solution)/shard_map/ppermute | solution.py:66
  7.6 13.8 %collective-permute-start = (bf16[16,15,128]{2,0,1:T(8,128)(2,1)S(1)}, bf16[16,15,128]{2,0,1:T(8,128)(2,1)S(1)}, u32[]{:S(2)}, u32[]{:S(2)}) collective-permute-start(bf16[16,15,128]{2,0,1:T(8,128)(2,1)S(1)} %slice.599), channel_id=1, source_target_pairs={{1,0},{2,1},{3,2},{4,3},{5,4},{6,5},{7,6},{8,7},{9,8},{10,9},{11,1... | collective-permute-start | bytes 184328 | tf_op jit(solution)/shard_map/ppermute | solution.py:32
  19.2 6.1 %collective-permute-start.2 = (bf16[16,15,128]{2,0,1:T(8,128)(2,1)S(1)}, bf16[16,15,128]{2,0,1:T(8,128)(2,1)S(1)}, u32[]{:S(2)}, u32[]{:S(2)}) collective-permute-start(bf16[16,15,128]{2,0,1:T(8,128)(2,1)S(1)} %slice.599), channel_id=1, source_target_pairs={{1,32},{2,33},{3,34},{4,35},{5,36},{6,37},{7,38},{8,39},{9,40},{10... | collective-permute-start | bytes 184328 | tf_op jit(solution)/shard_map/ppermute | solution.py:72
  31.7 7.2 %copy-start.1 = (s32[15,8,16]{2,1,0:T(8,128)S(1)}, s32[15,8,16]{2,1,0:T(8,128)}, u32[]{:S(2)}) copy-start(s32[15,8,16]{2,1,0:T(8,128)} %param.6) | copy-start | bytes 23044
  31.7 18.0 %copy-start.2 = (s32[15,2]{0,1:T(2,128)S(1)}, s32[15,2]{0,1:T(2,128)}, u32[]{:S(2)}) copy-start(s32[15,2]{0,1:T(2,128)} %param.7) | copy-start | bytes 364
  33.1 20.5 %all-to-all-start = ((f32[16,8,16,68]{3,2,0,1:T(8,128)}), f32[16,8,16,68]{3,2,0,1:T(8,128)S(1)}, u32[]{:S(2)}, u32[]{:S(2)}) async-start(f32[16,8,16,68]{3,2,0,1:T(8,128)} %copy.89), calls=%async_computation | async-start | bytes 2097152 | tf_op jit(solution)/shard_map/all_to_all | solution.py:83
  39.6 23.6 %collective-permute-start.6 = (f32[15,8,1]{2,1,0:T(8,128)}, f32[15,8,1]{2,1,0:T(8,128)S(1)}, u32[]{:S(2)}, u32[]{:S(2)}) collective-permute-start(f32[15,8,1]{2,1,0:T(8,128)} %get-tuple-element.24), channel_id=1, source_target_pairs={{0,1},{1,2},{2,3},{3,4},{4,5},{5,6},{6,7},{7,8},{8,9},{9,10},{10,1... | collective-permute-start | bytes 1448 | tf_op jit(solution)/shard_map/ppermute | solution.py:27
  41.5 21.8 %collective-permute-start.7 = (f32[15,8,1]{2,1,0:T(8,128)S(1)}, f32[15,8,1]{2,1,0:T(8,128)S(1)}, u32[]{:S(2)}, u32[]{:S(2)}) collective-permute-start(f32[15,8,1]{2,1,0:T(8,128)S(1)} %get-tuple-element.25), channel_id=1, source_target_pairs={{1,0},{2,1},{3,2},{4,3},{5,4},{6,5},{7,6},{8,7},{9,8},{10,9},{11,1... | collective-permute-start | bytes 1448 | tf_op jit(solution)/shard_map/ppermute | solution.py:32
  56.2 18.1 %all-to-all-start.1 = ((f32[8,1,15360]{2,1,0:T(1,128)}), f32[8,1,15360]{2,1,0:T(1,128)S(1)}, u32[]{:S(2)}, u32[]{:S(2)}) async-start(f32[8,1,15360]{2,1,0:T(1,128)} %reshape.107), calls=%async_computation.1 | async-start | bytes 983040 | tf_op jit(solution)/shard_map/all_to_all | solution.py:90
  64.0 14.2 %collective-permute-start.4 = (f32[16,16,34]{2,1,0:T(8,128)S(1)}, f32[16,16,34]{2,1,0:T(8,128)S(1)}, u32[]{:S(2)}, u32[]{:S(2)}) collective-permute-start(f32[16,16,34]{2,1,0:T(8,128)S(1)} %get-tuple-element.23), channel_id=1, source_target_pairs={{0,1},{1,2},{2,3},{3,4},{4,5},{5,6},{6,7},{7,8},{8,9},{9,10},{10,1... | collective-permute-start | bytes 104456 | tf_op jit(solution)/shard_map/ppermute | solution.py:27
  66.0 12.3 %collective-permute-start.5 = (f32[16,16,34]{2,1,0:T(8,128)S(1)}, f32[16,16,34]{2,1,0:T(8,128)S(1)}, u32[]{:S(2)}, u32[]{:S(2)}) collective-permute-start(f32[16,16,34]{2,1,0:T(8,128)S(1)} %get-tuple-element.22), channel_id=1, source_target_pairs={{1,0},{2,1},{3,2},{4,3},{5,4},{6,5},{7,6},{8,7},{9,8},{10,9},{11,1... | collective-permute-start | bytes 104456 | tf_op jit(solution)/shard_map/ppermute | solution.py:32

commit v4 on v1

--- a/solution.py
+++ b/solution.py
@@ -55,7 +55,8 @@
     lag_next = from_right(lag_f[:, :, :1], "tile")
 
     rim_rows = from_right(channel_data[:, : tap_count - 1, :], "tile")
-    extended = jnp.concatenate([channel_data, rim_rows], axis=1)
+    main_rows = sample_rows - tap_count + 1
+    tail_rows = jnp.concatenate([channel_data[:, main_rows:, :], rim_rows], axis=1)
 
     weights = delay_weights[0]
     taps, cin, cols = weights.shape
@@ -64,15 +65,26 @@
     core = lax.axis_index("cc")
     w_mine = lax.dynamic_index_in_dim(w6, core, 4, keepdims=False).reshape(taps, cin, -1)
     w_other = lax.dynamic_index_in_dim(w6, 1 - core, 4, keepdims=False).reshape(taps, cin, -1)
-    vol_other = beamform(extended, w_other)
-    vol_mine = beamform(extended, w_mine)
-    vol = vol_mine + lax.ppermute(vol_other, "cc", [(0, 1), (1, 0)])
-    vol = vol.reshape(frames, nx * ny, per_dev, sample_rows)
-    vol = lax.all_to_all(vol, ("cx", "cy"), 1, 1, tiled=True).sum(axis=1)
 
-    head = vol[..., :HALO]
-    tail = vol[..., sample_rows - HALO :]
-    padded = jnp.concatenate([from_left(tail, "tile"), vol, from_right(head, "tile")], axis=2)
+    def beam(w):
+        return jnp.concatenate([beamform(channel_data, w), beamform(tail_rows, w)], axis=2)
+
+    vol_other = beam(w_other)
+    vol_mine = beam(w_mine)
+    swap = [(0, 1), (1, 0)]
+    to_next = [(c * tiles + t, (1 - c) * tiles + t + 1) for c in range(nc) for t in range(tiles - 1)]
+    to_prev = [(c * tiles + t + 1, (1 - c) * tiles + t) for c in range(nc) for t in range(tiles - 1)]
+    left = from_left(vol_mine[..., sample_rows - HALO :], "tile") + lax.ppermute(
+        vol_other[..., sample_rows - HALO :], ("cc", "tile"), to_next
+    )
+    right = from_right(vol_mine[..., :HALO], "tile") + lax.ppermute(
+        vol_other[..., :HALO], ("cc", "tile"), to_prev
+    )
+    centre = vol_mine + lax.ppermute(vol_other, "cc", swap)
+    vol = jnp.concatenate([left, centre, right], axis=2)
+    span = vol.shape[2]
+    vol = vol.reshape(frames, nx * ny, per_dev, span)
+    padded = lax.all_to_all(vol, ("cx", "cy"), 1, 1, tiled=True).sum(axis=1)
 
     line_count = per_dev // 2
     pair_count = frame_pairs.shape[0]

time: 86.4 us -> 121 us (1.40)
  the two profiles are of different devices: /device:TPU:36 before, /device:TPU:54 now
where the time goes in v4:
time: 121 us
  starting transfers between devices  42.9 us (35%)
  waiting for transfers between devices  42.1 us (35%)
  other arithmetic  16.7 us (14%)
  local copies, waits for them, and re-layouts  12.4 us (10%)
  matrix products  5.04 us (4%)
  between operations  1.61 us (1%)
    ppermute x2, waiting for transfers between devices, from_left(): return lax.ppermute(block, axis, [(i, i + 1) for i in range(count - 1)])  38.2 us
    ppermute x3, starting transfers between devices, from_right(): return lax.ppermute(block, axis, [(i + 1, i) for i in range(count - 1)])  23.7 us
    ppermute x1, starting transfers between devices, shards(): lax.ppermute(vol_other[..., :HALO], ('cc', 'tile'), to_prev)  6.75 us
    add x12, other arithmetic, window_sum(): values = values[..., :n] + values[..., width:width + n]  5.24 us
    conv_general_dilated x4, matrix products, beamform(): lax.conv_general_dilated(extended, weights, window_strides=(1,), padding=...  5.04 us
    all_to_all x1, starting transfers between devices, shards(): padded = lax.all_to_all(vol, ('cx', 'cy'), 1, 1, tiled=True).sum(axis=1)  4.77 us
    unnamed x43, local copies, waits for them, and re-layouts  4.6 us
    unnamed x32, other arithmetic  4.24 us
  transfers between devices with their start and end apart: 9, of which 3 were waited for; matrix products, arithmetic and copies ran while one was open for 6% of the time, Pallas kernels for 0%

profile of v4, /device:TPU:54, one launch (start us, length us, event | category | flops | bytes accessed | tf_op | source)
XLA Modules:
  0.0 120.8 jit_solution(6557674961485040862)
XLA Ops:
  0.6 1.0 fusion.92
  1.6 12.5 %collective-permute-start = (bf16[16,15,128]{2,0,1:T(8,128)(2,1)S(1)}, bf16[16,15,128]{2,0,1:T(8,128)(2,1)S(1)}, u32[]{:S(2)}, u32[]{:S(2)}) collective-permute-start(bf16[16,15,128]{2,0,1:T(8,128)(2,1)S(1)} %copy.211), channel_id=1, source_target_pairs={{1,0},{2,1},{3,2},{4,3},{5,4},{6,5},{7,6},{8,7},{9,8},{10,9},{11,1... | collective-permute-start | bytes 184328 | tf_op jit(solution)/shard_map/ppermute | solution.py:32
  14.2 1.6 %copy.76 = bf16[1,16,128,256]{2,3,1,0:T(8,128)(2,1)S(1)} copy(bf16[1,16,128,256]{3,2,1,0:T(8,128)(2,1)} %param.5) | data formatting | bytes 2097152 | tf_op args[1]
  16.0 2.1 %fusion.87 = f32[16,128,113]{1,0,2:T(8,128)S(1)} fusion(bf16[16,128,128]{1,2,0:T(8,128)(2,1)S(1)} %bitcast.469, bf16[16,128,128]{2,1,0:T(8,128)(2,1)S(1)} %copy-done.1), kind=kOutput, calls=%fused_computation.302 | convolution fusion | flops 947912704 | bytes 1974272 | tf_op jit(solution)/shard_map/conv_general_dilated | solution.py:36
  18.2 0.4 fusion.78
  18.7 1.9 %collective-permute-start.3 = (f32[16,128,128]{1,0,2:T(8,128)S(1)}, f32[16,128,128]{1,0,2:T(8,128)S(1)}, u32[]{:S(2)}, u32[]{:S(2)}) collective-permute-start(f32[16,128,128]{1,0,2:T(8,128)S(1)} %pad_maximum_fusion.2), channel_id=1, source_target_pairs={{0,32},{32,0},{1,33},{33,1},{2,34},{34,2},{3,35},{35,3},{4,36},{36... | collective-permute-start | bytes 3145736 | tf_op jit(solution)/shard_map/ppermute | solution.py:83
  20.6 2.1 %fusion.89 = f32[16,128,113]{1,0,2:T(8,128)S(1)} fusion(bf16[16,128,128]{1,2,0:T(8,128)(2,1)S(1)} %bitcast.467, bf16[16,128,128]{2,1,0:T(8,128)(2,1)S(1)} %copy-done.1), kind=kOutput, calls=%fused_computation.304 | convolution fusion | flops 947912704 | bytes 1974272 | tf_op jit(solution)/shard_map/conv_general_dilated | solution.py:36
  22.8 1.9 %collective-permute-start.2 = (f32[16,128,34]{1,0,2:T(8,128)S(1)}, f32[16,128,34]{1,0,2:T(8,128)S(1)}, u32[]{:S(2)}, u32[]{:S(2)}) collective-permute-start(f32[16,128,34]{1,0,2:T(8,128)S(1)} %get-tuple-element.10), channel_id=1, source_target_pairs={{0,33},{1,34},{2,35},{3,36},{4,37},{5,38},{6,39},{7,40},{8,41},{9,... | collective-permute-start | bytes 835592 | tf_op jit(solution)/shard_map/ppermute | solution.py:77
  24.7 0.4 fusion.79
  25.2 1.9 %collective-permute-start.1 = (f32[16,128,34]{1,0,2:T(8,128)S(1)}, f32[16,128,34]{1,0,2:T(8,128)S(1)}, u32[]{:S(2)}, u32[]{:S(2)}) collective-permute-start(f32[16,128,34]{1,0,2:T(8,128)S(1)} %get-tuple-element.12), channel_id=1, source_target_pairs={{0,1},{1,2},{2,3},{3,4},{4,5},{5,6},{6,7},{7,8},{8,9},{9,10},{10,1... | collective-permute-start | bytes 835592 | tf_op jit(solution)/shard_map/ppermute | solution.py:27
  27.1 6.8 %collective-permute-start.5 = (f32[16,128,34]{1,0,2:T(8,128)S(1)}, f32[16,128,34]{1,0,2:T(8,128)S(1)}, u32[]{:S(2)}, u32[]{:S(2)}) collective-permute-start(f32[16,128,34]{1,0,2:T(8,128)S(1)} %get-tuple-element.11), channel_id=1, source_target_pairs={{1,32},{2,33},{3,34},{4,35},{5,36},{6,37},{7,38},{8,39},{9,40},{10... | collective-permute-start | bytes 835592 | tf_op jit(solution)/shard_map/ppermute | solution.py:80
  33.8 3.5 %collective-permute-start.4 = (f32[16,128,34]{1,0,2:T(8,128)S(1)}, f32[16,128,34]{1,0,2:T(8,128)S(1)}, u32[]{:S(2)}, u32[]{:S(2)}) collective-permute-start(f32[16,128,34]{1,0,2:T(8,128)S(1)} %get-tuple-element.13), channel_id=1, source_target_pairs={{1,0},{2,1},{3,2},{4,3},{5,4},{6,5},{7,6},{8,7},{9,8},{10,9},{11,1... | collective-permute-start | bytes 835592 | tf_op jit(solution)/shard_map/ppermute | solution.py:32
  37.4 17.2 %collective-permute-done.1 = f32[16,128,34]{1,0,2:T(8,128)S(1)} collective-permute-done((f32[16,128,34]{1,0,2:T(8,128)S(1)}, f32[16,128,34]{1,0,2:T(8,128)S(1)}, u32[]{:S(2)}, u32[]{:S(2)}) %collective-permute-start.1) | collective-permute-done | bytes 278560 | tf_op jit(solution)/shard_map/ppermute | solution.py:27
  54.6 3.9 %collective-permute-done.4 = f32[16,128,34]{1,0,2:T(8,128)S(1)} collective-permute-done((f32[16,128,34]{1,0,2:T(8,128)S(1)}, f32[16,128,34]{1,0,2:T(8,128)S(1)}, u32[]{:S(2)}, u32[]{:S(2)}) %collective-permute-start.4) | collective-permute-done | bytes 278560 | tf_op jit(solution)/shard_map/ppermute | solution.py:32
  58.7 1.3 %pad_maximum_fusion = f32[16,128,196]{1,0,2:T(8,128)} fusion(f32[16,128,34]{1,0,2:T(8,128)S(1)} %add.233, f32[16,128,128]{1,0,2:T(8,128)S(1)} %fusion.1, f32[16,128,34]{1,0,2:T(8,128)S(1)} %add.231), kind=kLoop, calls=%fused_computation.12 | loop fusion | flops 802816 | bytes 3211264 | tf_op jit(solution)/shard_map/concatenate | solution.py:84
  59.9 1.9 %copy.81 = f32[16,128,196]{2,1,0:T(8,128)S(1)} copy(f32[16,128,196]{1,0,2:T(8,128)} %pad_maximum_fusion) | data formatting | bytes 3211264 | tf_op jit(solution)/shard_map/concatenate | solution.py:84
  61.8 1.6 %copy.82 = f32[16,8,16,196]{3,2,0,1:T(8,128)} copy(f32[16,8,16,196]{3,2,1,0:T(8,128)S(1)} %bitcast.465) | data formatting | bytes 3211264 | tf_op jit(solution)/shard_map/reshape | solution.py:86
  63.4 4.8 %all-to-all-start = ((f32[16,8,16,196]{3,2,0,1:T(8,128)}), f32[16,8,16,196]{3,2,0,1:T(8,128)S(1)}, u32[]{:S(2)}, u32[]{:S(2)}) async-start(f32[16,8,16,196]{3,2,0,1:T(8,128)} %copy.82), calls=%async_computation | async-start | bytes 4194304 | tf_op jit(solution)/shard_map/all_to_all | solution.py:87
  68.3 1.9 %collective-permute-start.6 = (f32[15,8,1]{2,1,0:T(8,128)S(1)}, f32[15,8,1]{2,1,0:T(8,128)S(1)}, u32[]{:S(2)}, u32[]{:S(2)}) collective-permute-start(f32[15,8,1]{2,1,0:T(8,128)S(1)} %get-tuple-element.22), channel_id=1, source_target_pairs={{0,1},{1,2},{2,3},{3,4},{4,5},{5,6},{6,7},{7,8},{8,9},{9,10},{10,1... | collective-permute-start | bytes 1448 | tf_op jit(solution)/shard_map/ppermute | solution.py:27
  70.2 7.6 %collective-permute-start.7 = (f32[15,8,1]{2,1,0:T(8,128)S(1)}, f32[15,8,1]{2,1,0:T(8,128)S(1)}, u32[]{:S(2)}, u32[]{:S(2)}) collective-permute-start(f32[15,8,1]{2,1,0:T(8,128)S(1)} %get-tuple-element.23), channel_id=1, source_target_pairs={{1,0},{2,1},{3,2},{4,3},{5,4},{6,5},{7,6},{8,7},{9,8},{10,9},{11,1... | collective-permute-start | bytes 1448 | tf_op jit(solution)/shard_map/ppermute | solution.py:32
  78.3 21.1 %collective-permute-done.6 = f32[15,8,1]{2,1,0:T(8,128)S(1)} collective-permute-done((f32[15,8,1]{2,1,0:T(8,128)S(1)}, f32[15,8,1]{2,1,0:T(8,128)S(1)}, u32[]{:S(2)}, u32[]{:S(2)}) %collective-permute-start.6) | collective-permute-done | bytes 512 | tf_op jit(solution)/shard_map/ppermute | solution.py:27
  100.1 0.2 reduce_sum.36
  100.3 0.6 gather_fusion.1
  101.3 0.6 gather_fusion
  102.0 0.6 fusion.93
  107.3 1.1 slice_add_fusion.4
  108.4 1.1 slice_add_fusion.3
  109.5 1.1 slice_add_fusion.2
  110.6 1.1 slice_add_fusion.1
  116.1 2.6 %select_reduce_fusion = (f32[15,8,132]{2,1,0:T(8,128)S(1)}, f32[15,8,132]{2,1,0:T(8,128)S(1)}, f32[15,8,132]{2,1,0:T(8,128)S(1)}, f32[33,15,8,132]{3,2,1,0:T(8,128)S(1)}) fusion(s32[15,8,132]{2,1,0:T(8,128)S(1)} %maximum_convert_fusion, s32[33]{0:T(128)S(1)} %iota_add_fusion, s32[15,8,132]{2,1,0:T(8,128)S(1)} %get-tuple-element.21, ...), kind=kLoop, calls=%fused_computation.8 | loop fusion | flops 6225120 | bytes 8807172 | tf_op jit(solution)/shard_map/reduce_sum | solution.py:119
  118.8 0.7 fusion.80
  119.5 1.2 %slice_reduce_fusion = f32[15,8,128]{2,1,0:T(8,128)} fusion(f32[33,15,8,132]{3,2,1,0:T(8,128)S(1)} %get-tuple-element.7), kind=kLoop, calls=%fused_computation.11 | loop fusion | flops 491520 | bytes 2088960 | tf_op jit(solution)/shard_map/reduce_max | solution.py:110
  (120 shorter events, 10.9 us)
Async XLA Ops:
  0.6 15.4 %copy-start.1 = (bf16[16,128,128]{2,1,0:T(8,128)(2,1)S(1)}, bf16[16,128,128]{2,1,0:T(8,128)(2,1)}, u32[]{:S(2)}) copy-start(bf16[16,128,128]{2,1,0:T(8,128)(2,1)} %param.4) | copy-start | bytes 1572868
  1.6 16.5 %collective-permute-start = (bf16[16,15,128]{2,0,1:T(8,128)(2,1)S(1)}, bf16[16,15,128]{2,0,1:T(8,128)(2,1)S(1)}, u32[]{:S(2)}, u32[]{:S(2)}) collective-permute-start(bf16[16,15,128]{2,0,1:T(8,128)(2,1)S(1)} %copy.211), channel_id=1, source_target_pairs={{1,0},{2,1},{3,2},{4,3},{5,4},{6,5},{7,6},{8,7},{9,8},{10,9},{11,1... | collective-permute-start | bytes 184328 | tf_op jit(solution)/shard_map/ppermute | solution.py:32
  18.7 39.9 %collective-permute-start.3 = (f32[16,128,128]{1,0,2:T(8,128)S(1)}, f32[16,128,128]{1,0,2:T(8,128)S(1)}, u32[]{:S(2)}, u32[]{:S(2)}) collective-permute-start(f32[16,128,128]{1,0,2:T(8,128)S(1)} %pad_maximum_fusion.2), channel_id=1, source_target_pairs={{0,32},{32,0},{1,33},{33,1},{2,34},{34,2},{3,35},{35,3},{4,36},{36... | collective-permute-start | bytes 3145736 | tf_op jit(solution)/shard_map/ppermute | solution.py:83
  22.8 14.6 %collective-permute-start.2 = (f32[16,128,34]{1,0,2:T(8,128)S(1)}, f32[16,128,34]{1,0,2:T(8,128)S(1)}, u32[]{:S(2)}, u32[]{:S(2)}) collective-permute-start(f32[16,128,34]{1,0,2:T(8,128)S(1)} %get-tuple-element.10), channel_id=1, source_target_pairs={{0,33},{1,34},{2,35},{3,36},{4,37},{5,38},{6,39},{7,40},{8,41},{9,... | collective-permute-start | bytes 835592 | tf_op jit(solution)/shard_map/ppermute | solution.py:77
  25.2 29.4 %collective-permute-start.1 = (f32[16,128,34]{1,0,2:T(8,128)S(1)}, f32[16,128,34]{1,0,2:T(8,128)S(1)}, u32[]{:S(2)}, u32[]{:S(2)}) collective-permute-start(f32[16,128,34]{1,0,2:T(8,128)S(1)} %get-tuple-element.12), channel_id=1, source_target_pairs={{0,1},{1,2},{2,3},{3,4},{4,5},{5,6},{6,7},{7,8},{8,9},{9,10},{10,1... | collective-permute-start | bytes 835592 | tf_op jit(solution)/shard_map/ppermute | solution.py:27
  27.1 27.5 %collective-permute-start.5 = (f32[16,128,34]{1,0,2:T(8,128)S(1)}, f32[16,128,34]{1,0,2:T(8,128)S(1)}, u32[]{:S(2)}, u32[]{:S(2)}) collective-permute-start(f32[16,128,34]{1,0,2:T(8,128)S(1)} %get-tuple-element.11), channel_id=1, source_target_pairs={{1,32},{2,33},{3,34},{4,35},{5,36},{6,37},{7,38},{8,39},{9,40},{10... | collective-permute-start | bytes 835592 | tf_op jit(solution)/shard_map/ppermute | solution.py:80
  33.8 24.6 %collective-permute-start.4 = (f32[16,128,34]{1,0,2:T(8,128)S(1)}, f32[16,128,34]{1,0,2:T(8,128)S(1)}, u32[]{:S(2)}, u32[]{:S(2)}) collective-permute-start(f32[16,128,34]{1,0,2:T(8,128)S(1)} %get-tuple-element.13), channel_id=1, source_target_pairs={{1,0},{2,1},{3,2},{4,3},{5,4},{6,5},{7,6},{8,7},{9,8},{10,9},{11,1... | collective-permute-start | bytes 835592 | tf_op jit(solution)/shard_map/ppermute | solution.py:32
  61.8 6.4 %copy-start = (s32[15,8,16]{2,1,0:T(8,128)S(1)}, s32[15,8,16]{2,1,0:T(8,128)}, u32[]{:S(2)}) copy-start(s32[15,8,16]{2,1,0:T(8,128)} %param.6) | copy-start | bytes 23044
  61.8 16.2 %copy-start.2 = (s32[15,2]{0,1:T(2,128)S(1)}, s32[15,2]{0,1:T(2,128)}, u32[]{:S(2)}) copy-start(s32[15,2]{0,1:T(2,128)} %param.7) | copy-start | bytes 364
  63.4 36.7 %all-to-all-start = ((f32[16,8,16,196]{3,2,0,1:T(8,128)}), f32[16,8,16,196]{3,2,0,1:T(8,128)S(1)}, u32[]{:S(2)}, u32[]{:S(2)}) async-start(f32[16,8,16,196]{3,2,0,1:T(8,128)} %copy.82), calls=%async_computation | async-start | bytes 4194304 | tf_op jit(solution)/shard_map/all_to_all | solution.py:87
  68.3 31.1 %collective-permute-start.6 = (f32[15,8,1]{2,1,0:T(8,128)S(1)}, f32[15,8,1]{2,1,0:T(8,128)S(1)}, u32[]{:S(2)}, u32[]{:S(2)}) collective-permute-start(f32[15,8,1]{2,1,0:T(8,128)S(1)} %get-tuple-element.22), channel_id=1, source_target_pairs={{0,1},{1,2},{2,3},{3,4},{4,5},{5,6},{6,7},{7,8},{8,9},{9,10},{10,1... | collective-permute-start | bytes 1448 | tf_op jit(solution)/shard_map/ppermute | solution.py:27
  70.2 29.3 %collective-permute-start.7 = (f32[15,8,1]{2,1,0:T(8,128)S(1)}, f32[15,8,1]{2,1,0:T(8,128)S(1)}, u32[]{:S(2)}, u32[]{:S(2)}) collective-permute-start(f32[15,8,1]{2,1,0:T(8,128)S(1)} %get-tuple-element.23), channel_id=1, source_target_pairs={{1,0},{2,1},{3,2},{4,3},{5,4},{6,5},{7,6},{8,7},{9,8},{10,9},{11,1... | collective-permute-start | bytes 1448 | tf_op jit(solution)/shard_map/ppermute | solution.py:32

commit v5 on v1

--- a/solution.py
+++ b/solution.py
@@ -51,11 +51,16 @@
     tiles = lax.axis_size("tile")
 
     lag_f = peak_lags.astype(jnp.float32)
-    lag_prev = from_left(lag_f[:, :, -1:], "tile")
-    lag_next = from_right(lag_f[:, :, :1], "tile")
-
-    rim_rows = from_right(channel_data[:, : tap_count - 1, :], "tile")
-    extended = jnp.concatenate([channel_data, rim_rows], axis=1)
+    pairs_n, lines_n, _ = peak_lags.shape
+    rim = channel_data[:, : tap_count - 1, :]
+    sent = jnp.concatenate(
+        [rim.reshape(-1), peak_lags[:, :, 0].astype(channel_data.dtype).reshape(-1)]
+    )
+    got = from_right(sent, "tile")
+    rim_rows = got[: rim.size].reshape(rim.shape)
+    lag_next = got[rim.size :].astype(jnp.float32).reshape(pairs_n, lines_n, 1)
+    main_rows = sample_rows - tap_count + 1
+    tail_rows = jnp.concatenate([channel_data[:, main_rows:, :], rim_rows], axis=1)
 
     weights = delay_weights[0]
     taps, cin, cols = weights.shape
@@ -64,15 +69,22 @@
     core = lax.axis_index("cc")
     w_mine = lax.dynamic_index_in_dim(w6, core, 4, keepdims=False).reshape(taps, cin, -1)
     w_other = lax.dynamic_index_in_dim(w6, 1 - core, 4, keepdims=False).reshape(taps, cin, -1)
-    vol_other = beamform(extended, w_other)
-    vol_mine = beamform(extended, w_mine)
+    def beam(w):
+        return jnp.concatenate([beamform(channel_data, w), beamform(tail_rows, w)], axis=2)
+
+    vol_other = beam(w_other)
+    vol_mine = beam(w_mine)
     vol = vol_mine + lax.ppermute(vol_other, "cc", [(0, 1), (1, 0)])
     vol = vol.reshape(frames, nx * ny, per_dev, sample_rows)
     vol = lax.all_to_all(vol, ("cx", "cy"), 1, 1, tiled=True).sum(axis=1)
 
     head = vol[..., :HALO]
     tail = vol[..., sample_rows - HALO :]
-    padded = jnp.concatenate([from_left(tail, "tile"), vol, from_right(head, "tile")], axis=2)
+    sent = jnp.concatenate([tail.reshape(-1), lag_f[:, :, -1].reshape(-1)])
+    got = from_left(sent, "tile")
+    left = got[: tail.size].reshape(tail.shape)
+    lag_prev = got[tail.size :].reshape(pairs_n, lines_n, 1)
+    padded = jnp.concatenate([left, vol, from_right(head, "tile")], axis=2)
 
     line_count = per_dev // 2
     pair_count = frame_pairs.shape[0]

time: 86.4 us -> 82.5 us (0.955)
  the two profiles are of different devices: /device:TPU:36 before, /device:TPU:32 now
where the time goes in v5:
time: 82.5 us; the launch traced here: 82.2 us
  starting transfers between devices  28.2 us (34%)
  waiting for transfers between devices  20 us (24%)
  other arithmetic  16.2 us (20%)
  local copies, waits for them, and re-layouts  11 us (13%)
  matrix products  5.03 us (6%)
  between operations  1.65 us (2%)
    ppermute x2, starting transfers between devices, from_right(): return lax.ppermute(block, axis, [(i + 1, i) for i in range(count - 1)])  19 us
    all_to_all x1, waiting for transfers between devices, shards(): vol = lax.all_to_all(vol, ('cx', 'cy'), 1, 1, tiled=True).sum(axis=1)  15.6 us
    all_to_all x1, starting transfers between devices, shards(): vol = lax.all_to_all(vol, ('cx', 'cy'), 1, 1, tiled=True).sum(axis=1)  5.32 us
    add x12, other arithmetic, window_sum(): values = values[..., :n] + values[..., width:width + n]  5.24 us
    conv_general_dilated x4, matrix products, beamform(): lax.conv_general_dilated(extended, weights, window_strides=(1,), padding=...  5.03 us
    unnamed x42, local copies, waits for them, and re-layouts  4.58 us
    ppermute x2, waiting for transfers between devices, from_right(): return lax.ppermute(block, axis, [(i + 1, i) for i in range(count - 1)])  4.32 us
    unnamed x32, other arithmetic  4.24 us
  transfers between devices with their start and end apart: 5, of which 3 were waited for; matrix products, arithmetic and copies ran while one was open for 9% of the time, Pallas kernels for 0%

profile of v5, /device:TPU:32, one launch (start us, length us, event | category | flops | bytes accessed | tf_op | source)
XLA Modules:
  0.0 82.2 jit_solution(18332373085382110803)
XLA Ops:
  0.6 1.0 %fusion.90 = (bf16[16,15,128]{2,1,0:T(8,128)(2,1)S(1)}, bf16[16,15,128]{2,1,0:T(8,128)(2,1)S(1)}) fusion(bf16[16,128,128]{2,1,0:T(8,128)(2,1)} %param.4), kind=kLoop, calls=%fused_computation.305 | loop fusion | bytes 245760 | tf_op jit(solution)/shard_map/slice | solution.py:63
  1.6 0.9 %fusion.80 = bf16[15,8]{1,0:T(8,128)(2,1)S(1)} fusion(s32[15,8,16]{2,1,0:T(8,128)} %param.6), kind=kLoop, calls=%fused_computation.287 | loop fusion | flops 120 | bytes 720 | tf_op jit(solution)/shard_map/slice | solution.py:57
  2.7 10.7 %collective-permute-start = (bf16[30840]{0:T(1024)(128)(2,1)S(1)}, bf16[30840]{0:T(1024)(128)(2,1)S(1)}, u32[]{:S(2)}, u32[]{:S(2)}) collective-permute-start(bf16[30840]{0:T(1024)(128)(2,1)S(1)} %pad_maximum_fusion.5), channel_id=1, source_target_pairs={{1,0},{2,1},{3,2},{4,3},{5,4},{6,5},{7,6},{8,7},{9,8},{10,9},{11,1... | collective-permute-start | bytes 185048 | tf_op jit(solution)/shard_map/ppermute | solution.py:32
  13.4 1.6 %copy.51 = bf16[1,16,128,256]{2,3,1,0:T(8,128)(2,1)S(1)} copy(bf16[1,16,128,256]{3,2,1,0:T(8,128)(2,1)} %param.5) | data formatting | bytes 2097152 | tf_op args[1]
  15.0 0.2 constant_dynamic-slice_fusion.1
  15.3 2.1 %fusion.85 = f32[16,128,113]{1,0,2:T(8,128)S(1)} fusion(bf16[16,128,128]{1,2,0:T(8,128)(2,1)S(1)} %bitcast.466, bf16[16,128,128]{2,1,0:T(8,128)(2,1)S(1)} %copy-done.1), kind=kOutput, calls=%fused_computation.301 | convolution fusion | flops 947912704 | bytes 1974272 | tf_op jit(solution)/shard_map/conv_general_dilated | solution.py:36
  17.5 0.4 fusion.75
  18.0 1.9 %collective-permute-start.1 = (f32[16,128,128]{1,0,2:T(8,128)S(1)}, f32[16,128,128]{1,0,2:T(8,128)S(1)}, u32[]{:S(2)}, u32[]{:S(2)}) collective-permute-start(f32[16,128,128]{1,0,2:T(8,128)S(1)} %pad_maximum_fusion), channel_id=1, source_target_pairs={{0,32},{32,0},{1,33},{33,1},{2,34},{34,2},{3,35},{35,3},{4,36},{36... | collective-permute-start | bytes 3145736 | tf_op jit(solution)/shard_map/ppermute | solution.py:77
  19.9 2.1 %fusion.87 = f32[16,128,113]{1,0,2:T(8,128)S(1)} fusion(bf16[16,128,128]{1,2,0:T(8,128)(2,1)S(1)} %bitcast.464, bf16[16,128,128]{2,1,0:T(8,128)(2,1)S(1)} %copy-done.1), kind=kOutput, calls=%fused_computation.303 | convolution fusion | flops 947912704 | bytes 1974272 | tf_op jit(solution)/shard_map/conv_general_dilated | solution.py:36
  22.0 0.4 fusion.76
  22.7 0.4 copy.56
  23.1 1.1 %copy.57 = f32[16,8,16,128]{3,2,0,1:T(8,128)} copy(f32[16,8,16,128]{3,2,1,0:T(8,128)S(1)} %bitcast.462) | data formatting | bytes 2097152 | tf_op jit(solution)/shard_map/reshape | solution.py:78
  24.2 5.3 %all-to-all-start = ((f32[16,8,16,128]{3,2,0,1:T(8,128)}), f32[16,8,16,128]{3,2,0,1:T(8,128)S(1)}, u32[]{:S(2)}, u32[]{:S(2)}) async-start(f32[16,8,16,128]{3,2,0,1:T(8,128)} %copy.57), calls=%async_computation | async-start | bytes 2097152 | tf_op jit(solution)/shard_map/all_to_all | solution.py:79
  29.7 0.2 slice_reduce_fusion.1
  30.0 0.2 copy.62
  30.3 15.6 %all-to-all-done = f32[16,8,16,128]{3,2,0,1:T(8,128)S(1)} async-done(((f32[16,8,16,128]{3,2,0,1:T(8,128)}), f32[16,8,16,128]{3,2,0,1:T(8,128)S(1)}, u32[]{:S(2)}, u32[]{:S(2)}) %all-to-all-start) | async-done | bytes 1048608 | tf_op jit(solution)/shard_map/all_to_all | solution.py:79
  46.2 1.9 %collective-permute-start.2 = (f32[8824]{0:T(1024)S(1)}, f32[8824]{0:T(1024)S(1)}, u32[]{:S(2)}, u32[]{:S(2)}) collective-permute-start(f32[8824]{0:T(1024)S(1)} %pad_maximum_fusion.6), channel_id=1, source_target_pairs={{0,1},{1,2},{2,3},{3,4},{4,5},{5,6},{6,7},{7,8},{8,9},{9,10},{10,1... | collective-permute-start | bytes 105896 | tf_op jit(solution)/shard_map/ppermute | solution.py:27
  48.2 8.3 %collective-permute-start.3 = (f32[16,16,34]{2,1,0:T(8,128)S(1)}, f32[16,16,34]{2,1,0:T(8,128)S(1)}, u32[]{:S(2)}, u32[]{:S(2)}) collective-permute-start(f32[16,16,34]{2,1,0:T(8,128)S(1)} %get-tuple-element.18), channel_id=1, source_target_pairs={{1,0},{2,1},{3,2},{4,3},{5,4},{6,5},{7,6},{8,7},{9,8},{10,9},{11,1... | collective-permute-start | bytes 104456 | tf_op jit(solution)/shard_map/ppermute | solution.py:32
  56.6 0.2 reshape.131
  56.8 4.3 %collective-permute-done.3 = f32[16,16,34]{2,1,0:T(8,128)S(1)} collective-permute-done((f32[16,16,34]{2,1,0:T(8,128)S(1)}, f32[16,16,34]{2,1,0:T(8,128)S(1)}, u32[]{:S(2)}, u32[]{:S(2)}) %collective-permute-start.3) | collective-permute-done | bytes 34848 | tf_op jit(solution)/shard_map/ppermute | solution.py:32
  61.1 0.2 pad_maximum_fusion.1
  61.2 0.6 gather_fusion.1
  62.0 0.2 fusion.92
  62.7 0.6 gather_fusion
  63.5 0.6 fusion.91
  68.7 1.1 %slice_add_fusion.4 = f32[33,15,8,162]{3,2,1,0:T(8,128)S(1)} fusion(f32[33,15,8,163]{3,2,1,0:T(8,128)S(1)} %constant_dynamic-update-slice_fusion), kind=kLoop, calls=%fused_computation.7 | loop fusion | flops 641520 | bytes 7698240 | tf_op jit(solution)/shard_map/add | solution.py:20
  69.8 1.1 %slice_add_fusion.3 = f32[33,15,8,160]{3,2,1,0:T(8,128)S(1)} fusion(f32[33,15,8,162]{3,2,1,0:T(8,128)S(1)} %slice_add_fusion.4), kind=kLoop, calls=%fused_computation.6 | loop fusion | flops 633600 | bytes 7603200 | tf_op jit(solution)/shard_map/add | solution.py:20
  70.9 1.1 %slice_add_fusion.2 = f32[33,15,8,156]{3,2,1,0:T(8,128)S(1)} fusion(f32[33,15,8,160]{3,2,1,0:T(8,128)S(1)} %slice_add_fusion.3), kind=kLoop, calls=%fused_computation.5 | loop fusion | flops 617760 | bytes 7413120 | tf_op jit(solution)/shard_map/add | solution.py:20
  72.0 1.1 %slice_add_fusion.1 = f32[33,15,8,148]{3,2,1,0:T(8,128)S(1)} fusion(f32[33,15,8,156]{3,2,1,0:T(8,128)S(1)} %slice_add_fusion.2), kind=kLoop, calls=%fused_computation.4 | loop fusion | flops 586080 | bytes 7032960 | tf_op jit(solution)/shard_map/add | solution.py:20
  77.5 2.6 %select_reduce_fusion = (f32[15,8,132]{2,1,0:T(8,128)S(1)}, f32[15,8,132]{2,1,0:T(8,128)S(1)}, f32[15,8,132]{2,1,0:T(8,128)S(1)}, f32[33,15,8,132]{3,2,1,0:T(8,128)S(1)}) fusion(s32[15,8,132]{2,1,0:T(8,128)S(1)} %maximum_convert_fusion, s32[33]{0:T(128)S(1)} %iota_add_fusion, s32[15,8,132]{2,1,0:T(8,128)S(1)} %get-tuple-element.17, ...), kind=kLoop, calls=%fused_computation.8 | loop fusion | flops 6225120 | bytes 8807172 | tf_op jit(solution)/shard_map/reduce_sum | solution.py:119
  80.2 0.7 fusion.77
  81.0 1.2 %slice_reduce_fusion = f32[15,8,128]{2,1,0:T(8,128)} fusion(f32[33,15,8,132]{3,2,1,0:T(8,128)S(1)} %get-tuple-element.7), kind=kLoop, calls=%fused_computation.11 | loop fusion | flops 491520 | bytes 2088960 | tf_op jit(solution)/shard_map/reduce_max | solution.py:110
  (121 shorter events, 10.6 us)
Async XLA Ops:
  0.6 14.7 %copy-start.1 = (bf16[16,128,128]{2,1,0:T(8,128)(2,1)S(1)}, bf16[16,128,128]{2,1,0:T(8,128)(2,1)}, u32[]{:S(2)}) copy-start(bf16[16,128,128]{2,1,0:T(8,128)(2,1)} %param.4) | copy-start | bytes 1572868
  2.7 14.7 %collective-permute-start = (bf16[30840]{0:T(1024)(128)(2,1)S(1)}, bf16[30840]{0:T(1024)(128)(2,1)S(1)}, u32[]{:S(2)}, u32[]{:S(2)}) collective-permute-start(bf16[30840]{0:T(1024)(128)(2,1)S(1)} %pad_maximum_fusion.5), channel_id=1, source_target_pairs={{1,0},{2,1},{3,2},{4,3},{5,4},{6,5},{7,6},{8,7},{9,8},{10,9},{11,1... | collective-permute-start | bytes 185048 | tf_op jit(solution)/shard_map/ppermute | solution.py:32
  18.0 4.6 %collective-permute-start.1 = (f32[16,128,128]{1,0,2:T(8,128)S(1)}, f32[16,128,128]{1,0,2:T(8,128)S(1)}, u32[]{:S(2)}, u32[]{:S(2)}) collective-permute-start(f32[16,128,128]{1,0,2:T(8,128)S(1)} %pad_maximum_fusion), channel_id=1, source_target_pairs={{0,32},{32,0},{1,33},{33,1},{2,34},{34,2},{3,35},{35,3},{4,36},{36... | collective-permute-start | bytes 3145736 | tf_op jit(solution)/shard_map/ppermute | solution.py:77
  22.5 7.1 %copy-start = (s32[15,8,16]{2,1,0:T(8,128)S(1)}, s32[15,8,16]{2,1,0:T(8,128)}, u32[]{:S(2)}) copy-start(s32[15,8,16]{2,1,0:T(8,128)} %param.6) | copy-start | bytes 23044
  22.7 7.5 %copy-start.2 = (s32[15,2]{0,1:T(2,128)S(1)}, s32[15,2]{0,1:T(2,128)}, u32[]{:S(2)}) copy-start(s32[15,2]{0,1:T(2,128)} %param.7) | copy-start | bytes 364
  24.2 21.7 %all-to-all-start = ((f32[16,8,16,128]{3,2,0,1:T(8,128)}), f32[16,8,16,128]{3,2,0,1:T(8,128)S(1)}, u32[]{:S(2)}, u32[]{:S(2)}) async-start(f32[16,8,16,128]{3,2,0,1:T(8,128)} %copy.57), calls=%async_computation | async-start | bytes 2097152 | tf_op jit(solution)/shard_map/all_to_all | solution.py:79
  46.2 10.4 %collective-permute-start.2 = (f32[8824]{0:T(1024)S(1)}, f32[8824]{0:T(1024)S(1)}, u32[]{:S(2)}, u32[]{:S(2)}) collective-permute-start(f32[8824]{0:T(1024)S(1)} %pad_maximum_fusion.6), channel_id=1, source_target_pairs={{0,1},{1,2},{2,3},{3,4},{4,5},{5,6},{6,7},{7,8},{8,9},{9,10},{10,1... | collective-permute-start | bytes 105896 | tf_op jit(solution)/shard_map/ppermute | solution.py:27
  48.2 12.9 %collective-permute-start.3 = (f32[16,16,34]{2,1,0:T(8,128)S(1)}, f32[16,16,34]{2,1,0:T(8,128)S(1)}, u32[]{:S(2)}, u32[]{:S(2)}) collective-permute-start(f32[16,16,34]{2,1,0:T(8,128)S(1)} %get-tuple-element.18), channel_id=1, source_target_pairs={{1,0},{2,1},{3,2},{4,3},{5,4},{6,5},{7,6},{8,7},{9,8},{10,9},{11,1... | collective-permute-start | bytes 104456 | tf_op jit(solution)/shard_map/ppermute | solution.py:32

commit v6 on v5

--- a/solution.py
+++ b/solution.py
@@ -105,24 +105,25 @@
     ey = yr * yr + yi * yi
     power_full = window_sum(ey[..., : out_len + nlag - 1 + WIN - 1]) / (2 * WIN)
     root_b = jnp.sqrt(power_full + epsilon)
-    root_b = jnp.stack([root_b[..., j : j + out_len] for j in range(nlag)])
-    scores = cross_sum / (2 * WIN * jnp.sqrt(power_a + epsilon)[None] * root_b)
-    quality = jnp.max(scores[..., 2 : 2 + sample_rows], axis=0)
+    root_a = 2 * WIN * jnp.sqrt(power_a + epsilon)
 
     own = jnp.repeat(lag_f, BLK, axis=2)
     peak_full = jnp.concatenate(
         [jnp.repeat(lag_prev, 2, axis=2), own, jnp.repeat(lag_next, 2, axis=2)], axis=2
     ).astype(jnp.int32)
-    lag_values = jnp.arange(-MAXLAG, MAXLAG + 1, dtype=jnp.int32)[:, None, None, None]
+    want = peak_full + MAXLAG
+    best = None
+    at_prev = jnp.zeros_like(root_a)
+    centre = jnp.zeros_like(root_a)
+    at_next = jnp.zeros_like(root_a)
+    for j in range(nlag):
+        score = cross_sum[j] / (root_a * root_b[..., j : j + out_len])
+        best = score if best is None else jnp.maximum(best, score)
+        at_prev = jnp.where(want == j + 1, score, at_prev)
+        centre = jnp.where(want == j, score, centre)
+        at_next = jnp.where(want == j - 1, score, at_next)
+    quality = best[..., 2 : 2 + sample_rows]
 
-    def pick_lag(delta):
-        return jnp.sum(
-            jnp.where(lag_values == peak_full[None] + delta, scores, jnp.zeros_like(scores)), axis=0
-        )
-
-    at_prev = pick_lag(-1)
-    centre = pick_lag(0)
-    at_next = pick_lag(1)
     curvature = jnp.maximum(2.0 * centre - at_prev - at_next, 0.25)
     displacement = peak_full.astype(jnp.float32) + (at_next - at_prev) / (2.0 * curvature)
     zo = lax.broadcasted_iota(jnp.int32, displacement.shape, 2)

time: 82.5 us -> 79.2 us (0.960)
  local copies, waits for them, and re-layouts: 11 us -> 7.97 us
    unnamed x42 -> x10, local copies, waits for them, and re-layouts: 4.58 us -> 1.67 us
    reduce_sum x1 -> x0, other arithmetic: 2.57 us -> none  [pick_lag(): jnp.sum(jnp.where(lag_values == peak_full[None] + delta, scores, jnp.zero...]
    max x0 -> x2, other arithmetic: none -> 1.71 us  [shards(): best = score if best is None else jnp.maximum(best, score)]
    select_n x1, other arithmetic: 0.13 us -> 1.47 us  [shards(): dz = jnp.where(outside, 0.0, displacement)]
    reduce_max x1 -> x0, other arithmetic: 1.21 us -> none  [shards(): quality = jnp.max(scores[..., 2:2 + sample_rows], axis=0)]
    add x12 -> x13, other arithmetic: 5.24 us -> 6.35 us  [window_sum(): values = values[..., :n] + values[..., width:width + n]]
where the time goes in v6:
time: 79.2 us; the launch traced here: 78.9 us
  starting transfers between devices  28.2 us (36%)
  waiting for transfers between devices  20.1 us (25%)
  other arithmetic  16.3 us (21%)
  local copies, waits for them, and re-layouts  7.97 us (10%)
  matrix products  5.03 us (6%)
  between operations  1.37 us (2%)
    ppermute x2, starting transfers between devices, from_right(): return lax.ppermute(block, axis, [(i + 1, i) for i in range(count - 1)])  19 us
    all_to_all x1, waiting for transfers between devices, shards(): vol = lax.all_to_all(vol, ('cx', 'cy'), 1, 1, tiled=True).sum(axis=1)  15.6 us
    add x13, other arithmetic, window_sum(): values = values[..., :n] + values[..., width:width + n]  6.35 us
    all_to_all x1, starting transfers between devices, shards(): vol = lax.all_to_all(vol, ('cx', 'cy'), 1, 1, tiled=True).sum(axis=1)  5.31 us
    conv_general_dilated x4, matrix products, beamform(): lax.conv_general_dilated(extended, weights, window_strides=(1,), padding=...  5.03 us
    ppermute x2, waiting for transfers between devices, from_right(): return lax.ppermute(block, axis, [(i + 1, i) for i in range(count - 1)])  4.32 us
    unnamed x32, other arithmetic  4.24 us
    ppermute x1, starting transfers between devices, from_left(): return lax.ppermute(block, axis, [(i, i + 1) for i in range(count - 1)])  1.92 us
  transfers between devices with their start and end apart: 5, of which 3 were waited for; matrix products, arithmetic and copies ran while one was open for 9% of the time, Pallas kernels for 0%

profile of v6, /device:TPU:32, one launch (start us, length us, event | category | flops | bytes accessed | tf_op | source)
XLA Modules:
  0.0 78.9 jit_solution(2245975160204784005)
XLA Ops:
  0.6 1.0 %fusion.145 = bf16[15,8]{1,0:T(8,128)(2,1)S(1)} fusion(s32[15,8,16]{2,1,0:T(8,128)} %param.6), kind=kLoop, calls=%fused_computation.328 | loop fusion | flops 120 | bytes 720 | tf_op jit(solution)/shard_map/slice | solution.py:57
  1.7 0.9 %fusion.161 = (bf16[16,15,128]{2,1,0:T(8,128)(2,1)S(1)}, bf16[16,15,128]{2,1,0:T(8,128)(2,1)S(1)}) fusion(bf16[16,128,128]{2,1,0:T(8,128)(2,1)} %param.4), kind=kLoop, calls=%fused_computation.345 | loop fusion | bytes 245760 | tf_op jit(solution)/shard_map/slice | solution.py:63
  2.7 10.7 %collective-permute-start = (bf16[30840]{0:T(1024)(128)(2,1)S(1)}, bf16[30840]{0:T(1024)(128)(2,1)S(1)}, u32[]{:S(2)}, u32[]{:S(2)}) collective-permute-start(bf16[30840]{0:T(1024)(128)(2,1)S(1)} %pad_maximum_fusion.5), channel_id=1, source_target_pairs={{1,0},{2,1},{3,2},{4,3},{5,4},{6,5},{7,6},{8,7},{9,8},{10,9},{11,1... | collective-permute-start | bytes 185048 | tf_op jit(solution)/shard_map/ppermute | solution.py:32
  13.4 1.6 %copy.22 = bf16[1,16,128,256]{2,3,1,0:T(8,128)(2,1)S(1)} copy(bf16[1,16,128,256]{3,2,1,0:T(8,128)(2,1)} %param.5) | data formatting | bytes 2097152 | tf_op args[1]
  15.1 0.2 constant_dynamic-slice_fusion.1
  15.3 2.1 %fusion.150 = f32[16,128,113]{1,0,2:T(8,128)S(1)} fusion(bf16[16,128,128]{1,2,0:T(8,128)(2,1)S(1)} %bitcast.580, bf16[16,128,128]{2,1,0:T(8,128)(2,1)S(1)} %copy-done.1), kind=kOutput, calls=%fused_computation.341 | convolution fusion | flops 947912704 | bytes 1974272 | tf_op jit(solution)/shard_map/conv_general_dilated | solution.py:36
  17.5 0.4 fusion.140
  18.0 1.9 %collective-permute-start.1 = (f32[16,128,128]{1,0,2:T(8,128)S(1)}, f32[16,128,128]{1,0,2:T(8,128)S(1)}, u32[]{:S(2)}, u32[]{:S(2)}) collective-permute-start(f32[16,128,128]{1,0,2:T(8,128)S(1)} %pad_maximum_fusion), channel_id=1, source_target_pairs={{0,32},{32,0},{1,33},{33,1},{2,34},{34,2},{3,35},{35,3},{4,36},{36... | collective-permute-start | bytes 3145736 | tf_op jit(solution)/shard_map/ppermute | solution.py:77
  19.9 2.1 %fusion.152 = f32[16,128,113]{1,0,2:T(8,128)S(1)} fusion(bf16[16,128,128]{1,2,0:T(8,128)(2,1)S(1)} %bitcast.578, bf16[16,128,128]{2,1,0:T(8,128)(2,1)S(1)} %copy-done.1), kind=kOutput, calls=%fused_computation.343 | convolution fusion | flops 947912704 | bytes 1974272 | tf_op jit(solution)/shard_map/conv_general_dilated | solution.py:36
  22.1 0.4 fusion.141
  22.7 0.4 copy.27
  23.2 1.1 %copy.28 = f32[16,8,16,128]{3,2,0,1:T(8,128)} copy(f32[16,8,16,128]{3,2,1,0:T(8,128)S(1)} %bitcast.576) | data formatting | bytes 2097152 | tf_op jit(solution)/shard_map/reshape | solution.py:78
  24.2 5.3 %all-to-all-start = ((f32[16,8,16,128]{3,2,0,1:T(8,128)}), f32[16,8,16,128]{3,2,0,1:T(8,128)S(1)}, u32[]{:S(2)}, u32[]{:S(2)}) async-start(f32[16,8,16,128]{3,2,0,1:T(8,128)} %copy.28), calls=%async_computation | async-start | bytes 2097152 | tf_op jit(solution)/shard_map/all_to_all | solution.py:79
  29.7 0.2 copy.33
  29.9 0.2 slice_reduce_fusion
  30.2 15.6 %all-to-all-done = f32[16,8,16,128]{3,2,0,1:T(8,128)S(1)} async-done(((f32[16,8,16,128]{3,2,0,1:T(8,128)}), f32[16,8,16,128]{3,2,0,1:T(8,128)S(1)}, u32[]{:S(2)}, u32[]{:S(2)}) %all-to-all-start) | async-done | bytes 1048608 | tf_op jit(solution)/shard_map/all_to_all | solution.py:79
  46.2 1.9 %collective-permute-start.2 = (f32[8824]{0:T(1024)S(1)}, f32[8824]{0:T(1024)S(1)}, u32[]{:S(2)}, u32[]{:S(2)}) collective-permute-start(f32[8824]{0:T(1024)S(1)} %pad_maximum_fusion.6), channel_id=1, source_target_pairs={{0,1},{1,2},{2,3},{3,4},{4,5},{5,6},{6,7},{7,8},{8,9},{9,10},{10,1... | collective-permute-start | bytes 105896 | tf_op jit(solution)/shard_map/ppermute | solution.py:27
  48.1 8.3 %collective-permute-start.3 = (f32[16,16,34]{2,1,0:T(8,128)S(1)}, f32[16,16,34]{2,1,0:T(8,128)S(1)}, u32[]{:S(2)}, u32[]{:S(2)}) collective-permute-start(f32[16,16,34]{2,1,0:T(8,128)S(1)} %get-tuple-element.18), channel_id=1, source_target_pairs={{1,0},{2,1},{3,2},{4,3},{5,4},{6,5},{7,6},{8,7},{9,8},{10,9},{11,1... | collective-permute-start | bytes 104456 | tf_op jit(solution)/shard_map/ppermute | solution.py:32
  56.7 4.3 %collective-permute-done.3 = f32[16,16,34]{2,1,0:T(8,128)S(1)} collective-permute-done((f32[16,16,34]{2,1,0:T(8,128)S(1)}, f32[16,16,34]{2,1,0:T(8,128)S(1)}, u32[]{:S(2)}, u32[]{:S(2)}) %collective-permute-start.3) | collective-permute-done | bytes 34848 | tf_op jit(solution)/shard_map/ppermute | solution.py:32
  61.2 0.6 gather_fusion.1
  61.9 0.2 fusion.163
  62.8 0.6 gather_fusion
  63.6 0.6 fusion.162
  68.8 1.1 %slice_add_fusion.4 = f32[33,15,8,162]{3,2,1,0:T(8,128)S(1)} fusion(f32[33,15,8,163]{3,2,1,0:T(8,128)S(1)} %fusion.42), kind=kLoop, calls=%fused_computation.6 | loop fusion | flops 641520 | bytes 7698240 | tf_op jit(solution)/shard_map/add | solution.py:20
  69.9 1.1 %slice_add_fusion.3 = f32[33,15,8,160]{3,2,1,0:T(8,128)S(1)} fusion(f32[33,15,8,162]{3,2,1,0:T(8,128)S(1)} %slice_add_fusion.4), kind=kLoop, calls=%fused_computation.5 | loop fusion | flops 633600 | bytes 7603200 | tf_op jit(solution)/shard_map/add | solution.py:20
  71.0 1.1 %slice_add_fusion.2 = f32[33,15,8,156]{3,2,1,0:T(8,128)S(1)} fusion(f32[33,15,8,160]{3,2,1,0:T(8,128)S(1)} %slice_add_fusion.3), kind=kLoop, calls=%fused_computation.4 | loop fusion | flops 617760 | bytes 7413120 | tf_op jit(solution)/shard_map/add | solution.py:20
  72.1 1.1 %slice_add_fusion.1 = f32[33,15,8,148]{3,2,1,0:T(8,128)S(1)} fusion(f32[33,15,8,156]{3,2,1,0:T(8,128)S(1)} %slice_add_fusion.2), kind=kLoop, calls=%fused_computation.3 | loop fusion | flops 586080 | bytes 7032960 | tf_op jit(solution)/shard_map/add | solution.py:20
  73.3 1.1 %slice_add_fusion = f32[33,15,8,132]{3,2,1,0:T(8,128)S(1)} fusion(f32[33,15,8,148]{3,2,1,0:T(8,128)S(1)} %slice_add_fusion.1), kind=kLoop, calls=%fused_computation.2 | loop fusion | flops 522720 | bytes 6272640 | tf_op jit(solution)/shard_map/add | solution.py:20
  74.9 1.5 %add_select_fusion = (f32[15,8,132]{2,1,0:T(8,128)S(1)}, f32[15,8,132]{2,1,0:T(8,128)S(1)}, f32[15,8,132]{2,1,0:T(8,128)S(1)}, f32[15,8,132]{2,1,0:T(8,128)S(1)}...) fusion(f32[15,8,2]{2,1,0:T(8,128)S(1)} %reshape.86, ...), kind=kLoop, calls=%fused_computation.299 | loop fusion | flops 3453120 | bytes 4878852 | tf_op jit(solution)/shard_map/jit(_where)/select_n | solution.py:131
  76.4 0.9 %maximum_maximum_fusion = f32[15,8,132]{2,1,0:T(8,128)S(1)} fusion(f32[15,8,132]{2,1,0:T(8,128)S(1)} %get-tuple-element.9, f32[15,8,164]{2,1,0:T(8,128)S(1)} %fusion.35, f32[33,15,8,132]{3,2,1,0:T(8,128)S(1)} %slice_add_fusion), kind=kLoop, calls=%fused_computation.300 | loop fusion | flops 1267200 | bytes 3548160 | tf_op jit(solution)/shard_map/max | solution.py:121
  77.3 0.7 fusion.142
  78.1 0.8 %slice_maximum_fusion = f32[15,8,128]{2,1,0:T(8,128)} fusion(f32[15,8,132]{2,1,0:T(8,128)S(1)} %get-tuple-element.8, f32[15,8,132]{2,1,0:T(8,128)S(1)} %get-tuple-element.7, f32[15,8,132]{2,1,0:T(8,128)S(1)} %get-tuple-element.6, f32[15,8,132]{2,1,0:T(8,128)S(1)} %get-tuple-element.5, f32[15,8,132]{2,1,0:T(8,128)S(1)} %get-tuple-element.4, ...), kind=kLoop, calls=%fused_computation.319 | loop fusion | flops 92160 | bytes 491520 | tf_op jit(solution)/shard_map/max | solution.py:121
  (85 shorter events, 7.3 us)
Async XLA Ops:
  0.6 14.7 %copy-start.1 = (bf16[16,128,128]{2,1,0:T(8,128)(2,1)S(1)}, bf16[16,128,128]{2,1,0:T(8,128)(2,1)}, u32[]{:S(2)}) copy-start(bf16[16,128,128]{2,1,0:T(8,128)(2,1)} %param.4) | copy-start | bytes 1572868
  2.7 14.7 %collective-permute-start = (bf16[30840]{0:T(1024)(128)(2,1)S(1)}, bf16[30840]{0:T(1024)(128)(2,1)S(1)}, u32[]{:S(2)}, u32[]{:S(2)}) collective-permute-start(bf16[30840]{0:T(1024)(128)(2,1)S(1)} %pad_maximum_fusion.5), channel_id=1, source_target_pairs={{1,0},{2,1},{3,2},{4,3},{5,4},{6,5},{7,6},{8,7},{9,8},{10,9},{11,1... | collective-permute-start | bytes 185048 | tf_op jit(solution)/shard_map/ppermute | solution.py:32
  18.0 4.6 %collective-permute-start.1 = (f32[16,128,128]{1,0,2:T(8,128)S(1)}, f32[16,128,128]{1,0,2:T(8,128)S(1)}, u32[]{:S(2)}, u32[]{:S(2)}) collective-permute-start(f32[16,128,128]{1,0,2:T(8,128)S(1)} %pad_maximum_fusion), channel_id=1, source_target_pairs={{0,32},{32,0},{1,33},{33,1},{2,34},{34,2},{3,35},{35,3},{4,36},{36... | collective-permute-start | bytes 3145736 | tf_op jit(solution)/shard_map/ppermute | solution.py:77
  22.5 7.1 %copy-start = (s32[15,8,16]{2,1,0:T(8,128)S(1)}, s32[15,8,16]{2,1,0:T(8,128)}, u32[]{:S(2)}) copy-start(s32[15,8,16]{2,1,0:T(8,128)} %param.6) | copy-start | bytes 23044
  22.7 7.5 %copy-start.2 = (s32[15,2]{0,1:T(2,128)S(1)}, s32[15,2]{0,1:T(2,128)}, u32[]{:S(2)}) copy-start(s32[15,2]{0,1:T(2,128)} %param.7) | copy-start | bytes 364
  24.2 21.7 %all-to-all-start = ((f32[16,8,16,128]{3,2,0,1:T(8,128)}), f32[16,8,16,128]{3,2,0,1:T(8,128)S(1)}, u32[]{:S(2)}, u32[]{:S(2)}) async-start(f32[16,8,16,128]{3,2,0,1:T(8,128)} %copy.28), calls=%async_computation | async-start | bytes 2097152 | tf_op jit(solution)/shard_map/all_to_all | solution.py:79
  46.2 10.4 %collective-permute-start.2 = (f32[8824]{0:T(1024)S(1)}, f32[8824]{0:T(1024)S(1)}, u32[]{:S(2)}, u32[]{:S(2)}) collective-permute-start(f32[8824]{0:T(1024)S(1)} %pad_maximum_fusion.6), channel_id=1, source_target_pairs={{0,1},{1,2},{2,3},{3,4},{4,5},{5,6},{6,7},{7,8},{8,9},{9,10},{10,1... | collective-permute-start | bytes 105896 | tf_op jit(solution)/shard_map/ppermute | solution.py:27
  48.1 12.9 %collective-permute-start.3 = (f32[16,16,34]{2,1,0:T(8,128)S(1)}, f32[16,16,34]{2,1,0:T(8,128)S(1)}, u32[]{:S(2)}, u32[]{:S(2)}) collective-permute-start(f32[16,16,34]{2,1,0:T(8,128)S(1)} %get-tuple-element.18), channel_id=1, source_target_pairs={{1,0},{2,1},{3,2},{4,3},{5,4},{6,5},{7,6},{8,7},{9,8},{10,9},{11,1... | collective-permute-start | bytes 104456 | tf_op jit(solution)/shard_map/ppermute | solution.py:32

commit v7 on v6

--- a/solution.py
+++ b/solution.py
@@ -38,7 +38,7 @@
         weights,
         window_strides=(1,),
         padding="VALID",
-        dimension_numbers=("NWC", "WIO", "NCW"),
+        dimension_numbers=("NWC", "WIO", "CNW"),
         preferred_element_type=jnp.float32,
     )
 
@@ -75,8 +75,8 @@
     vol_other = beam(w_other)
     vol_mine = beam(w_mine)
     vol = vol_mine + lax.ppermute(vol_other, "cc", [(0, 1), (1, 0)])
-    vol = vol.reshape(frames, nx * ny, per_dev, sample_rows)
-    vol = lax.all_to_all(vol, ("cx", "cy"), 1, 1, tiled=True).sum(axis=1)
+    vol = vol.reshape(nx * ny, per_dev, frames, sample_rows)
+    vol = lax.all_to_all(vol, ("cx", "cy"), 0, 0, tiled=True).sum(axis=0).transpose(1, 0, 2)
 
     head = vol[..., :HALO]
     tail = vol[..., sample_rows - HALO :]

time: 79.2 us -> 79.3 us (level)
    add x1, local copies, waits for them, and re-layouts: 0.42 us -> 1.58 us  [shards(): vol = vol_mine + lax.ppermute(vol_other, 'cc', [(0, 1), (1, 0)])]
    reshape x1 -> x0, local copies, waits for them, and re-layouts: 1.07 us -> none  [shards(): vol = vol.reshape(frames, nx * ny, per_dev, sample_rows)]
where the time goes in v7:
time: 79.3 us; the launch traced here: 79 us
  starting transfers between devices  28.2 us (36%)
  waiting for transfers between devices  20 us (25%)
  other arithmetic  16.3 us (21%)
  local copies, waits for them, and re-layouts  8.1 us (10%)
  matrix products  5.03 us (6%)
  between operations  1.37 us (2%)
    ppermute x2, starting transfers between devices, from_right(): return lax.ppermute(block, axis, [(i + 1, i) for i in range(count - 1)])  19 us
    all_to_all x1, waiting for transfers between devices, shards(): lax.all_to_all(vol, ('cx', 'cy'), 0, 0, tiled=True).sum(axis=0)  15.6 us
    add x13, other arithmetic, window_sum(): values = values[..., :n] + values[..., width:width + n]  6.35 us
    all_to_all x1, starting transfers between devices, shards(): lax.all_to_all(vol, ('cx', 'cy'), 0, 0, tiled=True).sum(axis=0)  5.31 us
    conv_general_dilated x4, matrix products, beamform(): lax.conv_general_dilated(extended, weights, window_strides=(1,), padding=...  5.03 us
    ppermute x2, waiting for transfers between devices, from_right(): return lax.ppermute(block, axis, [(i + 1, i) for i in range(count - 1)])  4.31 us
    unnamed x32, other arithmetic  4.24 us
    ppermute x1, starting transfers between devices, from_left(): return lax.ppermute(block, axis, [(i, i + 1) for i in range(count - 1)])  1.92 us
  transfers between devices with their start and end apart: 5, of which 3 were waited for; matrix products, arithmetic and copies ran while one was open for 9% of the time, Pallas kernels for 0%

profile of v7, /device:TPU:32, one launch (start us, length us, event | category | flops | bytes accessed | tf_op | source)
XLA Modules:
  0.0 79.0 jit_solution(2184509455624113543)
XLA Ops:
  0.6 1.0 %fusion.145 = bf16[15,8]{1,0:T(8,128)(2,1)S(1)} fusion(s32[15,8,16]{2,1,0:T(8,128)} %param.6), kind=kLoop, calls=%fused_computation.329 | loop fusion | flops 120 | bytes 720 | tf_op jit(solution)/shard_map/slice | solution.py:57
  1.7 0.9 %fusion.161 = (bf16[16,15,128]{2,1,0:T(8,128)(2,1)S(1)}, bf16[16,15,128]{2,1,0:T(8,128)(2,1)S(1)}) fusion(bf16[16,128,128]{2,1,0:T(8,128)(2,1)} %param.4), kind=kLoop, calls=%fused_computation.346 | loop fusion | bytes 245760 | tf_op jit(solution)/shard_map/slice | solution.py:63
  2.7 10.7 %collective-permute-start = (bf16[30840]{0:T(1024)(128)(2,1)S(1)}, bf16[30840]{0:T(1024)(128)(2,1)S(1)}, u32[]{:S(2)}, u32[]{:S(2)}) collective-permute-start(bf16[30840]{0:T(1024)(128)(2,1)S(1)} %pad_maximum_fusion.5), channel_id=1, source_target_pairs={{1,0},{2,1},{3,2},{4,3},{5,4},{6,5},{7,6},{8,7},{9,8},{10,9},{11,1... | collective-permute-start | bytes 185048 | tf_op jit(solution)/shard_map/ppermute | solution.py:32
  13.4 1.6 %copy.22 = bf16[1,16,128,256]{2,3,1,0:T(8,128)(2,1)S(1)} copy(bf16[1,16,128,256]{3,2,1,0:T(8,128)(2,1)} %param.5) | data formatting | bytes 2097152 | tf_op args[1]
  15.1 0.2 constant_dynamic-slice_fusion.1
  15.3 2.1 %fusion.150 = f32[128,16,113]{0,1,2:T(8,128)S(1)} fusion(bf16[16,128,128]{1,2,0:T(8,128)(2,1)S(1)} %bitcast.584, bf16[16,128,128]{2,1,0:T(8,128)(2,1)S(1)} %copy-done.1), kind=kOutput, calls=%fused_computation.342 | convolution fusion | flops 947912704 | bytes 1974272 | tf_op jit(solution)/shard_map/conv_general_dilated | solution.py:36
  17.5 0.4 fusion.140
  18.0 1.9 %collective-permute-start.1 = (f32[128,16,128]{0,1,2:T(8,128)S(1)}, f32[128,16,128]{0,1,2:T(8,128)S(1)}, u32[]{:S(2)}, u32[]{:S(2)}) collective-permute-start(f32[128,16,128]{0,1,2:T(8,128)S(1)} %pad_maximum_fusion), channel_id=1, source_target_pairs={{0,32},{32,0},{1,33},{33,1},{2,34},{34,2},{3,35},{35,3},{4,36},{36... | collective-permute-start | bytes 3145736 | tf_op jit(solution)/shard_map/ppermute | solution.py:77
  19.9 2.1 %fusion.152 = f32[128,16,113]{0,1,2:T(8,128)S(1)} fusion(bf16[16,128,128]{1,2,0:T(8,128)(2,1)S(1)} %bitcast.582, bf16[16,128,128]{2,1,0:T(8,128)(2,1)S(1)} %copy-done.1), kind=kOutput, calls=%fused_computation.344 | convolution fusion | flops 947912704 | bytes 1974272 | tf_op jit(solution)/shard_map/conv_general_dilated | solution.py:36
  22.1 0.4 fusion.141
  22.7 1.6 %copy.27 = f32[128,16,128]{2,1,0:T(8,128)} copy(f32[128,16,128]{0,1,2:T(8,128)S(1)} %maximum_add_fusion) | data formatting | bytes 2097152 | tf_op jit(solution)/shard_map/add | solution.py:77
  24.3 5.3 %all-to-all-start = ((f32[8,16,16,128]{3,2,1,0:T(8,128)}), f32[8,16,16,128]{3,2,1,0:T(8,128)S(1)}, u32[]{:S(2)}, u32[]{:S(2)}) async-start(f32[8,16,16,128]{3,2,1,0:T(8,128)} %bitcast.3), calls=%async_computation | async-start | bytes 2097152 | tf_op jit(solution)/shard_map/all_to_all | solution.py:79
  29.8 0.2 copy.33
  30.0 0.2 slice_reduce_fusion
  30.3 15.6 %all-to-all-done = f32[8,16,16,128]{3,2,1,0:T(8,128)S(1)} async-done(((f32[8,16,16,128]{3,2,1,0:T(8,128)}), f32[8,16,16,128]{3,2,1,0:T(8,128)S(1)}, u32[]{:S(2)}, u32[]{:S(2)}) %all-to-all-start) | async-done | bytes 1048608 | tf_op jit(solution)/shard_map/all_to_all | solution.py:79
  46.3 1.9 %collective-permute-start.2 = (f32[8824]{0:T(1024)S(1)}, f32[8824]{0:T(1024)S(1)}, u32[]{:S(2)}, u32[]{:S(2)}) collective-permute-start(f32[8824]{0:T(1024)S(1)} %pad_maximum_fusion.6), channel_id=1, source_target_pairs={{0,1},{1,2},{2,3},{3,4},{4,5},{5,6},{6,7},{7,8},{8,9},{9,10},{10,1... | collective-permute-start | bytes 105896 | tf_op jit(solution)/shard_map/ppermute | solution.py:27
  48.3 8.3 %collective-permute-start.3 = (f32[16,16,34]{2,1,0:T(8,128)S(1)}, f32[16,16,34]{2,1,0:T(8,128)S(1)}, u32[]{:S(2)}, u32[]{:S(2)}) collective-permute-start(f32[16,16,34]{2,1,0:T(8,128)S(1)} %get-tuple-element.18), channel_id=1, source_target_pairs={{1,0},{2,1},{3,2},{4,3},{5,4},{6,5},{7,6},{8,7},{9,8},{10,9},{11,1... | collective-permute-start | bytes 104456 | tf_op jit(solution)/shard_map/ppermute | solution.py:32
  56.9 4.3 %collective-permute-done.3 = f32[16,16,34]{2,1,0:T(8,128)S(1)} collective-permute-done((f32[16,16,34]{2,1,0:T(8,128)S(1)}, f32[16,16,34]{2,1,0:T(8,128)S(1)}, u32[]{:S(2)}, u32[]{:S(2)}) %collective-permute-start.3) | collective-permute-done | bytes 34848 | tf_op jit(solution)/shard_map/ppermute | solution.py:32
  61.2 0.2 pad_maximum_fusion.1
  61.3 0.6 gather_fusion.1
  62.1 0.2 fusion.163
  63.0 0.6 gather_fusion
  63.7 0.6 fusion.162
  68.9 1.1 %slice_add_fusion.4 = f32[33,15,8,162]{3,2,1,0:T(8,128)S(1)} fusion(f32[33,15,8,163]{3,2,1,0:T(8,128)S(1)} %fusion.42), kind=kLoop, calls=%fused_computation.6 | loop fusion | flops 641520 | bytes 7698240 | tf_op jit(solution)/shard_map/add | solution.py:20
  70.0 1.1 %slice_add_fusion.3 = f32[33,15,8,160]{3,2,1,0:T(8,128)S(1)} fusion(f32[33,15,8,162]{3,2,1,0:T(8,128)S(1)} %slice_add_fusion.4), kind=kLoop, calls=%fused_computation.5 | loop fusion | flops 633600 | bytes 7603200 | tf_op jit(solution)/shard_map/add | solution.py:20
  71.1 1.1 %slice_add_fusion.2 = f32[33,15,8,156]{3,2,1,0:T(8,128)S(1)} fusion(f32[33,15,8,160]{3,2,1,0:T(8,128)S(1)} %slice_add_fusion.3), kind=kLoop, calls=%fused_computation.4 | loop fusion | flops 617760 | bytes 7413120 | tf_op jit(solution)/shard_map/add | solution.py:20
  72.3 1.1 %slice_add_fusion.1 = f32[33,15,8,148]{3,2,1,0:T(8,128)S(1)} fusion(f32[33,15,8,156]{3,2,1,0:T(8,128)S(1)} %slice_add_fusion.2), kind=kLoop, calls=%fused_computation.3 | loop fusion | flops 586080 | bytes 7032960 | tf_op jit(solution)/shard_map/add | solution.py:20
  73.4 1.1 %slice_add_fusion = f32[33,15,8,132]{3,2,1,0:T(8,128)S(1)} fusion(f32[33,15,8,148]{3,2,1,0:T(8,128)S(1)} %slice_add_fusion.1), kind=kLoop, calls=%fused_computation.2 | loop fusion | flops 522720 | bytes 6272640 | tf_op jit(solution)/shard_map/add | solution.py:20
  75.1 1.5 %add_select_fusion = (f32[15,8,132]{2,1,0:T(8,128)S(1)}, f32[15,8,132]{2,1,0:T(8,128)S(1)}, f32[15,8,132]{2,1,0:T(8,128)S(1)}, f32[15,8,132]{2,1,0:T(8,128)S(1)}...) fusion(f32[15,8,2]{2,1,0:T(8,128)S(1)} %reshape.86, ...), kind=kLoop, calls=%fused_computation.300 | loop fusion | flops 3453120 | bytes 4878852 | tf_op jit(solution)/shard_map/jit(_where)/select_n | solution.py:131
  76.6 0.9 %maximum_maximum_fusion = f32[15,8,132]{2,1,0:T(8,128)S(1)} fusion(f32[15,8,132]{2,1,0:T(8,128)S(1)} %get-tuple-element.9, f32[15,8,164]{2,1,0:T(8,128)S(1)} %fusion.35, f32[33,15,8,132]{3,2,1,0:T(8,128)S(1)} %slice_add_fusion), kind=kLoop, calls=%fused_computation.301 | loop fusion | flops 1267200 | bytes 3548160 | tf_op jit(solution)/shard_map/max | solution.py:121
  77.5 0.7 fusion.142
  78.2 0.8 %slice_maximum_fusion = f32[15,8,128]{2,1,0:T(8,128)} fusion(f32[15,8,132]{2,1,0:T(8,128)S(1)} %get-tuple-element.8, f32[15,8,132]{2,1,0:T(8,128)S(1)} %get-tuple-element.7, f32[15,8,132]{2,1,0:T(8,128)S(1)} %get-tuple-element.6, f32[15,8,132]{2,1,0:T(8,128)S(1)} %get-tuple-element.5, f32[15,8,132]{2,1,0:T(8,128)S(1)} %get-tuple-element.4, ...), kind=kLoop, calls=%fused_computation.320 | loop fusion | flops 92160 | bytes 491520 | tf_op jit(solution)/shard_map/max | solution.py:121
  (85 shorter events, 7.2 us)
Async XLA Ops:
  0.6 14.7 %copy-start.1 = (bf16[16,128,128]{2,1,0:T(8,128)(2,1)S(1)}, bf16[16,128,128]{2,1,0:T(8,128)(2,1)}, u32[]{:S(2)}) copy-start(bf16[16,128,128]{2,1,0:T(8,128)(2,1)} %param.4) | copy-start | bytes 1572868
  2.7 14.7 %collective-permute-start = (bf16[30840]{0:T(1024)(128)(2,1)S(1)}, bf16[30840]{0:T(1024)(128)(2,1)S(1)}, u32[]{:S(2)}, u32[]{:S(2)}) collective-permute-start(bf16[30840]{0:T(1024)(128)(2,1)S(1)} %pad_maximum_fusion.5), channel_id=1, source_target_pairs={{1,0},{2,1},{3,2},{4,3},{5,4},{6,5},{7,6},{8,7},{9,8},{10,9},{11,1... | collective-permute-start | bytes 185048 | tf_op jit(solution)/shard_map/ppermute | solution.py:32
  18.0 4.6 %collective-permute-start.1 = (f32[128,16,128]{0,1,2:T(8,128)S(1)}, f32[128,16,128]{0,1,2:T(8,128)S(1)}, u32[]{:S(2)}, u32[]{:S(2)}) collective-permute-start(f32[128,16,128]{0,1,2:T(8,128)S(1)} %pad_maximum_fusion), channel_id=1, source_target_pairs={{0,32},{32,0},{1,33},{33,1},{2,34},{34,2},{3,35},{35,3},{4,36},{36... | collective-permute-start | bytes 3145736 | tf_op jit(solution)/shard_map/ppermute | solution.py:77
  22.1 7.6 %copy-start = (s32[15,8,16]{2,1,0:T(8,128)S(1)}, s32[15,8,16]{2,1,0:T(8,128)}, u32[]{:S(2)}) copy-start(s32[15,8,16]{2,1,0:T(8,128)} %param.6) | copy-start | bytes 23044
  22.5 7.8 %copy-start.2 = (s32[15,2]{0,1:T(2,128)S(1)}, s32[15,2]{0,1:T(2,128)}, u32[]{:S(2)}) copy-start(s32[15,2]{0,1:T(2,128)} %param.7) | copy-start | bytes 364
  24.3 21.7 %all-to-all-start = ((f32[8,16,16,128]{3,2,1,0:T(8,128)}), f32[8,16,16,128]{3,2,1,0:T(8,128)S(1)}, u32[]{:S(2)}, u32[]{:S(2)}) async-start(f32[8,16,16,128]{3,2,1,0:T(8,128)} %bitcast.3), calls=%async_computation | async-start | bytes 2097152 | tf_op jit(solution)/shard_map/all_to_all | solution.py:79
  46.3 10.4 %collective-permute-start.2 = (f32[8824]{0:T(1024)S(1)}, f32[8824]{0:T(1024)S(1)}, u32[]{:S(2)}, u32[]{:S(2)}) collective-permute-start(f32[8824]{0:T(1024)S(1)} %pad_maximum_fusion.6), channel_id=1, source_target_pairs={{0,1},{1,2},{2,3},{3,4},{4,5},{5,6},{6,7},{7,8},{8,9},{9,10},{10,1... | collective-permute-start | bytes 105896 | tf_op jit(solution)/shard_map/ppermute | solution.py:27
  48.3 12.9 %collective-permute-start.3 = (f32[16,16,34]{2,1,0:T(8,128)S(1)}, f32[16,16,34]{2,1,0:T(8,128)S(1)}, u32[]{:S(2)}, u32[]{:S(2)}) collective-permute-start(f32[16,16,34]{2,1,0:T(8,128)S(1)} %get-tuple-element.18), channel_id=1, source_target_pairs={{1,0},{2,1},{3,2},{4,3},{5,4},{6,5},{7,6},{8,7},{9,8},{10,9},{11,1... | collective-permute-start | bytes 104456 | tf_op jit(solution)/shard_map/ppermute | solution.py:32

commit v8 on v6

--- a/solution.py
+++ b/solution.py
@@ -20,6 +20,43 @@
         values = values[..., :n] + values[..., width : width + n]
         width *= 2
     return values
+
+
+def lag_scores(vol, frame_pairs, line_count, peak):
+    lead = vol.shape[:-3]
+    pair_count = frame_pairs.shape[0]
+    front = jnp.take(vol, frame_pairs[:, 0], axis=-3).reshape(lead + (pair_count, line_count, 2, -1))
+    later = jnp.take(vol, frame_pairs[:, 1], axis=-3).reshape(lead + (pair_count, line_count, 2, -1))
+    out_len = vol.shape[-1] - (2 * MAXLAG + WIN - 1)
+    prod_len = out_len + WIN - 1
+    xr = front[..., 0, WIN // 2 : WIN // 2 + prod_len]
+    xi = front[..., 1, WIN // 2 : WIN // 2 + prod_len]
+    yr = later[..., 0, :]
+    yi = later[..., 1, :]
+    nlag = 2 * MAXLAG + 1
+    prods = jnp.stack(
+        [xr * yr[..., j : j + prod_len] + xi * yi[..., j : j + prod_len] for j in range(nlag)]
+    )
+    cross_sum = window_sum(prods)
+    power_a = window_sum(xr * xr + xi * xi) / (2 * WIN)
+    ey = yr * yr + yi * yi
+    power_full = window_sum(ey[..., : out_len + nlag - 1 + WIN - 1]) / (2 * WIN)
+    root_b = jnp.sqrt(power_full + epsilon)
+    root_a = 2 * WIN * jnp.sqrt(power_a + epsilon)
+    want = peak + MAXLAG
+    best = None
+    at_prev = jnp.zeros_like(root_a)
+    centre = jnp.zeros_like(root_a)
+    at_next = jnp.zeros_like(root_a)
+    for j in range(nlag):
+        score = cross_sum[j] / (root_a * root_b[..., j : j + out_len])
+        best = score if best is None else jnp.maximum(best, score)
+        at_prev = jnp.where(want == j + 1, score, at_prev)
+        centre = jnp.where(want == j, score, centre)
+        at_next = jnp.where(want == j - 1, score, at_next)
+    curvature = jnp.maximum(2.0 * centre - at_prev - at_next, 0.25)
+    displacement = peak.astype(jnp.float32) + (at_next - at_prev) / (2.0 * curvature)
+    return best, displacement
 
 
 def from_left(block, axis):
@@ -84,48 +121,38 @@
     got = from_left(sent, "tile")
     left = got[: tail.size].reshape(tail.shape)
     lag_prev = got[tail.size :].reshape(pairs_n, lines_n, 1)
-    padded = jnp.concatenate([left, vol, from_right(head, "tile")], axis=2)
-
-    line_count = per_dev // 2
-    pair_count = frame_pairs.shape[0]
-    front = padded[frame_pairs[:, 0]].reshape(pair_count, line_count, 2, -1)
-    later = padded[frame_pairs[:, 1]].reshape(pair_count, line_count, 2, -1)
-    out_len = sample_rows + 4
-    prod_len = out_len + WIN - 1
-    xr = front[:, :, 0, WIN // 2 : WIN // 2 + prod_len]
-    xi = front[:, :, 1, WIN // 2 : WIN // 2 + prod_len]
-    yr = later[:, :, 0]
-    yi = later[:, :, 1]
-    nlag = 2 * MAXLAG + 1
-    prods = jnp.stack(
-        [xr * yr[..., j : j + prod_len] + xi * yi[..., j : j + prod_len] for j in range(nlag)]
-    )
-    cross_sum = window_sum(prods)
-    power_a = window_sum(xr * xr + xi * xi) / (2 * WIN)
-    ey = yr * yr + yi * yi
-    power_full = window_sum(ey[..., : out_len + nlag - 1 + WIN - 1]) / (2 * WIN)
-    root_b = jnp.sqrt(power_full + epsilon)
-    root_a = 2 * WIN * jnp.sqrt(power_a + epsilon)
+    right = from_right(head, "tile")
 
     own = jnp.repeat(lag_f, BLK, axis=2)
     peak_full = jnp.concatenate(
         [jnp.repeat(lag_prev, 2, axis=2), own, jnp.repeat(lag_next, 2, axis=2)], axis=2
     ).astype(jnp.int32)
-    want = peak_full + MAXLAG
-    best = None
-    at_prev = jnp.zeros_like(root_a)
-    centre = jnp.zeros_like(root_a)
-    at_next = jnp.zeros_like(root_a)
-    for j in range(nlag):
-        score = cross_sum[j] / (root_a * root_b[..., j : j + out_len])
-        best = score if best is None else jnp.maximum(best, score)
-        at_prev = jnp.where(want == j + 1, score, at_prev)
-        centre = jnp.where(want == j, score, centre)
-        at_next = jnp.where(want == j - 1, score, at_next)
+    line_count = per_dev // 2
+    reach = 2 * MAXLAG + WIN - 1
+    out_len = sample_rows + 4
+    inner_lo = HALO
+    inner_len = sample_rows - 2 * HALO + 4
+    inner = lag_scores(
+        vol[..., : inner_len + reach],
+        frame_pairs,
+        line_count,
+        peak_full[..., inner_lo : inner_lo + inner_len],
+    )
+    edge_len = (out_len - inner_len) // 2
+    edge_rows = edge_len + reach
+    right_from = out_len - edge_len - HALO
+    edges = jnp.stack(
+        [
+            jnp.concatenate([left, vol[..., : edge_rows - HALO]], axis=2),
+            jnp.concatenate([vol[..., right_from:], right[..., : edge_rows - (sample_rows - right_from)]], axis=2),
+        ]
+    )
+    edge_peak = jnp.stack([peak_full[..., :edge_len], peak_full[..., out_len - edge_len :]])
+    outer = lag_scores(edges, frame_pairs, line_count, edge_peak)
+    best, displacement = (
+        jnp.concatenate([o[0], i, o[1]], axis=-1) for i, o in zip(inner, outer)
+    )
     quality = best[..., 2 : 2 + sample_rows]
-
-    curvature = jnp.maximum(2.0 * centre - at_prev - at_next, 0.25)
-    displacement = peak_full.astype(jnp.float32) + (at_next - at_prev) / (2.0 * curvature)
     zo = lax.broadcasted_iota(jnp.int32, displacement.shape, 2)
     outside = ((tile == 0) & (zo < 2)) | ((tile == tiles - 1) & (zo >= sample_rows + 2))
     dz = jnp.where(outside, 0.0, displacement)

time: 79.2 us -> 84.5 us (1.067)
  the two profiles are of different devices: /device:TPU:32 before, /device:TPU:56 now
where the time goes in v8:
time: 84.5 us; the launch traced here: 84.1 us
  starting transfers between devices  28.2 us (33%)
  other arithmetic  25.2 us (30%)
  waiting for transfers between devices  14.4 us (17%)
  local copies, waits for them, and re-layouts  9.42 us (11%)
  matrix products  5.03 us (6%)
  between operations  1.83 us (2%)
    ppermute x2, starting transfers between devices, from_right(): return lax.ppermute(block, axis, [(i + 1, i) for i in range(count - 1)])  18.4 us
    all_to_all x1, waiting for transfers between devices, shards(): vol = lax.all_to_all(vol, ('cx', 'cy'), 1, 1, tiled=True).sum(axis=1)  14.3 us
    add x26, other arithmetic, window_sum(): values = values[..., :n] + values[..., width:width + n]  10.1 us
    unnamed x64, other arithmetic  7.18 us
    all_to_all x1, starting transfers between devices, shards(): vol = lax.all_to_all(vol, ('cx', 'cy'), 1, 1, tiled=True).sum(axis=1)  5.75 us
    conv_general_dilated x4, matrix products, beamform(): lax.conv_general_dilated(extended, weights, window_strides=(1,), padding=...  5.03 us
    add x2, other arithmetic, lag_scores(): peak.astype(jnp.float32) + (at_next - at_prev) / (2.0 * curvature)  2.22 us
    ppermute x1, starting transfers between devices, from_left(): return lax.ppermute(block, axis, [(i, i + 1) for i in range(count - 1)])  2.1 us
  transfers between devices with their start and end apart: 5, of which 2 were waited for; matrix products, arithmetic and copies ran while one was open for 18% of the time, Pallas kernels for 0%

profile of v8, /device:TPU:56, one launch (start us, length us, event | category | flops | bytes accessed | tf_op | source)
XLA Modules:
  0.0 84.1 jit_solution(9515925564406833554)
XLA Ops:
  0.6 1.0 %fusion.217 = bf16[15,8]{1,0:T(8,128)(2,1)S(1)} fusion(s32[15,8,16]{2,1,0:T(8,128)} %param.10), kind=kLoop, calls=%fused_computation.636 | loop fusion | flops 120 | bytes 720 | tf_op jit(solution)/shard_map/slice | solution.py:94
  1.7 0.9 %fusion.224 = (bf16[16,15,128]{2,1,0:T(8,128)(2,1)S(1)}, bf16[16,15,128]{2,1,0:T(8,128)(2,1)S(1)}) fusion(bf16[16,128,128]{2,1,0:T(8,128)(2,1)} %param.8), kind=kLoop, calls=%fused_computation.653 | loop fusion | bytes 245760 | tf_op jit(solution)/shard_map/slice | solution.py:100
  2.7 12.5 %collective-permute-start = (bf16[30840]{0:T(1024)(128)(2,1)S(1)}, bf16[30840]{0:T(1024)(128)(2,1)S(1)}, u32[]{:S(2)}, u32[]{:S(2)}) collective-permute-start(bf16[30840]{0:T(1024)(128)(2,1)S(1)} %pad_maximum_fusion.5), channel_id=1, source_target_pairs={{1,0},{2,1},{3,2},{4,3},{5,4},{6,5},{7,6},{8,7},{9,8},{10,9},{11,1... | collective-permute-start | bytes 185048 | tf_op jit(solution)/shard_map/ppermute | solution.py:69
  15.2 1.6 %copy.43 = bf16[1,16,128,256]{2,3,1,0:T(8,128)(2,1)S(1)} copy(bf16[1,16,128,256]{3,2,1,0:T(8,128)(2,1)} %param.9) | data formatting | bytes 2097152 | tf_op args[1]
  17.1 2.1 %fusion.220 = f32[16,128,113]{1,0,2:T(8,128)S(1)} fusion(bf16[16,128,128]{1,2,0:T(8,128)(2,1)S(1)} %bitcast.1141, bf16[16,128,128]{2,1,0:T(8,128)(2,1)S(1)} %copy-done.1), kind=kOutput, calls=%fused_computation.649 | convolution fusion | flops 947912704 | bytes 1974272 | tf_op jit(solution)/shard_map/conv_general_dilated | solution.py:73
  19.8 1.9 %collective-permute-start.1 = (f32[16,128,128]{1,0,2:T(8,128)S(1)}, f32[16,128,128]{1,0,2:T(8,128)S(1)}, u32[]{:S(2)}, u32[]{:S(2)}) collective-permute-start(f32[16,128,128]{1,0,2:T(8,128)S(1)} %pad_maximum_fusion), channel_id=1, source_target_pairs={{0,32},{32,0},{1,33},{33,1},{2,34},{34,2},{3,35},{35,3},{4,36},{36... | collective-permute-start | bytes 3145736 | tf_op jit(solution)/shard_map/ppermute | solution.py:114
  21.7 2.1 %fusion.222 = f32[16,128,113]{1,0,2:T(8,128)S(1)} fusion(bf16[16,128,128]{1,2,0:T(8,128)(2,1)S(1)} %bitcast.1139, bf16[16,128,128]{2,1,0:T(8,128)(2,1)S(1)} %copy-done.1), kind=kOutput, calls=%fused_computation.651 | convolution fusion | flops 947912704 | bytes 1974272 | tf_op jit(solution)/shard_map/conv_general_dilated | solution.py:73
  25.0 1.1 %copy.49 = f32[16,8,16,128]{3,2,0,1:T(8,128)} copy(f32[16,8,16,128]{3,2,1,0:T(8,128)S(1)} %bitcast.1135) | data formatting | bytes 2097152 | tf_op jit(solution)/shard_map/reshape | solution.py:115
  26.0 5.8 %all-to-all-start = ((f32[16,8,16,128]{3,2,0,1:T(8,128)}), f32[16,8,16,128]{3,2,0,1:T(8,128)S(1)}, u32[]{:S(2)}, u32[]{:S(2)}) async-start(f32[16,8,16,128]{3,2,0,1:T(8,128)} %copy.49), calls=%async_computation | async-start | bytes 2097152 | tf_op jit(solution)/shard_map/all_to_all | solution.py:116
  32.6 14.3 %all-to-all-done = f32[16,8,16,128]{3,2,0,1:T(8,128)S(1)} async-done(((f32[16,8,16,128]{3,2,0,1:T(8,128)}), f32[16,8,16,128]{3,2,0,1:T(8,128)S(1)}, u32[]{:S(2)}, u32[]{:S(2)}) %all-to-all-start) | async-done | bytes 1048608 | tf_op jit(solution)/shard_map/all_to_all | solution.py:116
  47.1 0.6 gather_fusion.3
  47.7 0.6 gather_fusion.2
  48.8 5.9 %collective-permute-start.3 = (f32[16,16,34]{2,1,0:T(8,128)S(1)}, f32[16,16,34]{2,1,0:T(8,128)S(1)}, u32[]{:S(2)}, u32[]{:S(2)}) collective-permute-start(f32[16,16,34]{2,1,0:T(8,128)S(1)} %get-tuple-element.17), channel_id=1, source_target_pairs={{1,0},{2,1},{3,2},{4,3},{5,4},{6,5},{7,6},{8,7},{9,8},{10,9},{11,1... | collective-permute-start | bytes 104456 | tf_op jit(solution)/shard_map/ppermute | solution.py:69
  54.9 2.1 %collective-permute-start.2 = (f32[8824]{0:T(1024)S(1)}, f32[8824]{0:T(1024)S(1)}, u32[]{:S(2)}, u32[]{:S(2)}) collective-permute-start(f32[8824]{0:T(1024)S(1)} %pad_maximum_fusion.8), channel_id=1, source_target_pairs={{0,1},{1,2},{2,3},{3,4},{4,5},{5,6},{6,7},{7,8},{8,9},{9,10},{10,1... | collective-permute-start | bytes 105896 | tf_op jit(solution)/shard_map/ppermute | solution.py:64
  60.9 0.6 slice_add_fusion.9
  61.5 0.6 slice_add_fusion.8
  62.0 0.6 slice_add_fusion.7
  62.6 0.6 slice_add_fusion.6
  63.2 0.6 slice_add_fusion.5
  64.2 0.6 maximum_maximum_fusion.1
  65.3 0.6 gather_fusion
  67.3 0.8 divide_add_fusion.1
  68.6 0.6 fusion.225
  73.7 1.1 %slice_add_fusion.4 = f32[33,2,15,8,64]{4,3,2,1,0:T(8,128)S(1)} fusion(f32[33,2,15,8,65]{4,3,2,1,0:T(8,128)S(1)} %constant_dynamic-update-slice_fusion), kind=kLoop, calls=%fused_computation.8 | loop fusion | flops 506880 | bytes 6082560 | tf_op jit(solution)/shard_map/add | solution.py:20
  74.8 1.1 %slice_add_fusion.3 = f32[33,2,15,8,62]{4,3,2,1,0:T(8,128)S(1)} fusion(f32[33,2,15,8,64]{4,3,2,1,0:T(8,128)S(1)} %slice_add_fusion.4), kind=kLoop, calls=%fused_computation.7 | loop fusion | flops 491040 | bytes 5892480 | tf_op jit(solution)/shard_map/add | solution.py:20
  75.9 1.3 %slice_add_fusion.2 = f32[33,2,15,8,58]{4,3,2,1,0:T(8,128)S(1)} fusion(f32[33,2,15,8,62]{4,3,2,1,0:T(8,128)S(1)} %slice_add_fusion.3), kind=kLoop, calls=%fused_computation.6 | loop fusion | flops 459360 | bytes 5512320 | tf_op jit(solution)/shard_map/add | solution.py:20
  77.2 1.1 %slice_add_fusion.1 = f32[33,2,15,8,50]{4,3,2,1,0:T(8,128)S(1)} fusion(f32[33,2,15,8,58]{4,3,2,1,0:T(8,128)S(1)} %slice_add_fusion.2), kind=kLoop, calls=%fused_computation.5 | loop fusion | flops 396000 | bytes 4752000 | tf_op jit(solution)/shard_map/add | solution.py:20
  78.4 1.1 %slice_add_fusion = f32[33,2,15,8,34]{4,3,2,1,0:T(8,128)S(1)} fusion(f32[33,2,15,8,50]{4,3,2,1,0:T(8,128)S(1)} %slice_add_fusion.1), kind=kLoop, calls=%fused_computation.4 | loop fusion | flops 269280 | bytes 3231360 | tf_op jit(solution)/shard_map/add | solution.py:20
  79.9 1.1 %maximum_maximum_fusion = f32[2,15,8,34]{3,2,1,0:T(8,128)S(1)} fusion(f32[2,15,8,66]{3,2,1,0:T(8,128)S(1)} %fusion.35, f32[33,2,15,8,34]{4,3,2,1,0:T(8,128)S(1)} %slice_add_fusion, f32[2,15,8,50]{3,2,1,0:T(8,128)S(1)} %slice_add_fusion.16), kind=kLoop, calls=%fused_computation.343 | loop fusion | flops 832320 | bytes 2252160 | tf_op jit(solution)/shard_map/max | solution.py:53
  81.0 1.5 %divide_add_fusion = f32[2,15,8,34]{3,2,1,0:T(8,128)S(1)} fusion(s32[1,15,8,34]{3,2,1,0:T(8,128)S(1)} %get-tuple-element.21, s32[1,15,8,34]{3,2,1,0:T(8,128)S(1)} %get-tuple-element.20, f32[2,15,8,66]{3,2,1,0:T(8,128)S(1)} %fusion.35, f32[33,2,15,8,34]{4,3,2,1,0:T(8,128)S(1)} %slice_add_fusion, f32[2,15,8,50]{3,2,1,0:T(8,128)S(1)} %slice_add_fusion.16), kind=kLoop, calls=%fused_computation.342 | loop fusion | flops 1754400 | bytes 2284800 | tf_op jit(solution)/shard_map/add | solution.py:58
  82.6 0.7 fusion.108
  83.4 0.7 pad_maximum_fusion.6
  (150 shorter events, 14.6 us)
Async XLA Ops:
  0.6 16.5 %copy-start.1 = (bf16[16,128,128]{2,1,0:T(8,128)(2,1)S(1)}, bf16[16,128,128]{2,1,0:T(8,128)(2,1)}, u32[]{:S(2)}) copy-start(bf16[16,128,128]{2,1,0:T(8,128)(2,1)} %param.8) | copy-start | bytes 1572868
  2.7 16.5 %collective-permute-start = (bf16[30840]{0:T(1024)(128)(2,1)S(1)}, bf16[30840]{0:T(1024)(128)(2,1)S(1)}, u32[]{:S(2)}, u32[]{:S(2)}) collective-permute-start(bf16[30840]{0:T(1024)(128)(2,1)S(1)} %pad_maximum_fusion.5), channel_id=1, source_target_pairs={{1,0},{2,1},{3,2},{4,3},{5,4},{6,5},{7,6},{8,7},{9,8},{10,9},{11,1... | collective-permute-start | bytes 185048 | tf_op jit(solution)/shard_map/ppermute | solution.py:69
  19.8 4.6 %collective-permute-start.1 = (f32[16,128,128]{1,0,2:T(8,128)S(1)}, f32[16,128,128]{1,0,2:T(8,128)S(1)}, u32[]{:S(2)}, u32[]{:S(2)}) collective-permute-start(f32[16,128,128]{1,0,2:T(8,128)S(1)} %pad_maximum_fusion), channel_id=1, source_target_pairs={{0,32},{32,0},{1,33},{33,1},{2,34},{34,2},{3,35},{35,3},{4,36},{36... | collective-permute-start | bytes 3145736 | tf_op jit(solution)/shard_map/ppermute | solution.py:114
  24.3 7.5 %copy-start = (s32[15,8,16]{2,1,0:T(8,128)S(1)}, s32[15,8,16]{2,1,0:T(8,128)}, u32[]{:S(2)}) copy-start(s32[15,8,16]{2,1,0:T(8,128)} %param.10) | copy-start | bytes 23044
  24.5 7.9 %copy-start.2 = (s32[15,2]{0,1:T(2,128)S(1)}, s32[15,2]{0,1:T(2,128)}, u32[]{:S(2)}) copy-start(s32[15,2]{0,1:T(2,128)} %param.11) | copy-start | bytes 364
  26.0 20.9 %all-to-all-start = ((f32[16,8,16,128]{3,2,0,1:T(8,128)}), f32[16,8,16,128]{3,2,0,1:T(8,128)S(1)}, u32[]{:S(2)}, u32[]{:S(2)}) async-start(f32[16,8,16,128]{3,2,0,1:T(8,128)} %copy.49), calls=%async_computation | async-start | bytes 2097152 | tf_op jit(solution)/shard_map/all_to_all | solution.py:116
  48.8 16.1 %collective-permute-start.3 = (f32[16,16,34]{2,1,0:T(8,128)S(1)}, f32[16,16,34]{2,1,0:T(8,128)S(1)}, u32[]{:S(2)}, u32[]{:S(2)}) collective-permute-start(f32[16,16,34]{2,1,0:T(8,128)S(1)} %get-tuple-element.17), channel_id=1, source_target_pairs={{1,0},{2,1},{3,2},{4,3},{5,4},{6,5},{7,6},{8,7},{9,8},{10,9},{11,1... | collective-permute-start | bytes 104456 | tf_op jit(solution)/shard_map/ppermute | solution.py:69
  54.9 10.1 %collective-permute-start.2 = (f32[8824]{0:T(1024)S(1)}, f32[8824]{0:T(1024)S(1)}, u32[]{:S(2)}, u32[]{:S(2)}) collective-permute-start(f32[8824]{0:T(1024)S(1)} %pad_maximum_fusion.8), channel_id=1, source_target_pairs={{0,1},{1,2},{2,3},{3,4},{4,5},{5,6},{6,7},{7,8},{8,9},{9,10},{10,1... | collective-permute-start | bytes 105896 | tf_op jit(solution)/shard_map/ppermute | solution.py:64

commit v9 on v6

--- a/solution.py
+++ b/solution.py
@@ -53,12 +53,13 @@
     lag_f = peak_lags.astype(jnp.float32)
     pairs_n, lines_n, _ = peak_lags.shape
     rim = channel_data[:, : tap_count - 1, :]
-    sent = jnp.concatenate(
-        [rim.reshape(-1), peak_lags[:, :, 0].astype(channel_data.dtype).reshape(-1)]
-    )
-    got = from_right(sent, "tile")
-    rim_rows = got[: rim.size].reshape(rim.shape)
-    lag_next = got[rim.size :].astype(jnp.float32).reshape(pairs_n, lines_n, 1)
+    first_lags = peak_lags[:, :, 0].astype(channel_data.dtype).reshape(-1)
+    plane = rim.shape[1] * rim.shape[2]
+    first_lags = jnp.pad(first_lags, (0, plane - first_lags.size)).reshape((1,) + rim.shape[1:])
+    got = from_right(jnp.concatenate([rim, first_lags], axis=0), "tile")
+    rim_rows = got[:frames]
+    lag_next = got[frames].reshape(-1)[: pairs_n * lines_n].astype(jnp.float32)
+    lag_next = lag_next.reshape(pairs_n, lines_n, 1)
     main_rows = sample_rows - tap_count + 1
     tail_rows = jnp.concatenate([channel_data[:, main_rows:, :], rim_rows], axis=1)
 
@@ -88,8 +89,10 @@
 
     line_count = per_dev // 2
     pair_count = frame_pairs.shape[0]
-    front = padded[frame_pairs[:, 0]].reshape(pair_count, line_count, 2, -1)
-    later = padded[frame_pairs[:, 1]].reshape(pair_count, line_count, 2, -1)
+    order = jnp.concatenate([frame_pairs[:, 0], frame_pairs[-1:, 1]])
+    chain = padded[order].reshape(pair_count + 1, line_count, 2, -1)
+    front = chain[:-1]
+    later = chain[1:]
     out_len = sample_rows + 4
     prod_len = out_len + WIN - 1
     xr = front[:, :, 0, WIN // 2 : WIN // 2 + prod_len]

time: 79.2 us -> 78.8 us (level)
  the two profiles are of different devices: /device:TPU:32 before, /device:TPU:48 now
where the time goes in v9:
time: 78.8 us; the launch traced here: 78.5 us
  starting transfers between devices  28.1 us (36%)
  waiting for transfers between devices  18.8 us (24%)
  other arithmetic  17 us (22%)
  local copies, waits for them, and re-layouts  8.22 us (10%)
  matrix products  5.03 us (6%)
  between operations  1.36 us (2%)
    ppermute x2, starting transfers between devices, from_right(): return lax.ppermute(block, axis, [(i + 1, i) for i in range(count - 1)])  19.8 us
    all_to_all x1, waiting for transfers between devices, shards(): vol = lax.all_to_all(vol, ('cx', 'cy'), 1, 1, tiled=True).sum(axis=1)  14.1 us
    add x13, other arithmetic, window_sum(): values = values[..., :n] + values[..., width:width + n]  6.35 us
    conv_general_dilated x4, matrix products, beamform(): lax.conv_general_dilated(extended, weights, window_strides=(1,), padding=...  5.03 us
    ppermute x2, waiting for transfers between devices, from_right(): return lax.ppermute(block, axis, [(i + 1, i) for i in range(count - 1)])  4.61 us
    all_to_all x1, starting transfers between devices, shards(): vol = lax.all_to_all(vol, ('cx', 'cy'), 1, 1, tiled=True).sum(axis=1)  4.42 us
    unnamed x32, other arithmetic  4.24 us
    ppermute x1, starting transfers between devices, shards(): vol = vol_mine + lax.ppermute(vol_other, 'cc', [(0, 1), (1, 0)])  1.92 us
  transfers between devices with their start and end apart: 5, of which 3 were waited for; matrix products, arithmetic and copies ran while one was open for 11% of the time, Pallas kernels for 0%

profile of v9, /device:TPU:48, one launch (start us, length us, event | category | flops | bytes accessed | tf_op | source)
XLA Modules:
  0.0 78.5 jit_solution(518693857985460056)
XLA Ops:
  0.6 1.0 %fusion.145 = bf16[15,8]{1,0:T(8,128)(2,1)S(1)} fusion(s32[15,8,16]{2,1,0:T(8,128)} %param.6), kind=kLoop, calls=%fused_computation.327 | loop fusion | flops 120 | bytes 720 | tf_op jit(solution)/shard_map/slice | solution.py:56
  1.8 0.9 %fusion.160 = (bf16[16,15,128]{2,1,0:T(8,128)(2,1)S(1)}, bf16[16,15,128]{2,1,0:T(8,128)(2,1)S(1)}) fusion(bf16[16,128,128]{2,1,0:T(8,128)(2,1)} %param.4), kind=kLoop, calls=%fused_computation.343 | loop fusion | bytes 245760 | tf_op jit(solution)/shard_map/slice | solution.py:64
  2.7 12.5 %collective-permute-start = (bf16[17,15,128]{2,0,1:T(8,128)(2,1)S(1)}, bf16[17,15,128]{2,0,1:T(8,128)(2,1)S(1)}, u32[]{:S(2)}, u32[]{:S(2)}) collective-permute-start(bf16[17,15,128]{2,0,1:T(8,128)(2,1)S(1)} %pad_maximum_fusion.3), channel_id=1, source_target_pairs={{1,0},{2,1},{3,2},{4,3},{5,4},{6,5},{7,6},{8,7},{9,8},{10,9},{11,1... | collective-permute-start | bytes 195848 | tf_op jit(solution)/shard_map/ppermute | solution.py:32
  15.2 1.6 %copy.43 = bf16[1,16,128,256]{2,3,1,0:T(8,128)(2,1)S(1)} copy(bf16[1,16,128,256]{3,2,1,0:T(8,128)(2,1)} %param.5) | data formatting | bytes 2097152 | tf_op args[1]
  16.9 0.2 constant_dynamic-slice_fusion.1
  17.1 2.1 %fusion.149 = f32[16,128,113]{1,0,2:T(8,128)S(1)} fusion(bf16[16,128,128]{1,2,0:T(8,128)(2,1)S(1)} %bitcast.515, bf16[16,128,128]{2,1,0:T(8,128)(2,1)S(1)} %copy-done.1), kind=kOutput, calls=%fused_computation.339 | convolution fusion | flops 947912704 | bytes 1974272 | tf_op jit(solution)/shard_map/conv_general_dilated | solution.py:36
  19.3 0.4 fusion.140
  19.8 1.9 %collective-permute-start.1 = (f32[16,128,128]{1,0,2:T(8,128)S(1)}, f32[16,128,128]{1,0,2:T(8,128)S(1)}, u32[]{:S(2)}, u32[]{:S(2)}) collective-permute-start(f32[16,128,128]{1,0,2:T(8,128)S(1)} %pad_maximum_fusion), channel_id=1, source_target_pairs={{0,32},{32,0},{1,33},{33,1},{2,34},{34,2},{3,35},{35,3},{4,36},{36... | collective-permute-start | bytes 3145736 | tf_op jit(solution)/shard_map/ppermute | solution.py:78
  21.7 2.1 %fusion.151 = f32[16,128,113]{1,0,2:T(8,128)S(1)} fusion(bf16[16,128,128]{1,2,0:T(8,128)(2,1)S(1)} %bitcast.513, bf16[16,128,128]{2,1,0:T(8,128)(2,1)S(1)} %copy-done.1), kind=kOutput, calls=%fused_computation.341 | convolution fusion | flops 947912704 | bytes 1974272 | tf_op jit(solution)/shard_map/conv_general_dilated | solution.py:36
  23.8 0.4 fusion.141
  24.5 0.4 copy.49
  24.9 1.1 %copy.50 = f32[16,8,16,128]{3,2,0,1:T(8,128)} copy(f32[16,8,16,128]{3,2,1,0:T(8,128)S(1)} %bitcast.511) | data formatting | bytes 2097152 | tf_op jit(solution)/shard_map/reshape | solution.py:79
  26.0 4.4 %all-to-all-start = ((f32[16,8,16,128]{3,2,0,1:T(8,128)}), f32[16,8,16,128]{3,2,0,1:T(8,128)S(1)}, u32[]{:S(2)}, u32[]{:S(2)}) async-start(f32[16,8,16,128]{3,2,0,1:T(8,128)} %copy.50), calls=%async_computation | async-start | bytes 2097152 | tf_op jit(solution)/shard_map/all_to_all | solution.py:80
  30.4 0.6 slice.588
  31.2 0.2 copy.57
  31.6 0.7 fusion.146
  32.6 14.1 %all-to-all-done = f32[16,8,16,128]{3,2,0,1:T(8,128)S(1)} async-done(((f32[16,8,16,128]{3,2,0,1:T(8,128)}), f32[16,8,16,128]{3,2,0,1:T(8,128)S(1)}, u32[]{:S(2)}, u32[]{:S(2)}) %all-to-all-start) | async-done | bytes 1048608 | tf_op jit(solution)/shard_map/all_to_all | solution.py:80
  47.1 1.9 %collective-permute-start.2 = (f32[8824]{0:T(1024)S(1)}, f32[8824]{0:T(1024)S(1)}, u32[]{:S(2)}, u32[]{:S(2)}) collective-permute-start(f32[8824]{0:T(1024)S(1)} %pad_maximum_fusion.6), channel_id=1, source_target_pairs={{0,1},{1,2},{2,3},{3,4},{4,5},{5,6},{6,7},{7,8},{8,9},{9,10},{10,1... | collective-permute-start | bytes 105896 | tf_op jit(solution)/shard_map/ppermute | solution.py:27
  49.0 7.3 %collective-permute-start.3 = (f32[16,16,34]{2,1,0:T(8,128)S(1)}, f32[16,16,34]{2,1,0:T(8,128)S(1)}, u32[]{:S(2)}, u32[]{:S(2)}) collective-permute-start(f32[16,16,34]{2,1,0:T(8,128)S(1)} %get-tuple-element.20), channel_id=1, source_target_pairs={{1,0},{2,1},{3,2},{4,3},{5,4},{6,5},{7,6},{8,7},{9,8},{10,9},{11,1... | collective-permute-start | bytes 104456 | tf_op jit(solution)/shard_map/ppermute | solution.py:32
  56.6 4.6 %collective-permute-done.3 = f32[16,16,34]{2,1,0:T(8,128)S(1)} collective-permute-done((f32[16,16,34]{2,1,0:T(8,128)S(1)}, f32[16,16,34]{2,1,0:T(8,128)S(1)}, u32[]{:S(2)}, u32[]{:S(2)}) %collective-permute-start.3) | collective-permute-done | bytes 34848 | tf_op jit(solution)/shard_map/ppermute | solution.py:32
  61.3 0.6 gather_fusion
  62.1 0.2 fusion.163
  63.1 0.6 fusion.162
  68.4 1.1 %slice_add_fusion.4 = f32[33,15,8,162]{3,2,1,0:T(8,128)S(1)} fusion(f32[33,15,8,163]{3,2,1,0:T(8,128)S(1)} %fusion.42), kind=kLoop, calls=%fused_computation.5 | loop fusion | flops 641520 | bytes 7698240 | tf_op jit(solution)/shard_map/add | solution.py:20
  69.5 1.1 %slice_add_fusion.3 = f32[33,15,8,160]{3,2,1,0:T(8,128)S(1)} fusion(f32[33,15,8,162]{3,2,1,0:T(8,128)S(1)} %slice_add_fusion.4), kind=kLoop, calls=%fused_computation.4 | loop fusion | flops 633600 | bytes 7603200 | tf_op jit(solution)/shard_map/add | solution.py:20
  70.6 1.1 %slice_add_fusion.2 = f32[33,15,8,156]{3,2,1,0:T(8,128)S(1)} fusion(f32[33,15,8,160]{3,2,1,0:T(8,128)S(1)} %slice_add_fusion.3), kind=kLoop, calls=%fused_computation.3 | loop fusion | flops 617760 | bytes 7413120 | tf_op jit(solution)/shard_map/add | solution.py:20
  71.7 1.1 %slice_add_fusion.1 = f32[33,15,8,148]{3,2,1,0:T(8,128)S(1)} fusion(f32[33,15,8,156]{3,2,1,0:T(8,128)S(1)} %slice_add_fusion.2), kind=kLoop, calls=%fused_computation.2 | loop fusion | flops 586080 | bytes 7032960 | tf_op jit(solution)/shard_map/add | solution.py:20
  72.9 1.1 %slice_add_fusion = f32[33,15,8,132]{3,2,1,0:T(8,128)S(1)} fusion(f32[33,15,8,148]{3,2,1,0:T(8,128)S(1)} %slice_add_fusion.1), kind=kLoop, calls=%fused_computation.1 | loop fusion | flops 522720 | bytes 6272640 | tf_op jit(solution)/shard_map/add | solution.py:20
  74.5 1.5 %add_select_fusion = (f32[15,8,132]{2,1,0:T(8,128)S(1)}, f32[15,8,132]{2,1,0:T(8,128)S(1)}, f32[15,8,132]{2,1,0:T(8,128)S(1)}, f32[15,8,132]{2,1,0:T(8,128)S(1)}...) fusion(f32[15,8,2]{2,1,0:T(8,128)S(1)} %reshape.139, ...), kind=kLoop, calls=%fused_computation.298 | loop fusion | flops 3453120 | bytes 4878852 | tf_op jit(solution)/shard_map/jit(_where)/select_n | solution.py:134
  76.0 0.9 %maximum_maximum_fusion = f32[15,8,132]{2,1,0:T(8,128)S(1)} fusion(f32[15,8,132]{2,1,0:T(8,128)S(1)} %get-tuple-element.9, f32[15,8,164]{2,1,0:T(8,128)S(1)} %fusion.35, f32[33,15,8,132]{3,2,1,0:T(8,128)S(1)} %slice_add_fusion), kind=kLoop, calls=%fused_computation.299 | loop fusion | flops 1267200 | bytes 3548160 | tf_op jit(solution)/shard_map/max | solution.py:124
  76.9 0.7 fusion.142
  77.7 0.8 %slice_maximum_fusion = f32[15,8,128]{2,1,0:T(8,128)} fusion(f32[15,8,132]{2,1,0:T(8,128)S(1)} %get-tuple-element.8, f32[15,8,132]{2,1,0:T(8,128)S(1)} %get-tuple-element.7, f32[15,8,132]{2,1,0:T(8,128)S(1)} %get-tuple-element.6, f32[15,8,132]{2,1,0:T(8,128)S(1)} %get-tuple-element.5, f32[15,8,132]{2,1,0:T(8,128)S(1)} %get-tuple-element.4, ...), kind=kLoop, calls=%fused_computation.318 | loop fusion | flops 92160 | bytes 491520 | tf_op jit(solution)/shard_map/max | solution.py:124
  (91 shorter events, 7.7 us)
Async XLA Ops:
  0.6 16.5 %copy-start.1 = (bf16[16,128,128]{2,1,0:T(8,128)(2,1)S(1)}, bf16[16,128,128]{2,1,0:T(8,128)(2,1)}, u32[]{:S(2)}) copy-start(bf16[16,128,128]{2,1,0:T(8,128)(2,1)} %param.4) | copy-start | bytes 1572868
  2.7 16.5 %collective-permute-start = (bf16[17,15,128]{2,0,1:T(8,128)(2,1)S(1)}, bf16[17,15,128]{2,0,1:T(8,128)(2,1)S(1)}, u32[]{:S(2)}, u32[]{:S(2)}) collective-permute-start(bf16[17,15,128]{2,0,1:T(8,128)(2,1)S(1)} %pad_maximum_fusion.3), channel_id=1, source_target_pairs={{1,0},{2,1},{3,2},{4,3},{5,4},{6,5},{7,6},{8,7},{9,8},{10,9},{11,1... | collective-permute-start | bytes 195848 | tf_op jit(solution)/shard_map/ppermute | solution.py:32
  19.8 4.6 %collective-permute-start.1 = (f32[16,128,128]{1,0,2:T(8,128)S(1)}, f32[16,128,128]{1,0,2:T(8,128)S(1)}, u32[]{:S(2)}, u32[]{:S(2)}) collective-permute-start(f32[16,128,128]{1,0,2:T(8,128)S(1)} %pad_maximum_fusion), channel_id=1, source_target_pairs={{0,32},{32,0},{1,33},{33,1},{2,34},{34,2},{3,35},{35,3},{4,36},{36... | collective-permute-start | bytes 3145736 | tf_op jit(solution)/shard_map/ppermute | solution.py:78
  24.2 6.2 %copy-start = (s32[15,8,16]{2,1,0:T(8,128)S(1)}, s32[15,8,16]{2,1,0:T(8,128)}, u32[]{:S(2)}) copy-start(s32[15,8,16]{2,1,0:T(8,128)} %param.6) | copy-start | bytes 23044
  24.2 6.2 %copy-start.2 = (s32[15,2]{0,1:T(2,128)S(1)}, s32[15,2]{0,1:T(2,128)}, u32[]{:S(2)}) copy-start(s32[15,2]{0,1:T(2,128)} %param.7) | copy-start | bytes 364
  24.5 7.2 %slice-start = ((s32[15,2]{0,1:T(2,128)}), s32[15,1]{0,1:T(1,128)S(1)}, s32[]{:S(2)}) async-start(s32[15,2]{0,1:T(2,128)} %param.7), calls=%async_computation.1 | async-start | bytes 1024 | tf_op jit(solution)/shard_map/slice | solution.py:92
  26.0 20.8 %all-to-all-start = ((f32[16,8,16,128]{3,2,0,1:T(8,128)}), f32[16,8,16,128]{3,2,0,1:T(8,128)S(1)}, u32[]{:S(2)}, u32[]{:S(2)}) async-start(f32[16,8,16,128]{3,2,0,1:T(8,128)} %copy.50), calls=%async_computation | async-start | bytes 2097152 | tf_op jit(solution)/shard_map/all_to_all | solution.py:80
  47.1 9.3 %collective-permute-start.2 = (f32[8824]{0:T(1024)S(1)}, f32[8824]{0:T(1024)S(1)}, u32[]{:S(2)}, u32[]{:S(2)}) collective-permute-start(f32[8824]{0:T(1024)S(1)} %pad_maximum_fusion.6), channel_id=1, source_target_pairs={{0,1},{1,2},{2,3},{3,4},{4,5},{5,6},{6,7},{7,8},{8,9},{9,10},{10,1... | collective-permute-start | bytes 105896 | tf_op jit(solution)/shard_map/ppermute | solution.py:27
  49.0 12.2 %collective-permute-start.3 = (f32[16,16,34]{2,1,0:T(8,128)S(1)}, f32[16,16,34]{2,1,0:T(8,128)S(1)}, u32[]{:S(2)}, u32[]{:S(2)}) collective-permute-start(f32[16,16,34]{2,1,0:T(8,128)S(1)} %get-tuple-element.20), channel_id=1, source_target_pairs={{1,0},{2,1},{3,2},{4,3},{5,4},{6,5},{7,6},{8,7},{9,8},{10,9},{11,1... | collective-permute-start | bytes 104456 | tf_op jit(solution)/shard_map/ppermute | solution.py:32

commit v10 on v9

--- a/solution.py
+++ b/solution.py
@@ -53,13 +53,7 @@
     lag_f = peak_lags.astype(jnp.float32)
     pairs_n, lines_n, _ = peak_lags.shape
     rim = channel_data[:, : tap_count - 1, :]
-    first_lags = peak_lags[:, :, 0].astype(channel_data.dtype).reshape(-1)
-    plane = rim.shape[1] * rim.shape[2]
-    first_lags = jnp.pad(first_lags, (0, plane - first_lags.size)).reshape((1,) + rim.shape[1:])
-    got = from_right(jnp.concatenate([rim, first_lags], axis=0), "tile")
-    rim_rows = got[:frames]
-    lag_next = got[frames].reshape(-1)[: pairs_n * lines_n].astype(jnp.float32)
-    lag_next = lag_next.reshape(pairs_n, lines_n, 1)
+    rim_rows = from_right(rim, "tile")
     main_rows = sample_rows - tap_count + 1
     tail_rows = jnp.concatenate([channel_data[:, main_rows:, :], rim_rows], axis=1)
 
@@ -85,7 +79,11 @@
     got = from_left(sent, "tile")
     left = got[: tail.size].reshape(tail.shape)
     lag_prev = got[tail.size :].reshape(pairs_n, lines_n, 1)
-    padded = jnp.concatenate([left, vol, from_right(head, "tile")], axis=2)
+    sent = jnp.concatenate([head.reshape(-1), lag_f[:, :, 0].reshape(-1)])
+    got = from_right(sent, "tile")
+    right = got[: head.size].reshape(head.shape)
+    lag_next = got[head.size :].reshape(pairs_n, lines_n, 1)
+    padded = jnp.concatenate([left, vol, right], axis=2)
 
     line_count = per_dev // 2
     pair_count = frame_pairs.shape[0]

time: 78.8 us -> 79.8 us (1.013)
  the two profiles are of different devices: /device:TPU:48 before, /device:TPU:40 now
where the time goes in v10:
time: 79.8 us; the launch traced here: 79.5 us
  starting transfers between devices  27.9 us (35%)
  waiting for transfers between devices  20.9 us (26%)
  other arithmetic  16 us (20%)
  local copies, waits for them, and re-layouts  8.27 us (10%)
  matrix products  5.04 us (6%)
  between operations  1.33 us (2%)
    ppermute x2, starting transfers between devices, from_right(): return lax.ppermute(block, axis, [(i + 1, i) for i in range(count - 1)])  18.1 us
    all_to_all x1, waiting for transfers between devices, shards(): vol = lax.all_to_all(vol, ('cx', 'cy'), 1, 1, tiled=True).sum(axis=1)  13.3 us
    ppermute x1, waiting for transfers between devices, from_left(): return lax.ppermute(block, axis, [(i, i + 1) for i in range(count - 1)])  7.58 us
    add x13, other arithmetic, window_sum(): values = values[..., :n] + values[..., width:width + n]  6.36 us
    all_to_all x1, starting transfers between devices, shards(): vol = lax.all_to_all(vol, ('cx', 'cy'), 1, 1, tiled=True).sum(axis=1)  5.75 us
    conv_general_dilated x4, matrix products, beamform(): lax.conv_general_dilated(extended, weights, window_strides=(1,), padding=...  5.04 us
    unnamed x32, other arithmetic  4.24 us
    ppermute x1, starting transfers between devices, from_left(): return lax.ppermute(block, axis, [(i, i + 1) for i in range(count - 1)])  2.1 us
  transfers between devices with their start and end apart: 5, of which 3 were waited for; matrix products, arithmetic and copies ran while one was open for 11% of the time, Pallas kernels for 0%

profile of v10, /device:TPU:40, one launch (start us, length us, event | category | flops | bytes accessed | tf_op | source)
XLA Modules:
  0.0 79.5 jit_solution(5746343994429269165)
XLA Ops:
  0.6 1.0 %fusion.159 = (bf16[16,15,128]{2,1,0:T(8,128)(2,1)S(1)}, bf16[16,15,128]{2,1,0:T(8,128)(2,1)S(1)}) fusion(bf16[16,128,128]{2,1,0:T(8,128)(2,1)} %param.4), kind=kLoop, calls=%fused_computation.339 | loop fusion | bytes 245760 | tf_op jit(solution)/shard_map/slice | solution.py:58
  1.6 11.6 %collective-permute-start = (bf16[16,15,128]{2,0,1:T(8,128)(2,1)S(1)}, bf16[16,15,128]{2,0,1:T(8,128)(2,1)S(1)}, u32[]{:S(2)}, u32[]{:S(2)}) collective-permute-start(bf16[16,15,128]{2,0,1:T(8,128)(2,1)S(1)} %copy.152), channel_id=1, source_target_pairs={{1,0},{2,1},{3,2},{4,3},{5,4},{6,5},{7,6},{8,7},{9,8},{10,9},{11,1... | collective-permute-start | bytes 184328 | tf_op jit(solution)/shard_map/ppermute | solution.py:32
  13.3 1.6 %copy.23 = bf16[1,16,128,256]{2,3,1,0:T(8,128)(2,1)S(1)} copy(bf16[1,16,128,256]{3,2,1,0:T(8,128)(2,1)} %param.5) | data formatting | bytes 2097152 | tf_op args[1]
  14.9 0.2 constant_dynamic-slice_fusion.1
  15.1 2.1 %fusion.148 = f32[16,128,113]{1,0,2:T(8,128)S(1)} fusion(bf16[16,128,128]{1,2,0:T(8,128)(2,1)S(1)} %bitcast.511, bf16[16,128,128]{2,1,0:T(8,128)(2,1)S(1)} %copy-done.1), kind=kOutput, calls=%fused_computation.335 | convolution fusion | flops 947912704 | bytes 1974272 | tf_op jit(solution)/shard_map/conv_general_dilated | solution.py:36
  17.3 0.4 fusion.140
  17.8 1.9 %collective-permute-start.1 = (f32[16,128,128]{1,0,2:T(8,128)S(1)}, f32[16,128,128]{1,0,2:T(8,128)S(1)}, u32[]{:S(2)}, u32[]{:S(2)}) collective-permute-start(f32[16,128,128]{1,0,2:T(8,128)S(1)} %pad_maximum_fusion), channel_id=1, source_target_pairs={{0,32},{32,0},{1,33},{33,1},{2,34},{34,2},{3,35},{35,3},{4,36},{36... | collective-permute-start | bytes 3145736 | tf_op jit(solution)/shard_map/ppermute | solution.py:72
  19.7 2.1 %fusion.150 = f32[16,128,113]{1,0,2:T(8,128)S(1)} fusion(bf16[16,128,128]{1,2,0:T(8,128)(2,1)S(1)} %bitcast.509, bf16[16,128,128]{2,1,0:T(8,128)(2,1)S(1)} %copy-done.1), kind=kOutput, calls=%fused_computation.337 | convolution fusion | flops 947912704 | bytes 1974272 | tf_op jit(solution)/shard_map/conv_general_dilated | solution.py:36
  21.8 0.4 fusion.141
  22.5 0.4 copy.28
  22.9 1.1 %copy.29 = f32[16,8,16,128]{3,2,0,1:T(8,128)} copy(f32[16,8,16,128]{3,2,1,0:T(8,128)S(1)} %bitcast.507) | data formatting | bytes 2097152 | tf_op jit(solution)/shard_map/reshape | solution.py:73
  24.0 5.8 %all-to-all-start = ((f32[16,8,16,128]{3,2,0,1:T(8,128)}), f32[16,8,16,128]{3,2,0,1:T(8,128)S(1)}, u32[]{:S(2)}, u32[]{:S(2)}) async-start(f32[16,8,16,128]{3,2,0,1:T(8,128)} %copy.29), calls=%async_computation | async-start | bytes 2097152 | tf_op jit(solution)/shard_map/all_to_all | solution.py:74
  29.7 0.6 slice.589
  30.8 0.7 fusion.145
  31.6 13.3 %all-to-all-done = f32[16,8,16,128]{3,2,0,1:T(8,128)S(1)} async-done(((f32[16,8,16,128]{3,2,0,1:T(8,128)}), f32[16,8,16,128]{3,2,0,1:T(8,128)S(1)}, u32[]{:S(2)}, u32[]{:S(2)}) %all-to-all-start) | async-done | bytes 1048608 | tf_op jit(solution)/shard_map/all_to_all | solution.py:74
  45.2 6.5 %collective-permute-start.3 = (f32[8824]{0:T(1024)S(1)}, f32[8824]{0:T(1024)S(1)}, u32[]{:S(2)}, u32[]{:S(2)}) collective-permute-start(f32[8824]{0:T(1024)S(1)} %pad_maximum_fusion.6), channel_id=1, source_target_pairs={{1,0},{2,1},{3,2},{4,3},{5,4},{6,5},{7,6},{8,7},{9,8},{10,9},{11,1... | collective-permute-start | bytes 105896 | tf_op jit(solution)/shard_map/ppermute | solution.py:32
  51.9 2.1 %collective-permute-start.2 = (f32[8824]{0:T(1024)S(1)}, f32[8824]{0:T(1024)S(1)}, u32[]{:S(2)}, u32[]{:S(2)}) collective-permute-start(f32[8824]{0:T(1024)S(1)} %pad_maximum_fusion.5), channel_id=1, source_target_pairs={{0,1},{1,2},{2,3},{3,4},{4,5},{5,6},{6,7},{7,8},{8,9},{9,10},{10,1... | collective-permute-start | bytes 105896 | tf_op jit(solution)/shard_map/ppermute | solution.py:27
  54.0 0.2 copy.34
  54.4 7.6 %collective-permute-done.2 = f32[8824]{0:T(1024)S(1)} collective-permute-done((f32[8824]{0:T(1024)S(1)}, f32[8824]{0:T(1024)S(1)}, u32[]{:S(2)}, u32[]{:S(2)}) %collective-permute-start.2) | collective-permute-done | bytes 35328 | tf_op jit(solution)/shard_map/ppermute | solution.py:27
  62.1 0.2 pad_maximum_fusion.1
  62.3 0.6 gather_fusion
  63.0 0.2 fusion.162
  64.2 0.6 fusion.161
  69.4 1.1 %slice_add_fusion.4 = f32[33,15,8,162]{3,2,1,0:T(8,128)S(1)} fusion(f32[33,15,8,163]{3,2,1,0:T(8,128)S(1)} %fusion.42), kind=kLoop, calls=%fused_computation.5 | loop fusion | flops 641520 | bytes 7698240 | tf_op jit(solution)/shard_map/add | solution.py:20
  70.5 1.1 %slice_add_fusion.3 = f32[33,15,8,160]{3,2,1,0:T(8,128)S(1)} fusion(f32[33,15,8,162]{3,2,1,0:T(8,128)S(1)} %slice_add_fusion.4), kind=kLoop, calls=%fused_computation.4 | loop fusion | flops 633600 | bytes 7603200 | tf_op jit(solution)/shard_map/add | solution.py:20
  71.6 1.1 %slice_add_fusion.2 = f32[33,15,8,156]{3,2,1,0:T(8,128)S(1)} fusion(f32[33,15,8,160]{3,2,1,0:T(8,128)S(1)} %slice_add_fusion.3), kind=kLoop, calls=%fused_computation.3 | loop fusion | flops 617760 | bytes 7413120 | tf_op jit(solution)/shard_map/add | solution.py:20
  72.7 1.1 %slice_add_fusion.1 = f32[33,15,8,148]{3,2,1,0:T(8,128)S(1)} fusion(f32[33,15,8,156]{3,2,1,0:T(8,128)S(1)} %slice_add_fusion.2), kind=kLoop, calls=%fused_computation.2 | loop fusion | flops 586080 | bytes 7032960 | tf_op jit(solution)/shard_map/add | solution.py:20
  73.9 1.1 %slice_add_fusion = f32[33,15,8,132]{3,2,1,0:T(8,128)S(1)} fusion(f32[33,15,8,148]{3,2,1,0:T(8,128)S(1)} %slice_add_fusion.1), kind=kLoop, calls=%fused_computation.1 | loop fusion | flops 522720 | bytes 6272640 | tf_op jit(solution)/shard_map/add | solution.py:20
  75.6 1.5 %add_select_fusion = (f32[15,8,132]{2,1,0:T(8,128)S(1)}, f32[15,8,132]{2,1,0:T(8,128)S(1)}, f32[15,8,132]{2,1,0:T(8,128)S(1)}, f32[15,8,132]{2,1,0:T(8,128)S(1)}...) fusion(f32[15,8,2]{2,1,0:T(8,128)S(1)} %reshape.143, ...), kind=kLoop, calls=%fused_computation.298 | loop fusion | flops 3453120 | bytes 4878852 | tf_op jit(solution)/shard_map/jit(_where)/select_n | solution.py:132
  77.0 0.9 %maximum_maximum_fusion = f32[15,8,132]{2,1,0:T(8,128)S(1)} fusion(f32[15,8,132]{2,1,0:T(8,128)S(1)} %get-tuple-element.11, f32[15,8,164]{2,1,0:T(8,128)S(1)} %fusion.35, f32[33,15,8,132]{3,2,1,0:T(8,128)S(1)} %slice_add_fusion), kind=kLoop, calls=%fused_computation.299 | loop fusion | flops 1267200 | bytes 3548160 | tf_op jit(solution)/shard_map/max | solution.py:122
  77.9 0.7 fusion.142
  78.7 0.8 %slice_maximum_fusion = f32[15,8,128]{2,1,0:T(8,128)} fusion(f32[15,8,132]{2,1,0:T(8,128)S(1)} %get-tuple-element.10, f32[15,8,132]{2,1,0:T(8,128)S(1)} %get-tuple-element.9, f32[15,8,132]{2,1,0:T(8,128)S(1)} %get-tuple-element.8, f32[15,8,132]{2,1,0:T(8,128)S(1)} %get-tuple-element.7, f32[15,8,132]{2,1,0:T(8,128)S(1)} %get-tuple-element.6, ...), kind=kLoop, calls=%fused_computation.317 | loop fusion | flops 92160 | bytes 491520 | tf_op jit(solution)/shard_map/max | solution.py:122
  (85 shorter events, 7.6 us)
Async XLA Ops:
  0.6 14.5 %copy-start.1 = (bf16[16,128,128]{2,1,0:T(8,128)(2,1)S(1)}, bf16[16,128,128]{2,1,0:T(8,128)(2,1)}, u32[]{:S(2)}) copy-start(bf16[16,128,128]{2,1,0:T(8,128)(2,1)} %param.4) | copy-start | bytes 1572868
  1.6 15.6 %collective-permute-start = (bf16[16,15,128]{2,0,1:T(8,128)(2,1)S(1)}, bf16[16,15,128]{2,0,1:T(8,128)(2,1)S(1)}, u32[]{:S(2)}, u32[]{:S(2)}) collective-permute-start(bf16[16,15,128]{2,0,1:T(8,128)(2,1)S(1)} %copy.152), channel_id=1, source_target_pairs={{1,0},{2,1},{3,2},{4,3},{5,4},{6,5},{7,6},{8,7},{9,8},{10,9},{11,1... | collective-permute-start | bytes 184328 | tf_op jit(solution)/shard_map/ppermute | solution.py:32
  17.8 4.6 %collective-permute-start.1 = (f32[16,128,128]{1,0,2:T(8,128)S(1)}, f32[16,128,128]{1,0,2:T(8,128)S(1)}, u32[]{:S(2)}, u32[]{:S(2)}) collective-permute-start(f32[16,128,128]{1,0,2:T(8,128)S(1)} %pad_maximum_fusion), channel_id=1, source_target_pairs={{0,32},{32,0},{1,33},{33,1},{2,34},{34,2},{3,35},{35,3},{4,36},{36... | collective-permute-start | bytes 3145736 | tf_op jit(solution)/shard_map/ppermute | solution.py:72
  22.2 7.5 %copy-start.2 = (s32[15,2]{0,1:T(2,128)S(1)}, s32[15,2]{0,1:T(2,128)}, u32[]{:S(2)}) copy-start(s32[15,2]{0,1:T(2,128)} %param.7) | copy-start | bytes 364
  22.2 8.1 %copy-start = (s32[15,8,16]{2,1,0:T(8,128)S(1)}, s32[15,8,16]{2,1,0:T(8,128)}, u32[]{:S(2)}) copy-start(s32[15,8,16]{2,1,0:T(8,128)} %param.6) | copy-start | bytes 23044
  22.5 8.3 %slice-start = ((s32[15,2]{0,1:T(2,128)}), s32[15,1]{0,1:T(1,128)S(1)}, s32[]{:S(2)}) async-start(s32[15,2]{0,1:T(2,128)} %param.7), calls=%async_computation.1 | async-start | bytes 1024 | tf_op jit(solution)/shard_map/slice | solution.py:90
  24.0 20.9 %all-to-all-start = ((f32[16,8,16,128]{3,2,0,1:T(8,128)}), f32[16,8,16,128]{3,2,0,1:T(8,128)S(1)}, u32[]{:S(2)}, u32[]{:S(2)}) async-start(f32[16,8,16,128]{3,2,0,1:T(8,128)} %copy.29), calls=%async_computation | async-start | bytes 2097152 | tf_op jit(solution)/shard_map/all_to_all | solution.py:74
  45.2 9.0 %collective-permute-start.3 = (f32[8824]{0:T(1024)S(1)}, f32[8824]{0:T(1024)S(1)}, u32[]{:S(2)}, u32[]{:S(2)}) collective-permute-start(f32[8824]{0:T(1024)S(1)} %pad_maximum_fusion.6), channel_id=1, source_target_pairs={{1,0},{2,1},{3,2},{4,3},{5,4},{6,5},{7,6},{8,7},{9,8},{10,9},{11,1... | collective-permute-start | bytes 105896 | tf_op jit(solution)/shard_map/ppermute | solution.py:32
  51.9 10.1 %collective-permute-start.2 = (f32[8824]{0:T(1024)S(1)}, f32[8824]{0:T(1024)S(1)}, u32[]{:S(2)}, u32[]{:S(2)}) collective-permute-start(f32[8824]{0:T(1024)S(1)} %pad_maximum_fusion.5), channel_id=1, source_target_pairs={{0,1},{1,2},{2,3},{3,4},{4,5},{5,6},{6,7},{7,8},{8,9},{9,10},{10,1... | collective-permute-start | bytes 105896 | tf_op jit(solution)/shard_map/ppermute | solution.py:27

commit v11 on v9

--- a/solution.py
+++ b/solution.py
@@ -103,7 +103,9 @@
     prods = jnp.stack(
         [xr * yr[..., j : j + prod_len] + xi * yi[..., j : j + prod_len] for j in range(nlag)]
     )
-    cross_sum = window_sum(prods)
+    flat = prods.reshape(nlag, pair_count, line_count * prod_len)
+    flat = jnp.pad(window_sum(flat), ((0, 0), (0, 0), (0, WIN - 1)))
+    cross_sum = flat.reshape(nlag, pair_count, line_count, prod_len)[..., :out_len]
     power_a = window_sum(xr * xr + xi * xi) / (2 * WIN)
     ey = yr * yr + yi * yi
     power_full = window_sum(ey[..., : out_len + nlag - 1 + WIN - 1]) / (2 * WIN)

time: 78.8 us -> 153 us (1.94)
  local copies, waits for them, and re-layouts: 8.22 us -> 79.8 us
  other arithmetic: 17 us -> 20 us
  waiting for transfers between devices: 18.8 us -> 17 us
    another operation x0 -> x34, local copies, waits for them, and re-layouts: none -> 49.6 us  [shards(): jnp.stack([xr * yr[..., j:j + prod_len] + xi * yi[..., j:j + prod_len] fo...]
    unnamed x10 -> x78, local copies, waits for them, and re-layouts: 1.77 us -> 17.4 us
    add x1 -> x5, other arithmetic: 0.02 us -> 6 us  [shards(): xr * yr[..., j:j + prod_len] + xi * yi[..., j:j + prod_len]]
    reshape x0 -> x1, local copies, waits for them, and re-layouts: none -> 4.33 us  [shards(): flat.reshape(nlag, pair_count, line_count, prod_len)[..., :out_len]]
    unnamed x32 -> x0, other arithmetic: 4.24 us -> none
    select_n x1, other arithmetic: 1.47 us -> 3.75 us  [shards(): dz = jnp.where(outside, 0.0, displacement)]
  transfers between devices with their start and end apart: 5 -> 5, of which waited for: 3 -> 3; matrix products, arithmetic and copies ran while one was open for 11% -> 7% of each run, Pallas kernels for 0% -> 0%
where the time goes in v11:
time: 153 us; the launch traced here: 151 us
  local copies, waits for them, and re-layouts  79.8 us (52%)
  starting transfers between devices  28.1 us (18%)
  other arithmetic  20 us (13%)
  waiting for transfers between devices  17 us (11%)
  matrix products  5.03 us (3%)
  between operations  1.55 us (1%)
    another operation x34, local copies, waits for them, and re-layouts, shards(): jnp.stack([xr * yr[..., j:j + prod_len] + xi * yi[..., j:j + prod_len] fo...  49.6 us
    ppermute x2, starting transfers between devices, from_right(): return lax.ppermute(block, axis, [(i + 1, i) for i in range(count - 1)])  19.8 us
    unnamed x78, local copies, waits for them, and re-layouts  17.4 us
    all_to_all x1, waiting for transfers between devices, shards(): vol = lax.all_to_all(vol, ('cx', 'cy'), 1, 1, tiled=True).sum(axis=1)  12.9 us
    add x5, other arithmetic, shards(): xr * yr[..., j:j + prod_len] + xi * yi[..., j:j + prod_len]  6 us
    conv_general_dilated x4, matrix products, beamform(): lax.conv_general_dilated(extended, weights, window_strides=(1,), padding=...  5.03 us
    add x13, other arithmetic, window_sum(): values = values[..., :n] + values[..., width:width + n]  4.86 us
    all_to_all x1, starting transfers between devices, shards(): vol = lax.all_to_all(vol, ('cx', 'cy'), 1, 1, tiled=True).sum(axis=1)  4.41 us
  transfers between devices with their start and end apart: 5, of which 3 were waited for; matrix products, arithmetic and copies ran while one was open for 7% of the time, Pallas kernels for 0%

profile of v11, /device:TPU:48, one launch (start us, length us, event | category | flops | bytes accessed | tf_op | source)
XLA Modules:
  0.0 151.5 jit_solution(7449092950010592264)
XLA Ops:
  2.7 12.5 %collective-permute-start = (bf16[17,15,128]{2,0,1:T(8,128)(2,1)S(1)}, bf16[17,15,128]{2,0,1:T(8,128)(2,1)S(1)}, u32[]{:S(2)}, u32[]{:S(2)}) collective-permute-start(bf16[17,15,128]{2,0,1:T(8,128)(2,1)S(1)} %pad_maximum_fusion.3), channel_id=1, source_target_pairs={{1,0},{2,1},{3,2},{4,3},{5,4},{6,5},{7,6},{8,7},{9,8},{10,9},{11,1... | collective-permute-start | bytes 195848 | tf_op jit(solution)/shard_map/ppermute | solution.py:32
  17.1 2.1 %fusion.83 = f32[16,128,113]{1,0,2:T(8,128)S(1)} fusion(bf16[16,128,128]{1,2,0:T(8,128)(2,1)S(1)} %bitcast.383, bf16[16,128,128]{2,1,0:T(8,128)(2,1)S(1)} %copy-done.18), kind=kOutput, calls=%fused_computation.306 | convolution fusion | flops 947912704 | bytes 1974272 | tf_op jit(solution)/shard_map/conv_general_dilated | solution.py:36
  19.8 1.9 %collective-permute-start.1 = (f32[16,128,128]{1,0,2:T(8,128)S(1)}, f32[16,128,128]{1,0,2:T(8,128)S(1)}, u32[]{:S(2)}, u32[]{:S(2)}) collective-permute-start(f32[16,128,128]{1,0,2:T(8,128)S(1)} %pad_maximum_fusion), channel_id=1, source_target_pairs={{0,32},{32,0},{1,33},{33,1},{2,34},{34,2},{3,35},{35,3},{4,36},{36... | collective-permute-start | bytes 3145736 | tf_op jit(solution)/shard_map/ppermute | solution.py:78
  21.7 2.1 %fusion.85 = f32[16,128,113]{1,0,2:T(8,128)S(1)} fusion(bf16[16,128,128]{1,2,0:T(8,128)(2,1)S(1)} %bitcast.381, bf16[16,128,128]{2,1,0:T(8,128)(2,1)S(1)} %copy-done.18), kind=kOutput, calls=%fused_computation.308 | convolution fusion | flops 947912704 | bytes 1974272 | tf_op jit(solution)/shard_map/conv_general_dilated | solution.py:36
  26.0 4.4 %all-to-all-start = ((f32[16,8,16,128]{3,2,0,1:T(8,128)}), f32[16,8,16,128]{3,2,0,1:T(8,128)S(1)}, u32[]{:S(2)}, u32[]{:S(2)}) async-start(f32[16,8,16,128]{3,2,0,1:T(8,128)} %copy.50), calls=%async_computation | async-start | bytes 2097152 | tf_op jit(solution)/shard_map/all_to_all | solution.py:80
  33.9 12.9 %all-to-all-done = f32[16,8,16,128]{3,2,0,1:T(8,128)S(1)} async-done(((f32[16,8,16,128]{3,2,0,1:T(8,128)}), f32[16,8,16,128]{3,2,0,1:T(8,128)S(1)}, u32[]{:S(2)}, u32[]{:S(2)}) %all-to-all-start) | async-done | bytes 1048608 | tf_op jit(solution)/shard_map/all_to_all | solution.py:80
  47.1 1.9 %collective-permute-start.2 = (f32[8824]{0:T(1024)S(1)}, f32[8824]{0:T(1024)S(1)}, u32[]{:S(2)}, u32[]{:S(2)}) collective-permute-start(f32[8824]{0:T(1024)S(1)} %pad_maximum_fusion.6), channel_id=1, source_target_pairs={{0,1},{1,2},{2,3},{3,4},{4,5},{5,6},{6,7},{7,8},{8,9},{9,10},{10,1... | collective-permute-start | bytes 105896 | tf_op jit(solution)/shard_map/ppermute | solution.py:27
  49.0 7.3 %collective-permute-start.3 = (f32[16,16,34]{2,1,0:T(8,128)S(1)}, f32[16,16,34]{2,1,0:T(8,128)S(1)}, u32[]{:S(2)}, u32[]{:S(2)}) collective-permute-start(f32[16,16,34]{2,1,0:T(8,128)S(1)} %get-tuple-element.53), channel_id=1, source_target_pairs={{1,0},{2,1},{3,2},{4,3},{5,4},{6,5},{7,6},{8,7},{9,8},{10,9},{11,1... | collective-permute-start | bytes 104456 | tf_op jit(solution)/shard_map/ppermute | solution.py:32
  57.2 4.0 %collective-permute-done.3 = f32[16,16,34]{2,1,0:T(8,128)S(1)} collective-permute-done((f32[16,16,34]{2,1,0:T(8,128)S(1)}, f32[16,16,34]{2,1,0:T(8,128)S(1)}, u32[]{:S(2)}, u32[]{:S(2)}) %collective-permute-start.3) | collective-permute-done | bytes 34848 | tf_op jit(solution)/shard_map/ppermute | solution.py:32
  70.5 1.6 %stack.103 = f32[1,15,1304]{2,1,0:T(8,128)} reshape(f32[15,8,163]{2,1,0:T(8,128)} %get-tuple-element.45) | data formatting | bytes 156480 | tf_op jit(solution)/shard_map/stack | solution.py:103
  72.1 1.6 %stack.104 = f32[1,15,1304]{2,1,0:T(8,128)} reshape(f32[15,8,163]{2,1,0:T(8,128)} %get-tuple-element.44) | data formatting | bytes 156480 | tf_op jit(solution)/shard_map/stack | solution.py:103
  73.8 1.7 %stack.105 = f32[1,15,1304]{2,1,0:T(8,128)} reshape(f32[15,8,163]{2,1,0:T(8,128)} %get-tuple-element.43) | data formatting | bytes 156480 | tf_op jit(solution)/shard_map/stack | solution.py:103
  75.4 1.7 %stack.106 = f32[1,15,1304]{2,1,0:T(8,128)} reshape(f32[15,8,163]{2,1,0:T(8,128)} %get-tuple-element.42) | data formatting | bytes 156480 | tf_op jit(solution)/shard_map/stack | solution.py:103
  77.1 1.6 %stack.107 = f32[1,15,1304]{2,1,0:T(8,128)} reshape(f32[15,8,163]{2,1,0:T(8,128)} %get-tuple-element.41) | data formatting | bytes 156480 | tf_op jit(solution)/shard_map/stack | solution.py:103
  78.7 1.6 %stack.108 = f32[1,15,1304]{2,1,0:T(8,128)} reshape(f32[15,8,163]{2,1,0:T(8,128)} %get-tuple-element.40) | data formatting | bytes 156480 | tf_op jit(solution)/shard_map/stack | solution.py:103
  80.4 1.6 %stack.109 = f32[1,15,1304]{2,1,0:T(8,128)} reshape(f32[15,8,163]{2,1,0:T(8,128)} %get-tuple-element.39) | data formatting | bytes 156480 | tf_op jit(solution)/shard_map/stack | solution.py:103
  85.3 1.6 %stack.112 = f32[1,15,1304]{2,1,0:T(8,128)} reshape(f32[15,8,163]{2,1,0:T(8,128)} %get-tuple-element.36) | data formatting | bytes 156480 | tf_op jit(solution)/shard_map/stack | solution.py:103
  86.9 1.6 %stack.113 = f32[1,15,1304]{2,1,0:T(8,128)} reshape(f32[15,8,163]{2,1,0:T(8,128)} %get-tuple-element.35) | data formatting | bytes 156480 | tf_op jit(solution)/shard_map/stack | solution.py:103
  88.6 1.6 %stack.114 = f32[1,15,1304]{2,1,0:T(8,128)} reshape(f32[15,8,163]{2,1,0:T(8,128)} %get-tuple-element.34) | data formatting | bytes 156480 | tf_op jit(solution)/shard_map/stack | solution.py:103
  91.9 1.6 %stack.116 = f32[1,15,1304]{2,1,0:T(8,128)} reshape(f32[15,8,163]{2,1,0:T(8,128)} %get-tuple-element.32) | data formatting | bytes 156480 | tf_op jit(solution)/shard_map/stack | solution.py:103
  96.8 1.6 %stack.119 = f32[1,15,1304]{2,1,0:T(8,128)} reshape(f32[15,8,163]{2,1,0:T(8,128)} %get-tuple-element.29) | data formatting | bytes 156480 | tf_op jit(solution)/shard_map/stack | solution.py:103
  98.4 1.6 %stack.120 = f32[1,15,1304]{2,1,0:T(8,128)} reshape(f32[15,8,163]{2,1,0:T(8,128)} %get-tuple-element.28) | data formatting | bytes 156480 | tf_op jit(solution)/shard_map/stack | solution.py:103
  101.7 1.6 %stack.122 = f32[1,15,1304]{2,1,0:T(8,128)} reshape(f32[15,8,163]{2,1,0:T(8,128)} %get-tuple-element.26) | data formatting | bytes 156480 | tf_op jit(solution)/shard_map/stack | solution.py:103
  103.4 1.6 %stack.123 = f32[1,15,1304]{2,1,0:T(8,128)} reshape(f32[15,8,163]{2,1,0:T(8,128)} %get-tuple-element.25) | data formatting | bytes 156480 | tf_op jit(solution)/shard_map/stack | solution.py:103
  108.3 1.6 %stack.126 = f32[1,15,1304]{2,1,0:T(8,128)} reshape(f32[15,8,163]{2,1,0:T(8,128)} %get-tuple-element.22) | data formatting | bytes 156480 | tf_op jit(solution)/shard_map/stack | solution.py:103
  109.9 1.6 %stack.127 = f32[1,15,1304]{2,1,0:T(8,128)} reshape(f32[15,8,163]{2,1,0:T(8,128)} %get-tuple-element.21) | data formatting | bytes 156480 | tf_op jit(solution)/shard_map/stack | solution.py:103
  111.6 1.6 %stack.128 = f32[1,15,1304]{2,1,0:T(8,128)} reshape(f32[15,8,163]{2,1,0:T(8,128)} %get-tuple-element.20) | data formatting | bytes 156480 | tf_op jit(solution)/shard_map/stack | solution.py:103
  113.2 1.6 %stack.129 = f32[1,15,1304]{2,1,0:T(8,128)} reshape(f32[15,8,163]{2,1,0:T(8,128)} %get-tuple-element.19) | data formatting | bytes 156480 | tf_op jit(solution)/shard_map/stack | solution.py:103
  116.5 1.6 %stack.131 = f32[1,15,1304]{2,1,0:T(8,128)} reshape(f32[15,8,163]{2,1,0:T(8,128)} %get-tuple-element.17) | data formatting | bytes 156480 | tf_op jit(solution)/shard_map/stack | solution.py:103
  118.1 1.6 %stack.132 = f32[1,15,1304]{2,1,0:T(8,128)} reshape(f32[15,8,163]{2,1,0:T(8,128)} %get-tuple-element.16) | data formatting | bytes 156480 | tf_op jit(solution)/shard_map/stack | solution.py:103
  140.3 4.3 %reshape.204 = f32[33,15,8,163]{3,2,1,0:T(8,128)} reshape(f32[33,15,1304]{2,1,0:T(8,128)S(1)} %pad.9) | data formatting | bytes 5163840 | tf_op jit(solution)/shard_map/reshape | solution.py:108
  145.3 3.8 %add_select_fusion = (f32[15,8,132]{2,1,0:T(8,128)S(1)}, f32[15,8,132]{2,1,0:T(8,128)S(1)}, f32[15,8,132]{2,1,0:T(8,128)S(1)}, f32[15,8,132]{2,1,0:T(8,128)S(1)}...) fusion(f32[15,8,2]{2,1,0:T(8,128)S(1)} %reshape.210, ...), kind=kLoop, calls=%fused_computation.232 | loop fusion | flops 3453120 | bytes 4878852 | tf_op jit(solution)/shard_map/jit(_where)/select_n | solution.py:136
  (166 shorter events, 58.1 us)
Async XLA Ops:
  0.6 16.5 %copy-start.18 = (bf16[16,128,128]{2,1,0:T(8,128)(2,1)S(1)}, bf16[16,128,128]{2,1,0:T(8,128)(2,1)}, u32[]{:S(2)}) copy-start(bf16[16,128,128]{2,1,0:T(8,128)(2,1)} %param.4) | copy-start | bytes 1572868
  2.7 16.5 %collective-permute-start = (bf16[17,15,128]{2,0,1:T(8,128)(2,1)S(1)}, bf16[17,15,128]{2,0,1:T(8,128)(2,1)S(1)}, u32[]{:S(2)}, u32[]{:S(2)}) collective-permute-start(bf16[17,15,128]{2,0,1:T(8,128)(2,1)S(1)} %pad_maximum_fusion.3), channel_id=1, source_target_pairs={{1,0},{2,1},{3,2},{4,3},{5,4},{6,5},{7,6},{8,7},{9,8},{10,9},{11,1... | collective-permute-start | bytes 195848 | tf_op jit(solution)/shard_map/ppermute | solution.py:32
  19.8 4.6 %collective-permute-start.1 = (f32[16,128,128]{1,0,2:T(8,128)S(1)}, f32[16,128,128]{1,0,2:T(8,128)S(1)}, u32[]{:S(2)}, u32[]{:S(2)}) collective-permute-start(f32[16,128,128]{1,0,2:T(8,128)S(1)} %pad_maximum_fusion), channel_id=1, source_target_pairs={{0,32},{32,0},{1,33},{33,1},{2,34},{34,2},{3,35},{35,3},{4,36},{36... | collective-permute-start | bytes 3145736 | tf_op jit(solution)/shard_map/ppermute | solution.py:78
  24.5 6.0 %copy-start.15 = (s32[15,8,16]{2,1,0:T(8,128)S(1)}, s32[15,8,16]{2,1,0:T(8,128)}, u32[]{:S(2)}) copy-start(s32[15,8,16]{2,1,0:T(8,128)} %param.6) | copy-start | bytes 23044
  24.5 6.0 %copy-start.20 = (s32[15,2]{0,1:T(2,128)S(1)}, s32[15,2]{0,1:T(2,128)}, u32[]{:S(2)}) copy-start(s32[15,2]{0,1:T(2,128)} %param.7) | copy-start | bytes 364
  24.9 8.0 %slice-start = ((s32[15,2]{0,1:T(2,128)}), s32[15,1]{0,1:T(1,128)S(1)}, s32[]{:S(2)}) async-start(s32[15,2]{0,1:T(2,128)} %param.7), calls=%async_computation.1 | async-start | bytes 1024 | tf_op jit(solution)/shard_map/slice | solution.py:92
  26.0 20.8 %all-to-all-start = ((f32[16,8,16,128]{3,2,0,1:T(8,128)}), f32[16,8,16,128]{3,2,0,1:T(8,128)S(1)}, u32[]{:S(2)}, u32[]{:S(2)}) async-start(f32[16,8,16,128]{3,2,0,1:T(8,128)} %copy.50), calls=%async_computation | async-start | bytes 2097152 | tf_op jit(solution)/shard_map/all_to_all | solution.py:80
  47.1 9.9 %collective-permute-start.2 = (f32[8824]{0:T(1024)S(1)}, f32[8824]{0:T(1024)S(1)}, u32[]{:S(2)}, u32[]{:S(2)}) collective-permute-start(f32[8824]{0:T(1024)S(1)} %pad_maximum_fusion.6), channel_id=1, source_target_pairs={{0,1},{1,2},{2,3},{3,4},{4,5},{5,6},{6,7},{7,8},{8,9},{9,10},{10,1... | collective-permute-start | bytes 105896 | tf_op jit(solution)/shard_map/ppermute | solution.py:27
  49.0 12.2 %collective-permute-start.3 = (f32[16,16,34]{2,1,0:T(8,128)S(1)}, f32[16,16,34]{2,1,0:T(8,128)S(1)}, u32[]{:S(2)}, u32[]{:S(2)}) collective-permute-start(f32[16,16,34]{2,1,0:T(8,128)S(1)} %get-tuple-element.53), channel_id=1, source_target_pairs={{1,0},{2,1},{3,2},{4,3},{5,4},{6,5},{7,6},{8,7},{9,8},{10,9},{11,1... | collective-permute-start | bytes 104456 | tf_op jit(solution)/shard_map/ppermute | solution.py:32
  120.0 15.5 %copy-start.13 = (f32[1,15,1304]{2,1,0:T(8,128)S(1)}, f32[1,15,1304]{2,1,0:T(8,128)}, u32[]{:S(2)}) copy-start(f32[1,15,1304]{2,1,0:T(8,128)} %stack.120) | copy-start | bytes 234724
  120.0 15.5 %copy-start.12 = (f32[1,15,1304]{2,1,0:T(8,128)S(1)}, f32[1,15,1304]{2,1,0:T(8,128)}, u32[]{:S(2)}) copy-start(f32[1,15,1304]{2,1,0:T(8,128)} %stack.121) | copy-start | bytes 234724
  120.0 15.6 %copy-start.11 = (f32[1,15,1304]{2,1,0:T(8,128)S(1)}, f32[1,15,1304]{2,1,0:T(8,128)}, u32[]{:S(2)}) copy-start(f32[1,15,1304]{2,1,0:T(8,128)} %stack.122) | copy-start | bytes 234724
  120.0 15.6 %copy-start.10 = (f32[1,15,1304]{2,1,0:T(8,128)S(1)}, f32[1,15,1304]{2,1,0:T(8,128)}, u32[]{:S(2)}) copy-start(f32[1,15,1304]{2,1,0:T(8,128)} %stack.123) | copy-start | bytes 234724
  120.1 15.6 %copy-start.9 = (f32[1,15,1304]{2,1,0:T(8,128)S(1)}, f32[1,15,1304]{2,1,0:T(8,128)}, u32[]{:S(2)}) copy-start(f32[1,15,1304]{2,1,0:T(8,128)} %stack.124) | copy-start | bytes 234724
  120.1 15.6 %copy-start.7 = (f32[1,15,1304]{2,1,0:T(8,128)S(1)}, f32[1,15,1304]{2,1,0:T(8,128)}, u32[]{:S(2)}) copy-start(f32[1,15,1304]{2,1,0:T(8,128)} %stack.125) | copy-start | bytes 234724
  120.1 15.6 %copy-start.8 = (f32[1,15,1304]{2,1,0:T(8,128)S(1)}, f32[1,15,1304]{2,1,0:T(8,128)}, u32[]{:S(2)}) copy-start(f32[1,15,1304]{2,1,0:T(8,128)} %stack.126) | copy-start | bytes 234724
  120.1 15.7 %copy-start.6 = (f32[1,15,1304]{2,1,0:T(8,128)S(1)}, f32[1,15,1304]{2,1,0:T(8,128)}, u32[]{:S(2)}) copy-start(f32[1,15,1304]{2,1,0:T(8,128)} %stack.127) | copy-start | bytes 234724
  120.1 15.7 %copy-start.5 = (f32[1,15,1304]{2,1,0:T(8,128)S(1)}, f32[1,15,1304]{2,1,0:T(8,128)}, u32[]{:S(2)}) copy-start(f32[1,15,1304]{2,1,0:T(8,128)} %stack.128) | copy-start | bytes 234724
  120.1 15.7 %copy-start.4 = (f32[1,15,1304]{2,1,0:T(8,128)S(1)}, f32[1,15,1304]{2,1,0:T(8,128)}, u32[]{:S(2)}) copy-start(f32[1,15,1304]{2,1,0:T(8,128)} %stack.129) | copy-start | bytes 234724
  120.1 15.7 %copy-start.3 = (f32[1,15,1304]{2,1,0:T(8,128)S(1)}, f32[1,15,1304]{2,1,0:T(8,128)}, u32[]{:S(2)}) copy-start(f32[1,15,1304]{2,1,0:T(8,128)} %stack.130) | copy-start | bytes 234724
  120.1 15.7 %copy-start.2 = (f32[1,15,1304]{2,1,0:T(8,128)S(1)}, f32[1,15,1304]{2,1,0:T(8,128)}, u32[]{:S(2)}) copy-start(f32[1,15,1304]{2,1,0:T(8,128)} %stack.131) | copy-start | bytes 234724
  120.1 15.7 %copy-start.1 = (f32[1,15,1304]{2,1,0:T(8,128)S(1)}, f32[1,15,1304]{2,1,0:T(8,128)}, u32[]{:S(2)}) copy-start(f32[1,15,1304]{2,1,0:T(8,128)} %stack.132) | copy-start | bytes 234724
  140.3 4.8 %copy-start.16 = (f32[15,8]{1,0:T(8,128)S(1)}, f32[15,8]{1,0:T(8,128)}, u32[]{:S(2)}) copy-start(f32[15,8]{1,0:T(8,128)} %copy.56) | copy-start | bytes 1444
  140.3 4.9 %copy-start.17 = (f32[15,8]{1,0:T(8,128)S(1)}, f32[15,8]{1,0:T(8,128)}, u32[]{:S(2)}) copy-start(f32[15,8]{1,0:T(8,128)} %reshape.205) | copy-start | bytes 1444
  140.3 4.9 %copy-start.14 = (f32[15,8,128]{2,1,0:T(8,128)S(1)}, f32[15,8,128]{2,1,0:T(8,128)}, u32[]{:S(2)}) copy-start(f32[15,8,128]{2,1,0:T(8,128)} %copy.57) | copy-start | bytes 184324
  140.3 4.9 %copy-start.19 = (pred[132]{0:T(512)(128)(4,1)S(1)}, pred[132]{0:T(512)(128)(4,1)}, u32[]{:S(2)}) copy-start(pred[132]{0:T(512)(128)(4,1)} %and_or_fusion) | copy-start | bytes 400
  145.2 3.8 %copy-start = (f32[33,15,8,163]{3,2,1,0:T(8,128)S(1)}, f32[33,15,8,163]{3,2,1,0:T(8,128)}, u32[]{:S(2)}) copy-start(f32[33,15,8,163]{3,2,1,0:T(8,128)} %reshape.204) | copy-start | bytes 7745764

commit v12 on v9

--- a/solution.py
+++ b/solution.py
@@ -100,9 +100,15 @@
     yr = later[:, :, 0]
     yi = later[:, :, 1]
     nlag = 2 * MAXLAG + 1
-    prods = jnp.stack(
-        [xr * yr[..., j : j + prod_len] + xi * yi[..., j : j + prod_len] for j in range(nlag)]
-    )
+    group = 3
+
+    def lag_group(first):
+        lags = range(first, min(first + group, nlag))
+        yr_g = jnp.stack([yr[..., j : j + prod_len] for j in lags])
+        yi_g = jnp.stack([yi[..., j : j + prod_len] for j in lags])
+        return xr[None] * yr_g + xi[None] * yi_g
+
+    prods = jnp.concatenate([lag_group(first) for first in range(0, nlag, group)], axis=0)
     cross_sum = window_sum(prods)
     power_a = window_sum(xr * xr + xi * xi) / (2 * WIN)
     ey = yr * yr + yi * yi

time: 78.8 us -> 84.7 us (1.075)
  local copies, waits for them, and re-layouts: 8.22 us -> 14.7 us
  other arithmetic: 17 us -> 16.1 us
    another operation x0 -> x4, local copies, waits for them, and re-layouts: none -> 5.84 us  [the longest x2 3.55 us: lag_group(): yi_g = jnp.stack([yi[..., j:j + prod_len] for j in lags])]
    unnamed x32 -> x10, other arithmetic: 4.24 us -> 3.4 us
    unnamed x10 -> x76, local copies, waits for them, and re-layouts: 1.77 us -> 2.32 us
where the time goes in v12:
time: 84.7 us; the launch traced here: 84.3 us
  starting transfers between devices  28.1 us (33%)
  waiting for transfers between devices  18.8 us (22%)
  other arithmetic  16.1 us (19%)
  local copies, waits for them, and re-layouts  14.7 us (17%)
  matrix products  5.03 us (6%)
  between operations  1.61 us (2%)
    ppermute x2, starting transfers between devices, from_right(): return lax.ppermute(block, axis, [(i + 1, i) for i in range(count - 1)])  19.8 us
    all_to_all x1, waiting for transfers between devices, shards(): vol = lax.all_to_all(vol, ('cx', 'cy'), 1, 1, tiled=True).sum(axis=1)  14.1 us
    add x13, other arithmetic, window_sum(): values = values[..., :n] + values[..., width:width + n]  6.34 us
    conv_general_dilated x4, matrix products, beamform(): lax.conv_general_dilated(extended, weights, window_strides=(1,), padding=...  5.03 us
    ppermute x2, waiting for transfers between devices, from_right(): return lax.ppermute(block, axis, [(i + 1, i) for i in range(count - 1)])  4.6 us
    all_to_all x1, starting transfers between devices, shards(): vol = lax.all_to_all(vol, ('cx', 'cy'), 1, 1, tiled=True).sum(axis=1)  4.41 us
    another operation x2, local copies, waits for them, and re-layouts, lag_group(): yi_g = jnp.stack([yi[..., j:j + prod_len] for j in lags])  3.55 us
    unnamed x10, other arithmetic  3.4 us
  transfers between devices with their start and end apart: 5, of which 3 were waited for; matrix products, arithmetic and copies ran while one was open for 11% of the time, Pallas kernels for 0%

profile of v12, /device:TPU:48, one launch (start us, length us, event | category | flops | bytes accessed | tf_op | source)
XLA Modules:
  0.0 84.3 jit_solution(16876850122235982681)
XLA Ops:
  0.6 1.0 %fusion.67 = bf16[15,8]{1,0:T(8,128)(2,1)S(1)} fusion(s32[15,8,16]{2,1,0:T(8,128)} %param.6), kind=kLoop, calls=%fused_computation.272 | loop fusion | flops 120 | bytes 720 | tf_op jit(solution)/shard_map/slice | solution.py:56
  1.8 0.9 %fusion.82 = (bf16[16,15,128]{2,1,0:T(8,128)(2,1)S(1)}, bf16[16,15,128]{2,1,0:T(8,128)(2,1)S(1)}) fusion(bf16[16,128,128]{2,1,0:T(8,128)(2,1)} %param.4), kind=kLoop, calls=%fused_computation.288 | loop fusion | bytes 245760 | tf_op jit(solution)/shard_map/slice | solution.py:64
  2.7 12.5 %collective-permute-start = (bf16[17,15,128]{2,0,1:T(8,128)(2,1)S(1)}, bf16[17,15,128]{2,0,1:T(8,128)(2,1)S(1)}, u32[]{:S(2)}, u32[]{:S(2)}) collective-permute-start(bf16[17,15,128]{2,0,1:T(8,128)(2,1)S(1)} %pad_maximum_fusion.3), channel_id=1, source_target_pairs={{1,0},{2,1},{3,2},{4,3},{5,4},{6,5},{7,6},{8,7},{9,8},{10,9},{11,1... | collective-permute-start | bytes 195848 | tf_op jit(solution)/shard_map/ppermute | solution.py:32
  15.2 1.6 %copy.43 = bf16[1,16,128,256]{2,3,1,0:T(8,128)(2,1)S(1)} copy(bf16[1,16,128,256]{3,2,1,0:T(8,128)(2,1)} %param.5) | data formatting | bytes 2097152 | tf_op args[1]
  17.1 2.1 %fusion.71 = f32[16,128,113]{1,0,2:T(8,128)S(1)} fusion(bf16[16,128,128]{1,2,0:T(8,128)(2,1)S(1)} %bitcast.440, bf16[16,128,128]{2,1,0:T(8,128)(2,1)S(1)} %copy-done.33), kind=kOutput, calls=%fused_computation.284 | convolution fusion | flops 947912704 | bytes 1974272 | tf_op jit(solution)/shard_map/conv_general_dilated | solution.py:36
  19.8 1.9 %collective-permute-start.1 = (f32[16,128,128]{1,0,2:T(8,128)S(1)}, f32[16,128,128]{1,0,2:T(8,128)S(1)}, u32[]{:S(2)}, u32[]{:S(2)}) collective-permute-start(f32[16,128,128]{1,0,2:T(8,128)S(1)} %pad_maximum_fusion), channel_id=1, source_target_pairs={{0,32},{32,0},{1,33},{33,1},{2,34},{34,2},{3,35},{35,3},{4,36},{36... | collective-permute-start | bytes 3145736 | tf_op jit(solution)/shard_map/ppermute | solution.py:78
  21.7 2.1 %fusion.73 = f32[16,128,113]{1,0,2:T(8,128)S(1)} fusion(bf16[16,128,128]{1,2,0:T(8,128)(2,1)S(1)} %bitcast.438, bf16[16,128,128]{2,1,0:T(8,128)(2,1)S(1)} %copy-done.33), kind=kOutput, calls=%fused_computation.286 | convolution fusion | flops 947912704 | bytes 1974272 | tf_op jit(solution)/shard_map/conv_general_dilated | solution.py:36
  24.9 1.1 %copy.50 = f32[16,8,16,128]{3,2,0,1:T(8,128)} copy(f32[16,8,16,128]{3,2,1,0:T(8,128)S(1)} %bitcast.436) | data formatting | bytes 2097152 | tf_op jit(solution)/shard_map/reshape | solution.py:79
  26.0 4.4 %all-to-all-start = ((f32[16,8,16,128]{3,2,0,1:T(8,128)}), f32[16,8,16,128]{3,2,0,1:T(8,128)S(1)}, u32[]{:S(2)}, u32[]{:S(2)}) async-start(f32[16,8,16,128]{3,2,0,1:T(8,128)} %copy.50), calls=%async_computation | async-start | bytes 2097152 | tf_op jit(solution)/shard_map/all_to_all | solution.py:80
  30.4 0.6 slice.588
  31.7 0.7 fusion.68
  32.7 14.1 %all-to-all-done = f32[16,8,16,128]{3,2,0,1:T(8,128)S(1)} async-done(((f32[16,8,16,128]{3,2,0,1:T(8,128)}), f32[16,8,16,128]{3,2,0,1:T(8,128)S(1)}, u32[]{:S(2)}, u32[]{:S(2)}) %all-to-all-start) | async-done | bytes 1048608 | tf_op jit(solution)/shard_map/all_to_all | solution.py:80
  47.1 1.9 %collective-permute-start.2 = (f32[8824]{0:T(1024)S(1)}, f32[8824]{0:T(1024)S(1)}, u32[]{:S(2)}, u32[]{:S(2)}) collective-permute-start(f32[8824]{0:T(1024)S(1)} %pad_maximum_fusion.6), channel_id=1, source_target_pairs={{0,1},{1,2},{2,3},{3,4},{4,5},{5,6},{6,7},{7,8},{8,9},{9,10},{10,1... | collective-permute-start | bytes 105896 | tf_op jit(solution)/shard_map/ppermute | solution.py:27
  49.0 7.3 %collective-permute-start.3 = (f32[16,16,34]{2,1,0:T(8,128)S(1)}, f32[16,16,34]{2,1,0:T(8,128)S(1)}, u32[]{:S(2)}, u32[]{:S(2)}) collective-permute-start(f32[16,16,34]{2,1,0:T(8,128)S(1)} %get-tuple-element.20), channel_id=1, source_target_pairs={{1,0},{2,1},{3,2},{4,3},{5,4},{6,5},{7,6},{8,7},{9,8},{10,9},{11,1... | collective-permute-start | bytes 104456 | tf_op jit(solution)/shard_map/ppermute | solution.py:32
  56.6 4.6 %collective-permute-done.3 = f32[16,16,34]{2,1,0:T(8,128)S(1)} collective-permute-done((f32[16,16,34]{2,1,0:T(8,128)S(1)}, f32[16,16,34]{2,1,0:T(8,128)S(1)}, u32[]{:S(2)}, u32[]{:S(2)}) %collective-permute-start.3) | collective-permute-done | bytes 34848 | tf_op jit(solution)/shard_map/ppermute | solution.py:32
  61.4 0.6 gather_fusion
  62.4 1.6 %slice_bitcast_fusion.74 = (f32[1,15,8,163]{3,2,1,0:T(8,128)}, f32[1,15,8,163]{3,2,1,0:T(8,128)}, f32[1,15,8,163]{3,2,1,0:T(8,128)}, f32[1,15,8,163]{3,2,1,0:T(8...) fusion(f32[15,8,196]{2,1,0:T(8,128)S(1)} %get-tuple-element.89), kind=kLoop, calls=%fused_computation.211 | loop fusion | bytes 2190720 | tf_op jit(solution)/shard_map/stack | solution.py:107
  64.0 0.7 slice_bitcast_fusion.38
  64.7 1.6 %slice_bitcast_fusion.71 = (f32[1,15,8,163]{3,2,1,0:T(8,128)}, f32[1,15,8,163]{3,2,1,0:T(8,128)}, f32[1,15,8,163]{3,2,1,0:T(8,128)}, f32[1,15,8,163]{3,2,1,0:T(8...) fusion(f32[15,8,196]{2,1,0:T(8,128)S(1)} %get-tuple-element.88), kind=kLoop, calls=%fused_computation.208 | loop fusion | bytes 2190720 | tf_op jit(solution)/shard_map/stack | solution.py:108
  66.3 1.9 %slice_bitcast_fusion.35 = (f32[1,15,8,163]{3,2,1,0:T(8,128)S(1)}, f32[1,15,8,163]{3,2,1,0:T(8,128)S(1)}, f32[1,15,8,163]{3,2,1,0:T(8,128)S(1)}, f32[1,15,8,163]...) fusion(f32[15,8,196]{2,1,0:T(8,128)S(1)} %get-tuple-element.88), kind=kLoop, calls=%fused_computation.172 | loop fusion | bytes 2973120 | tf_op jit(solution)/shard_map/stack | solution.py:108
  68.4 0.6 fusion.84
  69.9 1.5 %fusion.1 = f32[33,15,8,163]{3,2,1,0:T(8,128)S(1)} fusion(f32[1,15,8,163]{3,2,1,0:T(8,128)} %get-tuple-element.85, f32[1,15,8,163]{3,2,1,0:T(8,128)} %get-tuple-element.86, f32[1,15,8,163]{3,2,1,0:T(8,128)} %get-tuple-element.87, f32[1,15,8,163]{3,2,1,0:T(8,128)} %get-tuple-element.71, f32[1,15,8,163]{3,2,1,0:T(8,128)} %get-tuple-element.72, ...), kind=kLoop, calls=%fused_computation.10 | loop fusion | flops 410759 | bytes 994560
  71.4 1.3 %fusion.3 = f32[33,15,8,163]{3,2,1,0:T(8,128)S(1)} fusion(f32[33,15,8,163]{3,2,1,0:T(8,128)S(1)} %fusion.1, f32[1,15,8,163]{3,2,1,0:T(8,128)} %get-tuple-element.82, f32[1,15,8,163]{3,2,1,0:T(8,128)} %get-tuple-element.83, f32[1,15,8,163]{3,2,1,0:T(8,128)} %get-tuple-element.84, f32[1,15,8,163]{3,2,1,0:T(8,128)} %get-tuple-element.68, ...), kind=kLoop, calls=%fused_computation.14 | loop fusion | flops 410760 | bytes 1083840
  74.2 1.1 %slice_add_fusion.4 = f32[33,15,8,162]{3,2,1,0:T(8,128)S(1)} fusion(f32[33,15,8,163]{3,2,1,0:T(8,128)S(1)} %fusion.21), kind=kLoop, calls=%fused_computation.5 | loop fusion | flops 641520 | bytes 7698240 | tf_op jit(solution)/shard_map/add | solution.py:20
  75.3 1.1 %slice_add_fusion.3 = f32[33,15,8,160]{3,2,1,0:T(8,128)S(1)} fusion(f32[33,15,8,162]{3,2,1,0:T(8,128)S(1)} %slice_add_fusion.4), kind=kLoop, calls=%fused_computation.4 | loop fusion | flops 633600 | bytes 7603200 | tf_op jit(solution)/shard_map/add | solution.py:20
  76.4 1.1 %slice_add_fusion.2 = f32[33,15,8,156]{3,2,1,0:T(8,128)S(1)} fusion(f32[33,15,8,160]{3,2,1,0:T(8,128)S(1)} %slice_add_fusion.3), kind=kLoop, calls=%fused_computation.3 | loop fusion | flops 617760 | bytes 7413120 | tf_op jit(solution)/shard_map/add | solution.py:20
  77.5 1.1 %slice_add_fusion.1 = f32[33,15,8,148]{3,2,1,0:T(8,128)S(1)} fusion(f32[33,15,8,156]{3,2,1,0:T(8,128)S(1)} %slice_add_fusion.2), kind=kLoop, calls=%fused_computation.2 | loop fusion | flops 586080 | bytes 7032960 | tf_op jit(solution)/shard_map/add | solution.py:20
  78.6 1.1 %slice_add_fusion = f32[33,15,8,132]{3,2,1,0:T(8,128)S(1)} fusion(f32[33,15,8,148]{3,2,1,0:T(8,128)S(1)} %slice_add_fusion.1), kind=kLoop, calls=%fused_computation.1 | loop fusion | flops 522720 | bytes 6272640 | tf_op jit(solution)/shard_map/add | solution.py:20
  80.3 1.5 %add_select_fusion = (f32[15,8,132]{2,1,0:T(8,128)S(1)}, f32[15,8,132]{2,1,0:T(8,128)S(1)}, f32[15,8,132]{2,1,0:T(8,128)S(1)}, f32[15,8,132]{2,1,0:T(8,128)S(1)}...) fusion(f32[15,8,2]{2,1,0:T(8,128)S(1)} %reshape.141, ...), kind=kLoop, calls=%fused_computation.242 | loop fusion | flops 3453120 | bytes 4878852 | tf_op jit(solution)/shard_map/jit(_where)/select_n | solution.py:140
  81.8 0.9 %maximum_maximum_fusion = f32[15,8,132]{2,1,0:T(8,128)S(1)} fusion(f32[15,8,132]{2,1,0:T(8,128)S(1)} %get-tuple-element.9, f32[15,8,164]{2,1,0:T(8,128)S(1)} %fusion.57, f32[33,15,8,132]{3,2,1,0:T(8,128)S(1)} %slice_add_fusion), kind=kLoop, calls=%fused_computation.243 | loop fusion | flops 1267200 | bytes 3548160 | tf_op jit(solution)/shard_map/max | solution.py:130
  82.7 0.7 fusion.64
  83.5 0.8 slice_maximum_fusion
  (139 shorter events, 6.5 us)
Async XLA Ops:
  0.6 16.5 %copy-start.33 = (bf16[16,128,128]{2,1,0:T(8,128)(2,1)S(1)}, bf16[16,128,128]{2,1,0:T(8,128)(2,1)}, u32[]{:S(2)}) copy-start(bf16[16,128,128]{2,1,0:T(8,128)(2,1)} %param.4) | copy-start | bytes 1572868
  2.7 16.5 %collective-permute-start = (bf16[17,15,128]{2,0,1:T(8,128)(2,1)S(1)}, bf16[17,15,128]{2,0,1:T(8,128)(2,1)S(1)}, u32[]{:S(2)}, u32[]{:S(2)}) collective-permute-start(bf16[17,15,128]{2,0,1:T(8,128)(2,1)S(1)} %pad_maximum_fusion.3), channel_id=1, source_target_pairs={{1,0},{2,1},{3,2},{4,3},{5,4},{6,5},{7,6},{8,7},{9,8},{10,9},{11,1... | collective-permute-start | bytes 195848 | tf_op jit(solution)/shard_map/ppermute | solution.py:32
  19.8 4.6 %collective-permute-start.1 = (f32[16,128,128]{1,0,2:T(8,128)S(1)}, f32[16,128,128]{1,0,2:T(8,128)S(1)}, u32[]{:S(2)}, u32[]{:S(2)}) collective-permute-start(f32[16,128,128]{1,0,2:T(8,128)S(1)} %pad_maximum_fusion), channel_id=1, source_target_pairs={{0,32},{32,0},{1,33},{33,1},{2,34},{34,2},{3,35},{35,3},{4,36},{36... | collective-permute-start | bytes 3145736 | tf_op jit(solution)/shard_map/ppermute | solution.py:78
  24.2 6.2 %copy-start.32 = (s32[15,8,16]{2,1,0:T(8,128)S(1)}, s32[15,8,16]{2,1,0:T(8,128)}, u32[]{:S(2)}) copy-start(s32[15,8,16]{2,1,0:T(8,128)} %param.6) | copy-start | bytes 23044
  24.2 6.2 %copy-start.34 = (s32[15,2]{0,1:T(2,128)S(1)}, s32[15,2]{0,1:T(2,128)}, u32[]{:S(2)}) copy-start(s32[15,2]{0,1:T(2,128)} %param.7) | copy-start | bytes 364
  24.5 7.2 %slice-start = ((s32[15,2]{0,1:T(2,128)}), s32[15,1]{0,1:T(1,128)S(1)}, s32[]{:S(2)}) async-start(s32[15,2]{0,1:T(2,128)} %param.7), calls=%async_computation.1 | async-start | bytes 1024 | tf_op jit(solution)/shard_map/slice | solution.py:92
  26.0 20.8 %all-to-all-start = ((f32[16,8,16,128]{3,2,0,1:T(8,128)}), f32[16,8,16,128]{3,2,0,1:T(8,128)S(1)}, u32[]{:S(2)}, u32[]{:S(2)}) async-start(f32[16,8,16,128]{3,2,0,1:T(8,128)} %copy.50), calls=%async_computation | async-start | bytes 2097152 | tf_op jit(solution)/shard_map/all_to_all | solution.py:80
  47.1 9.3 %collective-permute-start.2 = (f32[8824]{0:T(1024)S(1)}, f32[8824]{0:T(1024)S(1)}, u32[]{:S(2)}, u32[]{:S(2)}) collective-permute-start(f32[8824]{0:T(1024)S(1)} %pad_maximum_fusion.6), channel_id=1, source_target_pairs={{0,1},{1,2},{2,3},{3,4},{4,5},{5,6},{6,7},{7,8},{8,9},{9,10},{10,1... | collective-permute-start | bytes 105896 | tf_op jit(solution)/shard_map/ppermute | solution.py:27
  49.0 12.2 %collective-permute-start.3 = (f32[16,16,34]{2,1,0:T(8,128)S(1)}, f32[16,16,34]{2,1,0:T(8,128)S(1)}, u32[]{:S(2)}, u32[]{:S(2)}) collective-permute-start(f32[16,16,34]{2,1,0:T(8,128)S(1)} %get-tuple-element.20), channel_id=1, source_target_pairs={{1,0},{2,1},{3,2},{4,3},{5,4},{6,5},{7,6},{8,7},{9,8},{10,9},{11,1... | collective-permute-start | bytes 104456 | tf_op jit(solution)/shard_map/ppermute | solution.py:32
  69.0 4.1 %copy-start.15 = (f32[1,15,8,163]{3,2,1,0:T(8,128)S(1)}, f32[1,15,8,163]{3,2,1,0:T(8,128)}, u32[]{:S(2)}) copy-start(f32[1,15,8,163]{3,2,1,0:T(8,128)} %get-tuple-element.40) | copy-start | bytes 234724
  69.0 4.1 %copy-start.16 = (f32[1,15,8,163]{3,2,1,0:T(8,128)S(1)}, f32[1,15,8,163]{3,2,1,0:T(8,128)}, u32[]{:S(2)}) copy-start(f32[1,15,8,163]{3,2,1,0:T(8,128)} %get-tuple-element.74) | copy-start | bytes 234724
  69.1 3.6 %copy-start.21 = (f32[1,15,8,163]{3,2,1,0:T(8,128)S(1)}, f32[1,15,8,163]{3,2,1,0:T(8,128)}, u32[]{:S(2)}) copy-start(f32[1,15,8,163]{3,2,1,0:T(8,128)} %get-tuple-element.79) | copy-start | bytes 234724
  69.1 3.6 %copy-start.22 = (f32[1,15,8,163]{3,2,1,0:T(8,128)S(1)}, f32[1,15,8,163]{3,2,1,0:T(8,128)}, u32[]{:S(2)}) copy-start(f32[1,15,8,163]{3,2,1,0:T(8,128)} %get-tuple-element.80) | copy-start | bytes 234724
  69.2 3.6 %copy-start.23 = (f32[1,15,8,163]{3,2,1,0:T(8,128)S(1)}, f32[1,15,8,163]{3,2,1,0:T(8,128)}, u32[]{:S(2)}) copy-start(f32[1,15,8,163]{3,2,1,0:T(8,128)} %get-tuple-element.81) | copy-start | bytes 234724
  69.2 3.6 %copy-start.29 = (f32[1,15,8,163]{3,2,1,0:T(8,128)S(1)}, f32[1,15,8,163]{3,2,1,0:T(8,128)}, u32[]{:S(2)}) copy-start(f32[1,15,8,163]{3,2,1,0:T(8,128)} %get-tuple-element.65) | copy-start | bytes 234724
  69.2 3.6 %copy-start.30 = (f32[1,15,8,163]{3,2,1,0:T(8,128)S(1)}, f32[1,15,8,163]{3,2,1,0:T(8,128)}, u32[]{:S(2)}) copy-start(f32[1,15,8,163]{3,2,1,0:T(8,128)} %get-tuple-element.66) | copy-start | bytes 234724
  69.2 3.6 %copy-start.31 = (f32[1,15,8,163]{3,2,1,0:T(8,128)S(1)}, f32[1,15,8,163]{3,2,1,0:T(8,128)}, u32[]{:S(2)}) copy-start(f32[1,15,8,163]{3,2,1,0:T(8,128)} %get-tuple-element.67) | copy-start | bytes 234724
  69.2 3.7 %copy-start.18 = (f32[1,15,8,163]{3,2,1,0:T(8,128)S(1)}, f32[1,15,8,163]{3,2,1,0:T(8,128)}, u32[]{:S(2)}) copy-start(f32[1,15,8,163]{3,2,1,0:T(8,128)} %get-tuple-element.76) | copy-start | bytes 234724
  69.2 3.7 %copy-start.19 = (f32[1,15,8,163]{3,2,1,0:T(8,128)S(1)}, f32[1,15,8,163]{3,2,1,0:T(8,128)}, u32[]{:S(2)}) copy-start(f32[1,15,8,163]{3,2,1,0:T(8,128)} %get-tuple-element.77) | copy-start | bytes 234724
  69.2 3.7 %copy-start.20 = (f32[1,15,8,163]{3,2,1,0:T(8,128)S(1)}, f32[1,15,8,163]{3,2,1,0:T(8,128)}, u32[]{:S(2)}) copy-start(f32[1,15,8,163]{3,2,1,0:T(8,128)} %get-tuple-element.78) | copy-start | bytes 234724
  69.2 3.7 %copy-start.26 = (f32[1,15,8,163]{3,2,1,0:T(8,128)S(1)}, f32[1,15,8,163]{3,2,1,0:T(8,128)}, u32[]{:S(2)}) copy-start(f32[1,15,8,163]{3,2,1,0:T(8,128)} %get-tuple-element.62) | copy-start | bytes 234724
  69.2 3.7 %copy-start.27 = (f32[1,15,8,163]{3,2,1,0:T(8,128)S(1)}, f32[1,15,8,163]{3,2,1,0:T(8,128)}, u32[]{:S(2)}) copy-start(f32[1,15,8,163]{3,2,1,0:T(8,128)} %get-tuple-element.63) | copy-start | bytes 234724
  69.2 3.7 %copy-start.28 = (f32[1,15,8,163]{3,2,1,0:T(8,128)S(1)}, f32[1,15,8,163]{3,2,1,0:T(8,128)}, u32[]{:S(2)}) copy-start(f32[1,15,8,163]{3,2,1,0:T(8,128)} %get-tuple-element.64) | copy-start | bytes 234724
  69.3 3.8 %copy-start.17 = (f32[1,15,8,163]{3,2,1,0:T(8,128)S(1)}, f32[1,15,8,163]{3,2,1,0:T(8,128)}, u32[]{:S(2)}) copy-start(f32[1,15,8,163]{3,2,1,0:T(8,128)} %get-tuple-element.75) | copy-start | bytes 234724
  69.3 3.8 %copy-start.24 = (f32[1,15,8,163]{3,2,1,0:T(8,128)S(1)}, f32[1,15,8,163]{3,2,1,0:T(8,128)}, u32[]{:S(2)}) copy-start(f32[1,15,8,163]{3,2,1,0:T(8,128)} %get-tuple-element.60) | copy-start | bytes 234724
  69.3 3.8 %copy-start.25 = (f32[1,15,8,163]{3,2,1,0:T(8,128)S(1)}, f32[1,15,8,163]{3,2,1,0:T(8,128)}, u32[]{:S(2)}) copy-start(f32[1,15,8,163]{3,2,1,0:T(8,128)} %get-tuple-element.61) | copy-start | bytes 234724
  69.5 3.7 %copy-start.12 = (f32[1,15,8,163]{3,2,1,0:T(8,128)S(1)}, f32[1,15,8,163]{3,2,1,0:T(8,128)}, u32[]{:S(2)}) copy-start(f32[1,15,8,163]{3,2,1,0:T(8,128)} %get-tuple-element.37) | copy-start | bytes 234724
  69.5 3.7 %copy-start.13 = (f32[1,15,8,163]{3,2,1,0:T(8,128)S(1)}, f32[1,15,8,163]{3,2,1,0:T(8,128)}, u32[]{:S(2)}) copy-start(f32[1,15,8,163]{3,2,1,0:T(8,128)} %get-tuple-element.38) | copy-start | bytes 234724
  69.5 3.7 %copy-start.14 = (f32[1,15,8,163]{3,2,1,0:T(8,128)S(1)}, f32[1,15,8,163]{3,2,1,0:T(8,128)}, u32[]{:S(2)}) copy-start(f32[1,15,8,163]{3,2,1,0:T(8,128)} %get-tuple-element.39) | copy-start | bytes 234724
  69.8 3.4 %copy-start.9 = (f32[1,15,8,163]{3,2,1,0:T(8,128)S(1)}, f32[1,15,8,163]{3,2,1,0:T(8,128)}, u32[]{:S(2)}) copy-start(f32[1,15,8,163]{3,2,1,0:T(8,128)} %get-tuple-element.34) | copy-start | bytes 234724
  69.9 3.4 %copy-start.10 = (f32[1,15,8,163]{3,2,1,0:T(8,128)S(1)}, f32[1,15,8,163]{3,2,1,0:T(8,128)}, u32[]{:S(2)}) copy-start(f32[1,15,8,163]{3,2,1,0:T(8,128)} %get-tuple-element.35) | copy-start | bytes 234724
  69.9 3.4 %copy-start.11 = (f32[1,15,8,163]{3,2,1,0:T(8,128)S(1)}, f32[1,15,8,163]{3,2,1,0:T(8,128)}, u32[]{:S(2)}) copy-start(f32[1,15,8,163]{3,2,1,0:T(8,128)} %get-tuple-element.36) | copy-start | bytes 234724
  (9 other events, 12.0 us)

commit v13 on v9

--- a/solution.py
+++ b/solution.py
@@ -70,12 +70,11 @@
     core = lax.axis_index("cc")
     w_mine = lax.dynamic_index_in_dim(w6, core, 4, keepdims=False).reshape(taps, cin, -1)
     w_other = lax.dynamic_index_in_dim(w6, 1 - core, 4, keepdims=False).reshape(taps, cin, -1)
-    def beam(w):
-        return jnp.concatenate([beamform(channel_data, w), beamform(tail_rows, w)], axis=2)
-
-    vol_other = beam(w_other)
-    vol_mine = beam(w_mine)
-    vol = vol_mine + lax.ppermute(vol_other, "cc", [(0, 1), (1, 0)])
+    swap = [(0, 1), (1, 0)]
+    got_main = lax.ppermute(beamform(channel_data, w_other), "cc", swap)
+    got_tail = lax.ppermute(beamform(tail_rows, w_other), "cc", swap)
+    vol_mine = jnp.concatenate([beamform(channel_data, w_mine), beamform(tail_rows, w_mine)], axis=2)
+    vol = vol_mine + jnp.concatenate([got_main, got_tail], axis=2)
     vol = vol.reshape(frames, nx * ny, per_dev, sample_rows)
     vol = lax.all_to_all(vol, ("cx", "cy"), 1, 1, tiled=True).sum(axis=1)
 

time: 78.8 us -> 86.8 us (1.10)
  local copies, waits for them, and re-layouts: 8.22 us -> 10.6 us
  starting transfers between devices: 28.1 us -> 30.1 us
  waiting for transfers between devices: 18.8 us -> 20.6 us
  matrix products: 5.03 us -> 5.96 us
    ppermute x0 -> x1, local copies, waits for them, and re-layouts: none -> 2.51 us  [shards(): got_main = lax.ppermute(beamform(channel_data, w_other), 'cc', swap)]
    ppermute x1 -> x2, starting transfers between devices: 1.92 us -> 3.83 us  [the longest x1 1.92 us: shards(): got_tail = lax.ppermute(beamform(tail_rows, w_other), 'cc', swap)]
    add x1, other arithmetic: 0.14 us -> 1.84 us  [shards(): vol = vol_mine + jnp.concatenate([got_main, got_tail], axis=2)]
    ppermute x2, waiting for transfers between devices: 4.61 us -> 6.25 us  [from_right(): return lax.ppermute(block, axis, [(i + 1, i) for i in range(count - 1)])]
    reshape x1 -> x0, local copies, waits for them, and re-layouts: 1.07 us -> none  [shards(): vol = vol.reshape(frames, nx * ny, per_dev, sample_rows)]
    conv_general_dilated x4, matrix products: 5.03 us -> 5.96 us  [beamform(): lax.conv_general_dilated(extended, weights, window_strides=(1,), padding=...]
    slice x1, other arithmetic: 0.98 us -> 0.1 us  [shards(): first_lags = peak_lags[:, :, 0].astype(channel_data.dtype).reshape(-1)]
    slice x1, local copies, waits for them, and re-layouts: 0.9 us -> 0.02 us  [shards(): channel_data[:, main_rows:, :]]
  transfers between devices with their start and end apart: 5 -> 6, of which waited for: 3 -> 4; matrix products, arithmetic and copies ran while one was open for 11% -> 8% of each run, Pallas kernels for 0% -> 0%
where the time goes in v13:
time: 86.8 us; the launch traced here: 86.5 us
  starting transfers between devices  30.1 us (35%)
  waiting for transfers between devices  20.6 us (24%)
  other arithmetic  17.8 us (21%)
  local copies, waits for them, and re-layouts  10.6 us (12%)
  matrix products  5.96 us (7%)
  between operations  1.38 us (2%)
    ppermute x2, starting transfers between devices, from_right(): return lax.ppermute(block, axis, [(i + 1, i) for i in range(count - 1)])  20.1 us
    all_to_all x1, waiting for transfers between devices, shards(): vol = lax.all_to_all(vol, ('cx', 'cy'), 1, 1, tiled=True).sum(axis=1)  13.8 us
    add x13, other arithmetic, window_sum(): values = values[..., :n] + values[..., width:width + n]  6.37 us
    ppermute x2, waiting for transfers between devices, from_right(): return lax.ppermute(block, axis, [(i + 1, i) for i in range(count - 1)])  6.25 us
    conv_general_dilated x4, matrix products, beamform(): lax.conv_general_dilated(extended, weights, window_strides=(1,), padding=...  5.96 us
    all_to_all x1, starting transfers between devices, shards(): vol = lax.all_to_all(vol, ('cx', 'cy'), 1, 1, tiled=True).sum(axis=1)  4.3 us
    unnamed x32, other arithmetic  4.24 us
    ppermute x1, local copies, waits for them, and re-layouts, shards(): got_main = lax.ppermute(beamform(channel_data, w_other), 'cc', swap)  2.51 us
  transfers between devices with their start and end apart: 6, of which 4 were waited for; matrix products, arithmetic and copies ran while one was open for 8% of the time, Pallas kernels for 0%

profile of v13, /device:TPU:48, one launch (start us, length us, event | category | flops | bytes accessed | tf_op | source)
XLA Modules:
  0.0 86.5 jit_solution(14531381782980134023)
XLA Ops:
  0.6 1.7 %copy.49 = bf16[1,16,128,256]{2,3,1,0:T(8,128)(2,1)S(1)} copy(bf16[1,16,128,256]{3,2,1,0:T(8,128)(2,1)} %param.5) | data formatting | bytes 2097152 | tf_op args[1]
  2.6 3.0 %fusion.149 = f32[16,128,113]{1,0,2:T(8,128)} fusion(bf16[16,128,128]{1,2,0:T(8,128)(2,1)S(1)} %bitcast.521, bf16[16,128,128]{2,1,0:T(8,128)(2,1)S(1)} %copy-done.1), kind=kOutput, calls=%fused_computation.338 | convolution fusion | flops 947912704 | bytes 1974272 | tf_op jit(solution)/shard_map/conv_general_dilated | solution.py:36
  5.6 1.9 %collective-permute-start.1 = (f32[16,128,113]{1,0,2:T(8,128)}, f32[16,128,113]{1,0,2:T(8,128)}, u32[]{:S(2)}, u32[]{:S(2)}) collective-permute-start(f32[16,128,113]{1,0,2:T(8,128)} %fusion.149), channel_id=1, source_target_pairs={{0,32},{32,0},{1,33},{33,1},{2,34},{34,2},{3,35},{35,3},{4,36},{36... | collective-permute-start | bytes 2777096 | tf_op jit(solution)/shard_map/ppermute | solution.py:74
  7.9 12.5 %collective-permute-start = (bf16[17,15,128]{2,0,1:T(8,128)(2,1)S(1)}, bf16[17,15,128]{2,0,1:T(8,128)(2,1)S(1)}, u32[]{:S(2)}, u32[]{:S(2)}) collective-permute-start(bf16[17,15,128]{2,0,1:T(8,128)(2,1)S(1)} %pad_maximum_fusion.2), channel_id=1, source_target_pairs={{1,0},{2,1},{3,2},{4,3},{5,4},{6,5},{7,6},{8,7},{9,8},{10,9},{11,1... | collective-permute-start | bytes 195848 | tf_op jit(solution)/shard_map/ppermute | solution.py:32
  20.4 2.1 %fusion.151 = f32[16,128,113]{1,0,2:T(8,128)S(1)} fusion(bf16[16,128,128]{1,2,0:T(8,128)(2,1)S(1)} %bitcast.519, bf16[16,128,128]{2,1,0:T(8,128)(2,1)S(1)} %copy-done.2), kind=kOutput, calls=%fused_computation.340 | convolution fusion | flops 947912704 | bytes 1974272 | tf_op jit(solution)/shard_map/conv_general_dilated | solution.py:36
  22.5 0.4 copy.51
  23.0 2.0 %collective-permute-done = bf16[17,15,128]{2,0,1:T(8,128)(2,1)S(1)} collective-permute-done((bf16[17,15,128]{2,0,1:T(8,128)(2,1)S(1)}, bf16[17,15,128]{2,0,1:T(8,128)(2,1)S(1)}, u32[]{:S(2)}, u32[]{:S(2)}) %collective-permute-start) | collective-permute-done | bytes 65312 | tf_op jit(solution)/shard_map/ppermute | solution.py:32
  24.9 0.4 fusion.140
  25.4 1.9 %collective-permute-start.2 = (f32[16,128,15]{1,0,2:T(8,128)S(1)}, f32[16,128,15]{1,0,2:T(8,128)S(1)}, u32[]{:S(2)}, u32[]{:S(2)}) collective-permute-start(f32[16,128,15]{1,0,2:T(8,128)S(1)} %fusion.140), channel_id=1, source_target_pairs={{0,32},{32,0},{1,33},{33,1},{2,34},{34,2},{3,35},{35,3},{4,36},{36... | collective-permute-start | bytes 368648 | tf_op jit(solution)/shard_map/ppermute | solution.py:75
  27.3 0.4 fusion.141
  28.1 0.5 collective-permute-done.2
  29.0 2.5 %copy.57 = f32[16,128,113]{2,1,0:T(8,128)} copy(f32[16,128,113]{1,0,2:T(8,128)} %collective-permute-done.1) | data formatting | bytes 1851392 | tf_op jit(solution)/shard_map/ppermute | solution.py:74
  31.5 1.8 %maximum_add_fusion = f32[16,8,16,128]{3,2,1,0:T(8,128)S(1)} fusion(f32[16,8,16,15]{3,2,1,0:T(8,128)S(1)} %bitcast.514, f32[16,8,16,113]{3,2,1,0:T(8,128)S(1)} %bitcast.516, f32[16,8,16,15]{3,2,1,0:T(8,128)S(1)} %bitcast.515, f32[16,8,16,113]{3,2,1,0:T(8,128)} %bitcast.517), kind=kLoop, calls=%fused_computation.6 | loop fusion | flops 786432 | bytes 3145728 | tf_op jit(solution)/shard_map/add | solution.py:77
  33.4 1.1 %copy.59 = f32[16,8,16,128]{3,2,0,1:T(8,128)} copy(f32[16,8,16,128]{3,2,1,0:T(8,128)S(1)} %maximum_add_fusion) | data formatting | bytes 2097152 | tf_op jit(solution)/shard_map/add | solution.py:77
  34.4 4.3 %all-to-all-start = ((f32[16,8,16,128]{3,2,0,1:T(8,128)}), f32[16,8,16,128]{3,2,0,1:T(8,128)S(1)}, u32[]{:S(2)}, u32[]{:S(2)}) async-start(f32[16,8,16,128]{3,2,0,1:T(8,128)} %copy.59), calls=%async_computation | async-start | bytes 2097152 | tf_op jit(solution)/shard_map/all_to_all | solution.py:79
  38.7 0.6 slice.588
  40.0 0.7 fusion.146
  41.0 13.8 %all-to-all-done = f32[16,8,16,128]{3,2,0,1:T(8,128)S(1)} async-done(((f32[16,8,16,128]{3,2,0,1:T(8,128)}), f32[16,8,16,128]{3,2,0,1:T(8,128)S(1)}, u32[]{:S(2)}, u32[]{:S(2)}) %all-to-all-start) | async-done | bytes 1048608 | tf_op jit(solution)/shard_map/all_to_all | solution.py:79
  55.1 1.9 %collective-permute-start.3 = (f32[8824]{0:T(1024)S(1)}, f32[8824]{0:T(1024)S(1)}, u32[]{:S(2)}, u32[]{:S(2)}) collective-permute-start(f32[8824]{0:T(1024)S(1)} %pad_maximum_fusion.5), channel_id=1, source_target_pairs={{0,1},{1,2},{2,3},{3,4},{4,5},{5,6},{6,7},{7,8},{8,9},{9,10},{10,1... | collective-permute-start | bytes 105896 | tf_op jit(solution)/shard_map/ppermute | solution.py:27
  57.0 7.6 %collective-permute-start.4 = (f32[16,16,34]{2,1,0:T(8,128)S(1)}, f32[16,16,34]{2,1,0:T(8,128)S(1)}, u32[]{:S(2)}, u32[]{:S(2)}) collective-permute-start(f32[16,16,34]{2,1,0:T(8,128)S(1)} %get-tuple-element.20), channel_id=1, source_target_pairs={{1,0},{2,1},{3,2},{4,3},{5,4},{6,5},{7,6},{8,7},{9,8},{10,9},{11,1... | collective-permute-start | bytes 104456 | tf_op jit(solution)/shard_map/ppermute | solution.py:32
  64.9 4.3 %collective-permute-done.4 = f32[16,16,34]{2,1,0:T(8,128)S(1)} collective-permute-done((f32[16,16,34]{2,1,0:T(8,128)S(1)}, f32[16,16,34]{2,1,0:T(8,128)S(1)}, u32[]{:S(2)}, u32[]{:S(2)}) %collective-permute-start.4) | collective-permute-done | bytes 34848 | tf_op jit(solution)/shard_map/ppermute | solution.py:32
  69.3 0.6 gather_fusion
  71.1 0.6 fusion.162
  76.3 1.1 %slice_add_fusion.4 = f32[33,15,8,162]{3,2,1,0:T(8,128)S(1)} fusion(f32[33,15,8,163]{3,2,1,0:T(8,128)S(1)} %fusion.42), kind=kLoop, calls=%fused_computation.5 | loop fusion | flops 641520 | bytes 7698240 | tf_op jit(solution)/shard_map/add | solution.py:20
  77.5 1.1 %slice_add_fusion.3 = f32[33,15,8,160]{3,2,1,0:T(8,128)S(1)} fusion(f32[33,15,8,162]{3,2,1,0:T(8,128)S(1)} %slice_add_fusion.4), kind=kLoop, calls=%fused_computation.4 | loop fusion | flops 633600 | bytes 7603200 | tf_op jit(solution)/shard_map/add | solution.py:20
  78.6 1.1 %slice_add_fusion.2 = f32[33,15,8,156]{3,2,1,0:T(8,128)S(1)} fusion(f32[33,15,8,160]{3,2,1,0:T(8,128)S(1)} %slice_add_fusion.3), kind=kLoop, calls=%fused_computation.3 | loop fusion | flops 617760 | bytes 7413120 | tf_op jit(solution)/shard_map/add | solution.py:20
  79.7 1.1 %slice_add_fusion.1 = f32[33,15,8,148]{3,2,1,0:T(8,128)S(1)} fusion(f32[33,15,8,156]{3,2,1,0:T(8,128)S(1)} %slice_add_fusion.2), kind=kLoop, calls=%fused_computation.2 | loop fusion | flops 586080 | bytes 7032960 | tf_op jit(solution)/shard_map/add | solution.py:20
  80.8 1.1 %slice_add_fusion = f32[33,15,8,132]{3,2,1,0:T(8,128)S(1)} fusion(f32[33,15,8,148]{3,2,1,0:T(8,128)S(1)} %slice_add_fusion.1), kind=kLoop, calls=%fused_computation.1 | loop fusion | flops 522720 | bytes 6272640 | tf_op jit(solution)/shard_map/add | solution.py:20
  82.5 1.5 %add_select_fusion = (f32[15,8,132]{2,1,0:T(8,128)S(1)}, f32[15,8,132]{2,1,0:T(8,128)S(1)}, f32[15,8,132]{2,1,0:T(8,128)S(1)}, f32[15,8,132]{2,1,0:T(8,128)S(1)}...) fusion(f32[15,8,2]{2,1,0:T(8,128)S(1)} %reshape.140, ...), kind=kLoop, calls=%fused_computation.297 | loop fusion | flops 3453120 | bytes 4878852 | tf_op jit(solution)/shard_map/jit(_where)/select_n | solution.py:133
  84.0 0.9 %maximum_maximum_fusion = f32[15,8,132]{2,1,0:T(8,128)S(1)} fusion(f32[15,8,132]{2,1,0:T(8,128)S(1)} %get-tuple-element.9, f32[15,8,164]{2,1,0:T(8,128)S(1)} %fusion.35, f32[33,15,8,132]{3,2,1,0:T(8,128)S(1)} %slice_add_fusion), kind=kLoop, calls=%fused_computation.298 | loop fusion | flops 1267200 | bytes 3548160 | tf_op jit(solution)/shard_map/max | solution.py:123
  84.9 0.7 fusion.142
  85.7 0.8 slice_maximum_fusion
  (97 shorter events, 8.9 us)
Async XLA Ops:
  0.6 2.0 %copy-start.1 = (bf16[16,128,128]{2,1,0:T(8,128)(2,1)S(1)}, bf16[16,128,128]{2,1,0:T(8,128)(2,1)}, u32[]{:S(2)}) copy-start(bf16[16,128,128]{2,1,0:T(8,128)(2,1)} %param.4) | copy-start | bytes 1572868
  2.3 5.3 %copy-start = (s32[15,8,16]{2,1,0:T(8,128)S(1)}, s32[15,8,16]{2,1,0:T(8,128)}, u32[]{:S(2)}) copy-start(s32[15,8,16]{2,1,0:T(8,128)} %param.6) | copy-start | bytes 23044
  2.6 17.8 %copy-start.2 = (bf16[16,128,128]{2,1,0:T(8,128)(2,1)S(1)}, bf16[16,128,128]{2,1,0:T(8,128)(2,1)}, u32[]{:S(2)}) copy-start(bf16[16,128,128]{2,1,0:T(8,128)(2,1)} %param.4) | copy-start | bytes 1572868
  5.6 23.3 %collective-permute-start.1 = (f32[16,128,113]{1,0,2:T(8,128)}, f32[16,128,113]{1,0,2:T(8,128)}, u32[]{:S(2)}, u32[]{:S(2)}) collective-permute-start(f32[16,128,113]{1,0,2:T(8,128)} %fusion.149), channel_id=1, source_target_pairs={{0,32},{32,0},{1,33},{33,1},{2,34},{34,2},{3,35},{35,3},{4,36},{36... | collective-permute-start | bytes 2777096 | tf_op jit(solution)/shard_map/ppermute | solution.py:74
  7.9 17.1 %collective-permute-start = (bf16[17,15,128]{2,0,1:T(8,128)(2,1)S(1)}, bf16[17,15,128]{2,0,1:T(8,128)(2,1)S(1)}, u32[]{:S(2)}, u32[]{:S(2)}) collective-permute-start(bf16[17,15,128]{2,0,1:T(8,128)(2,1)S(1)} %pad_maximum_fusion.2), channel_id=1, source_target_pairs={{1,0},{2,1},{3,2},{4,3},{5,4},{6,5},{7,6},{8,7},{9,8},{10,9},{11,1... | collective-permute-start | bytes 195848 | tf_op jit(solution)/shard_map/ppermute | solution.py:32
  25.4 3.2 %collective-permute-start.2 = (f32[16,128,15]{1,0,2:T(8,128)S(1)}, f32[16,128,15]{1,0,2:T(8,128)S(1)}, u32[]{:S(2)}, u32[]{:S(2)}) collective-permute-start(f32[16,128,15]{1,0,2:T(8,128)S(1)} %fusion.140), channel_id=1, source_target_pairs={{0,32},{32,0},{1,33},{33,1},{2,34},{34,2},{3,35},{35,3},{4,36},{36... | collective-permute-start | bytes 368648 | tf_op jit(solution)/shard_map/ppermute | solution.py:75
  31.5 7.2 %copy-start.3 = (s32[15,2]{0,1:T(2,128)S(1)}, s32[15,2]{0,1:T(2,128)}, u32[]{:S(2)}) copy-start(s32[15,2]{0,1:T(2,128)} %param.7) | copy-start | bytes 364
  33.3 6.6 %slice-start = ((s32[15,2]{0,1:T(2,128)}), s32[15,1]{0,1:T(1,128)S(1)}, s32[]{:S(2)}) async-start(s32[15,2]{0,1:T(2,128)} %param.7), calls=%async_computation.1 | async-start | bytes 1024 | tf_op jit(solution)/shard_map/slice | solution.py:91
  34.4 20.4 %all-to-all-start = ((f32[16,8,16,128]{3,2,0,1:T(8,128)}), f32[16,8,16,128]{3,2,0,1:T(8,128)S(1)}, u32[]{:S(2)}, u32[]{:S(2)}) async-start(f32[16,8,16,128]{3,2,0,1:T(8,128)} %copy.59), calls=%async_computation | async-start | bytes 2097152 | tf_op jit(solution)/shard_map/all_to_all | solution.py:79
  55.1 9.6 %collective-permute-start.3 = (f32[8824]{0:T(1024)S(1)}, f32[8824]{0:T(1024)S(1)}, u32[]{:S(2)}, u32[]{:S(2)}) collective-permute-start(f32[8824]{0:T(1024)S(1)} %pad_maximum_fusion.5), channel_id=1, source_target_pairs={{0,1},{1,2},{2,3},{3,4},{4,5},{5,6},{6,7},{7,8},{8,9},{9,10},{10,1... | collective-permute-start | bytes 105896 | tf_op jit(solution)/shard_map/ppermute | solution.py:27
  57.0 12.1 %collective-permute-start.4 = (f32[16,16,34]{2,1,0:T(8,128)S(1)}, f32[16,16,34]{2,1,0:T(8,128)S(1)}, u32[]{:S(2)}, u32[]{:S(2)}) collective-permute-start(f32[16,16,34]{2,1,0:T(8,128)S(1)} %get-tuple-element.20), channel_id=1, source_target_pairs={{1,0},{2,1},{3,2},{4,3},{5,4},{6,5},{7,6},{8,7},{9,8},{10,9},{11,1... | collective-permute-start | bytes 104456 | tf_op jit(solution)/shard_map/ppermute | solution.py:32

commit v14 on v9

--- a/solution.py
+++ b/solution.py
@@ -81,10 +81,12 @@
 
     head = vol[..., :HALO]
     tail = vol[..., sample_rows - HALO :]
-    sent = jnp.concatenate([tail.reshape(-1), lag_f[:, :, -1].reshape(-1)])
-    got = from_left(sent, "tile")
-    left = got[: tail.size].reshape(tail.shape)
-    lag_prev = got[tail.size :].reshape(pairs_n, lines_n, 1)
+    last_lags = lag_f[:, :, -1].reshape(-1)
+    plane = tail.shape[1] * tail.shape[2]
+    last_lags = jnp.pad(last_lags, (0, plane - last_lags.size)).reshape((1,) + tail.shape[1:])
+    got = from_left(jnp.concatenate([tail, last_lags], axis=0), "tile")
+    left = got[:frames]
+    lag_prev = got[frames].reshape(-1)[: pairs_n * lines_n].reshape(pairs_n, lines_n, 1)
     padded = jnp.concatenate([left, vol, from_right(head, "tile")], axis=2)
 
     line_count = per_dev // 2

time: 78.8 us -> 78.7 us (level)
    ppermute x1, waiting for transfers between devices: 0.01 us -> 3.99 us  [from_left(): return lax.ppermute(block, axis, [(i, i + 1) for i in range(count - 1)])]
    ppermute x2, waiting for transfers between devices: 4.61 us -> 0.77 us  [from_right(): return lax.ppermute(block, axis, [(i + 1, i) for i in range(count - 1)])]
  transfers between devices with their start and end apart: 5 -> 5, of which waited for: 3 -> 4; matrix products, arithmetic and copies ran while one was open for 11% -> 11% of each run, Pallas kernels for 0% -> 0%
where the time goes in v14:
time: 78.7 us; the launch traced here: 78.3 us
  starting transfers between devices  28.1 us (36%)
  waiting for transfers between devices  18.8 us (24%)
  other arithmetic  17 us (22%)
  local copies, waits for them, and re-layouts  8.03 us (10%)
  matrix products  5.03 us (6%)
  between operations  1.38 us (2%)
    ppermute x2, starting transfers between devices, from_right(): return lax.ppermute(block, axis, [(i + 1, i) for i in range(count - 1)])  19.8 us
    all_to_all x1, waiting for transfers between devices, shards(): vol = lax.all_to_all(vol, ('cx', 'cy'), 1, 1, tiled=True).sum(axis=1)  14 us
    add x13, other arithmetic, window_sum(): values = values[..., :n] + values[..., width:width + n]  6.34 us
    conv_general_dilated x4, matrix products, beamform(): lax.conv_general_dilated(extended, weights, window_strides=(1,), padding=...  5.03 us
    all_to_all x1, starting transfers between devices, shards(): vol = lax.all_to_all(vol, ('cx', 'cy'), 1, 1, tiled=True).sum(axis=1)  4.42 us
    unnamed x32, other arithmetic  4.24 us
    ppermute x1, waiting for transfers between devices, from_left(): return lax.ppermute(block, axis, [(i, i + 1) for i in range(count - 1)])  3.99 us
    ppermute x1, starting transfers between devices, shards(): vol = vol_mine + lax.ppermute(vol_other, 'cc', [(0, 1), (1, 0)])  1.92 us
  transfers between devices with their start and end apart: 5, of which 4 were waited for; matrix products, arithmetic and copies ran while one was open for 11% of the time, Pallas kernels for 0%

profile of v14, /device:TPU:48, one launch (start us, length us, event | category | flops | bytes accessed | tf_op | source)
XLA Modules:
  0.0 78.3 jit_solution(6669515410892062487)
XLA Ops:
  0.6 1.0 %fusion.145 = bf16[15,8]{1,0:T(8,128)(2,1)S(1)} fusion(s32[15,8,16]{2,1,0:T(8,128)} %param.6), kind=kLoop, calls=%fused_computation.327 | loop fusion | flops 120 | bytes 720 | tf_op jit(solution)/shard_map/slice | solution.py:56
  1.8 0.9 %fusion.160 = (bf16[16,15,128]{2,1,0:T(8,128)(2,1)S(1)}, bf16[16,15,128]{2,1,0:T(8,128)(2,1)S(1)}) fusion(bf16[16,128,128]{2,1,0:T(8,128)(2,1)} %param.4), kind=kLoop, calls=%fused_computation.344 | loop fusion | bytes 245760 | tf_op jit(solution)/shard_map/slice | solution.py:64
  2.7 12.5 %collective-permute-start = (bf16[17,15,128]{2,0,1:T(8,128)(2,1)S(1)}, bf16[17,15,128]{2,0,1:T(8,128)(2,1)S(1)}, u32[]{:S(2)}, u32[]{:S(2)}) collective-permute-start(bf16[17,15,128]{2,0,1:T(8,128)(2,1)S(1)} %pad_maximum_fusion.4), channel_id=1, source_target_pairs={{1,0},{2,1},{3,2},{4,3},{5,4},{6,5},{7,6},{8,7},{9,8},{10,9},{11,1... | collective-permute-start | bytes 195848 | tf_op jit(solution)/shard_map/ppermute | solution.py:32
  15.2 1.6 %copy.48 = bf16[1,16,128,256]{2,3,1,0:T(8,128)(2,1)S(1)} copy(bf16[1,16,128,256]{3,2,1,0:T(8,128)(2,1)} %param.5) | data formatting | bytes 2097152 | tf_op args[1]
  16.9 0.2 constant_dynamic-slice_fusion.1
  17.1 2.1 %fusion.149 = f32[16,128,113]{1,0,2:T(8,128)S(1)} fusion(bf16[16,128,128]{1,2,0:T(8,128)(2,1)S(1)} %bitcast.516, bf16[16,128,128]{2,1,0:T(8,128)(2,1)S(1)} %copy-done.1), kind=kOutput, calls=%fused_computation.340 | convolution fusion | flops 947912704 | bytes 1974272 | tf_op jit(solution)/shard_map/conv_general_dilated | solution.py:36
  19.3 0.4 fusion.140
  19.8 1.9 %collective-permute-start.1 = (f32[16,128,128]{1,0,2:T(8,128)S(1)}, f32[16,128,128]{1,0,2:T(8,128)S(1)}, u32[]{:S(2)}, u32[]{:S(2)}) collective-permute-start(f32[16,128,128]{1,0,2:T(8,128)S(1)} %pad_maximum_fusion), channel_id=1, source_target_pairs={{0,32},{32,0},{1,33},{33,1},{2,34},{34,2},{3,35},{35,3},{4,36},{36... | collective-permute-start | bytes 3145736 | tf_op jit(solution)/shard_map/ppermute | solution.py:78
  21.7 2.1 %fusion.151 = f32[16,128,113]{1,0,2:T(8,128)S(1)} fusion(bf16[16,128,128]{1,2,0:T(8,128)(2,1)S(1)} %bitcast.514, bf16[16,128,128]{2,1,0:T(8,128)(2,1)S(1)} %copy-done.1), kind=kOutput, calls=%fused_computation.342 | convolution fusion | flops 947912704 | bytes 1974272 | tf_op jit(solution)/shard_map/conv_general_dilated | solution.py:36
  23.8 0.4 fusion.141
  24.5 0.4 copy.54
  24.9 1.1 %copy.55 = f32[16,8,16,128]{3,2,0,1:T(8,128)} copy(f32[16,8,16,128]{3,2,1,0:T(8,128)S(1)} %bitcast.512) | data formatting | bytes 2097152 | tf_op jit(solution)/shard_map/reshape | solution.py:79
  26.0 4.4 %all-to-all-start = ((f32[16,8,16,128]{3,2,0,1:T(8,128)}), f32[16,8,16,128]{3,2,0,1:T(8,128)S(1)}, u32[]{:S(2)}, u32[]{:S(2)}) async-start(f32[16,8,16,128]{3,2,0,1:T(8,128)} %copy.55), calls=%async_computation | async-start | bytes 2097152 | tf_op jit(solution)/shard_map/all_to_all | solution.py:80
  30.4 0.6 slice.586
  31.7 0.7 fusion.146
  32.7 14.0 %all-to-all-done = f32[16,8,16,128]{3,2,0,1:T(8,128)S(1)} async-done(((f32[16,8,16,128]{3,2,0,1:T(8,128)}), f32[16,8,16,128]{3,2,0,1:T(8,128)S(1)}, u32[]{:S(2)}, u32[]{:S(2)}) %all-to-all-start) | async-done | bytes 1048608 | tf_op jit(solution)/shard_map/all_to_all | solution.py:80
  46.9 1.9 %collective-permute-start.2 = (f32[17,16,34]{2,1,0:T(8,128)S(1)}, f32[17,16,34]{2,1,0:T(8,128)S(1)}, u32[]{:S(2)}, u32[]{:S(2)}) collective-permute-start(f32[17,16,34]{2,1,0:T(8,128)S(1)} %pad_maximum_fusion.2), channel_id=1, source_target_pairs={{0,1},{1,2},{2,3},{3,4},{4,5},{5,6},{6,7},{7,8},{8,9},{9,10},{10,1... | collective-permute-start | bytes 110984 | tf_op jit(solution)/shard_map/ppermute | solution.py:27
  48.9 7.3 %collective-permute-start.3 = (f32[16,16,34]{2,1,0:T(8,128)S(1)}, f32[16,16,34]{2,1,0:T(8,128)S(1)}, u32[]{:S(2)}, u32[]{:S(2)}) collective-permute-start(f32[16,16,34]{2,1,0:T(8,128)S(1)} %get-tuple-element.20), channel_id=1, source_target_pairs={{1,0},{2,1},{3,2},{4,3},{5,4},{6,5},{7,6},{8,7},{9,8},{10,9},{11,1... | collective-permute-start | bytes 104456 | tf_op jit(solution)/shard_map/ppermute | solution.py:32
  56.3 4.0 %collective-permute-done.2 = f32[17,16,34]{2,1,0:T(8,128)S(1)} collective-permute-done((f32[17,16,34]{2,1,0:T(8,128)S(1)}, f32[17,16,34]{2,1,0:T(8,128)S(1)}, u32[]{:S(2)}, u32[]{:S(2)}) %collective-permute-start.2) | collective-permute-done | bytes 37024 | tf_op jit(solution)/shard_map/ppermute | solution.py:27
  60.3 0.8 collective-permute-done.3
  61.2 0.6 gather_fusion
  62.0 0.2 fusion.163
  63.0 0.6 fusion.162
  68.2 1.1 %slice_add_fusion.4 = f32[33,15,8,162]{3,2,1,0:T(8,128)S(1)} fusion(f32[33,15,8,163]{3,2,1,0:T(8,128)S(1)} %fusion.42), kind=kLoop, calls=%fused_computation.5 | loop fusion | flops 641520 | bytes 7698240 | tf_op jit(solution)/shard_map/add | solution.py:20
  69.3 1.1 %slice_add_fusion.3 = f32[33,15,8,160]{3,2,1,0:T(8,128)S(1)} fusion(f32[33,15,8,162]{3,2,1,0:T(8,128)S(1)} %slice_add_fusion.4), kind=kLoop, calls=%fused_computation.4 | loop fusion | flops 633600 | bytes 7603200 | tf_op jit(solution)/shard_map/add | solution.py:20
  70.5 1.1 %slice_add_fusion.2 = f32[33,15,8,156]{3,2,1,0:T(8,128)S(1)} fusion(f32[33,15,8,160]{3,2,1,0:T(8,128)S(1)} %slice_add_fusion.3), kind=kLoop, calls=%fused_computation.3 | loop fusion | flops 617760 | bytes 7413120 | tf_op jit(solution)/shard_map/add | solution.py:20
  71.6 1.1 %slice_add_fusion.1 = f32[33,15,8,148]{3,2,1,0:T(8,128)S(1)} fusion(f32[33,15,8,156]{3,2,1,0:T(8,128)S(1)} %slice_add_fusion.2), kind=kLoop, calls=%fused_computation.2 | loop fusion | flops 586080 | bytes 7032960 | tf_op jit(solution)/shard_map/add | solution.py:20
  72.7 1.1 %slice_add_fusion = f32[33,15,8,132]{3,2,1,0:T(8,128)S(1)} fusion(f32[33,15,8,148]{3,2,1,0:T(8,128)S(1)} %slice_add_fusion.1), kind=kLoop, calls=%fused_computation.1 | loop fusion | flops 522720 | bytes 6272640 | tf_op jit(solution)/shard_map/add | solution.py:20
  74.4 1.5 %add_select_fusion = (f32[15,8,132]{2,1,0:T(8,128)S(1)}, f32[15,8,132]{2,1,0:T(8,128)S(1)}, f32[15,8,132]{2,1,0:T(8,128)S(1)}, f32[15,8,132]{2,1,0:T(8,128)S(1)}...) fusion(f32[15,8,2]{2,1,0:T(8,128)S(1)} %reshape.128, ...), kind=kLoop, calls=%fused_computation.299 | loop fusion | flops 3453120 | bytes 4878852 | tf_op jit(solution)/shard_map/jit(_where)/select_n | solution.py:136
  75.9 0.9 %maximum_maximum_fusion = f32[15,8,132]{2,1,0:T(8,128)S(1)} fusion(f32[15,8,132]{2,1,0:T(8,128)S(1)} %get-tuple-element.9, f32[15,8,164]{2,1,0:T(8,128)S(1)} %fusion.35, f32[33,15,8,132]{3,2,1,0:T(8,128)S(1)} %slice_add_fusion), kind=kLoop, calls=%fused_computation.300 | loop fusion | flops 1267200 | bytes 3548160 | tf_op jit(solution)/shard_map/max | solution.py:126
  76.8 0.7 fusion.142
  77.5 0.8 %slice_maximum_fusion = f32[15,8,128]{2,1,0:T(8,128)} fusion(f32[15,8,132]{2,1,0:T(8,128)S(1)} %get-tuple-element.8, f32[15,8,132]{2,1,0:T(8,128)S(1)} %get-tuple-element.7, f32[15,8,132]{2,1,0:T(8,128)S(1)} %get-tuple-element.6, f32[15,8,132]{2,1,0:T(8,128)S(1)} %get-tuple-element.5, f32[15,8,132]{2,1,0:T(8,128)S(1)} %get-tuple-element.4, ...), kind=kLoop, calls=%fused_computation.319 | loop fusion | flops 92160 | bytes 491520 | tf_op jit(solution)/shard_map/max | solution.py:126
  (93 shorter events, 7.7 us)
Async XLA Ops:
  0.6 16.5 %copy-start.1 = (bf16[16,128,128]{2,1,0:T(8,128)(2,1)S(1)}, bf16[16,128,128]{2,1,0:T(8,128)(2,1)}, u32[]{:S(2)}) copy-start(bf16[16,128,128]{2,1,0:T(8,128)(2,1)} %param.4) | copy-start | bytes 1572868
  2.7 16.5 %collective-permute-start = (bf16[17,15,128]{2,0,1:T(8,128)(2,1)S(1)}, bf16[17,15,128]{2,0,1:T(8,128)(2,1)S(1)}, u32[]{:S(2)}, u32[]{:S(2)}) collective-permute-start(bf16[17,15,128]{2,0,1:T(8,128)(2,1)S(1)} %pad_maximum_fusion.4), channel_id=1, source_target_pairs={{1,0},{2,1},{3,2},{4,3},{5,4},{6,5},{7,6},{8,7},{9,8},{10,9},{11,1... | collective-permute-start | bytes 195848 | tf_op jit(solution)/shard_map/ppermute | solution.py:32
  19.8 4.6 %collective-permute-start.1 = (f32[16,128,128]{1,0,2:T(8,128)S(1)}, f32[16,128,128]{1,0,2:T(8,128)S(1)}, u32[]{:S(2)}, u32[]{:S(2)}) collective-permute-start(f32[16,128,128]{1,0,2:T(8,128)S(1)} %pad_maximum_fusion), channel_id=1, source_target_pairs={{0,32},{32,0},{1,33},{33,1},{2,34},{34,2},{3,35},{35,3},{4,36},{36... | collective-permute-start | bytes 3145736 | tf_op jit(solution)/shard_map/ppermute | solution.py:78
  24.2 6.2 %copy-start = (s32[15,8,16]{2,1,0:T(8,128)S(1)}, s32[15,8,16]{2,1,0:T(8,128)}, u32[]{:S(2)}) copy-start(s32[15,8,16]{2,1,0:T(8,128)} %param.6) | copy-start | bytes 23044
  24.2 6.2 %copy-start.2 = (s32[15,2]{0,1:T(2,128)S(1)}, s32[15,2]{0,1:T(2,128)}, u32[]{:S(2)}) copy-start(s32[15,2]{0,1:T(2,128)} %param.7) | copy-start | bytes 364
  24.5 7.3 %slice-start = ((s32[15,2]{0,1:T(2,128)}), s32[15,1]{0,1:T(1,128)S(1)}, s32[]{:S(2)}) async-start(s32[15,2]{0,1:T(2,128)} %param.7), calls=%async_computation.1 | async-start | bytes 1024 | tf_op jit(solution)/shard_map/slice | solution.py:94
  26.0 20.8 %all-to-all-start = ((f32[16,8,16,128]{3,2,0,1:T(8,128)}), f32[16,8,16,128]{3,2,0,1:T(8,128)S(1)}, u32[]{:S(2)}, u32[]{:S(2)}) async-start(f32[16,8,16,128]{3,2,0,1:T(8,128)} %copy.55), calls=%async_computation | async-start | bytes 2097152 | tf_op jit(solution)/shard_map/all_to_all | solution.py:80
  46.9 13.3 %collective-permute-start.2 = (f32[17,16,34]{2,1,0:T(8,128)S(1)}, f32[17,16,34]{2,1,0:T(8,128)S(1)}, u32[]{:S(2)}, u32[]{:S(2)}) collective-permute-start(f32[17,16,34]{2,1,0:T(8,128)S(1)} %pad_maximum_fusion.2), channel_id=1, source_target_pairs={{0,1},{1,2},{2,3},{3,4},{4,5},{5,6},{6,7},{7,8},{8,9},{9,10},{10,1... | collective-permute-start | bytes 110984 | tf_op jit(solution)/shard_map/ppermute | solution.py:27
  48.9 12.2 %collective-permute-start.3 = (f32[16,16,34]{2,1,0:T(8,128)S(1)}, f32[16,16,34]{2,1,0:T(8,128)S(1)}, u32[]{:S(2)}, u32[]{:S(2)}) collective-permute-start(f32[16,16,34]{2,1,0:T(8,128)S(1)} %get-tuple-element.20), channel_id=1, source_target_pairs={{1,0},{2,1},{3,2},{4,3},{5,4},{6,5},{7,6},{8,7},{9,8},{10,9},{11,1... | collective-permute-start | bytes 104456 | tf_op jit(solution)/shard_map/ppermute | solution.py:32

commit v15 on v14

--- a/solution.py
+++ b/solution.py
@@ -53,13 +53,7 @@
     lag_f = peak_lags.astype(jnp.float32)
     pairs_n, lines_n, _ = peak_lags.shape
     rim = channel_data[:, : tap_count - 1, :]
-    first_lags = peak_lags[:, :, 0].astype(channel_data.dtype).reshape(-1)
-    plane = rim.shape[1] * rim.shape[2]
-    first_lags = jnp.pad(first_lags, (0, plane - first_lags.size)).reshape((1,) + rim.shape[1:])
-    got = from_right(jnp.concatenate([rim, first_lags], axis=0), "tile")
-    rim_rows = got[:frames]
-    lag_next = got[frames].reshape(-1)[: pairs_n * lines_n].astype(jnp.float32)
-    lag_next = lag_next.reshape(pairs_n, lines_n, 1)
+    rim_rows = from_right(rim, "tile")
     main_rows = sample_rows - tap_count + 1
     tail_rows = jnp.concatenate([channel_data[:, main_rows:, :], rim_rows], axis=1)
 
@@ -87,7 +81,12 @@
     got = from_left(jnp.concatenate([tail, last_lags], axis=0), "tile")
     left = got[:frames]
     lag_prev = got[frames].reshape(-1)[: pairs_n * lines_n].reshape(pairs_n, lines_n, 1)
-    padded = jnp.concatenate([left, vol, from_right(head, "tile")], axis=2)
+    first_lags = lag_f[:, :, 0].reshape(-1)
+    first_lags = jnp.pad(first_lags, (0, plane - first_lags.size)).reshape((1,) + head.shape[1:])
+    got = from_right(jnp.concatenate([head, first_lags], axis=0), "tile")
+    right = got[:frames]
+    lag_next = got[frames].reshape(-1)[: pairs_n * lines_n].reshape(pairs_n, lines_n, 1)
+    padded = jnp.concatenate([left, vol, right], axis=2)
 
     line_count = per_dev // 2
     pair_count = frame_pairs.shape[0]

time: 78.7 us -> 83 us (1.055)
  the two profiles are of different devices: /device:TPU:48 before, /device:TPU:40 now
where the time goes in v15:
time: 83 us; the launch traced here: 82.8 us
  starting transfers between devices  27.9 us (34%)
  waiting for transfers between devices  24.6 us (30%)
  other arithmetic  16 us (19%)
  local copies, waits for them, and re-layouts  7.89 us (10%)
  matrix products  5.04 us (6%)
  between operations  1.36 us (2%)
    ppermute x2, starting transfers between devices, from_right(): return lax.ppermute(block, axis, [(i + 1, i) for i in range(count - 1)])  18.1 us
    all_to_all x1, waiting for transfers between devices, shards(): vol = lax.all_to_all(vol, ('cx', 'cy'), 1, 1, tiled=True).sum(axis=1)  13.1 us
    ppermute x1, waiting for transfers between devices, from_left(): return lax.ppermute(block, axis, [(i, i + 1) for i in range(count - 1)])  10.9 us
    add x13, other arithmetic, window_sum(): values = values[..., :n] + values[..., width:width + n]  6.34 us
    all_to_all x1, starting transfers between devices, shards(): vol = lax.all_to_all(vol, ('cx', 'cy'), 1, 1, tiled=True).sum(axis=1)  5.75 us
    conv_general_dilated x4, matrix products, beamform(): lax.conv_general_dilated(extended, weights, window_strides=(1,), padding=...  5.04 us
    unnamed x32, other arithmetic  4.24 us
    ppermute x1, starting transfers between devices, from_left(): return lax.ppermute(block, axis, [(i, i + 1) for i in range(count - 1)])  2.1 us
  transfers between devices with their start and end apart: 5, of which 4 were waited for; matrix products, arithmetic and copies ran while one was open for 10% of the time, Pallas kernels for 0%

profile of v15, /device:TPU:40, one launch (start us, length us, event | category | flops | bytes accessed | tf_op | source)
XLA Modules:
  0.0 82.8 jit_solution(8632635331562485875)
XLA Ops:
  0.6 1.0 %fusion.159 = (bf16[16,15,128]{2,1,0:T(8,128)(2,1)S(1)}, bf16[16,15,128]{2,1,0:T(8,128)(2,1)S(1)}) fusion(bf16[16,128,128]{2,1,0:T(8,128)(2,1)} %param.4), kind=kLoop, calls=%fused_computation.341 | loop fusion | bytes 245760 | tf_op jit(solution)/shard_map/slice | solution.py:58
  1.6 11.6 %collective-permute-start = (bf16[16,15,128]{2,0,1:T(8,128)(2,1)S(1)}, bf16[16,15,128]{2,0,1:T(8,128)(2,1)S(1)}, u32[]{:S(2)}, u32[]{:S(2)}) collective-permute-start(bf16[16,15,128]{2,0,1:T(8,128)(2,1)S(1)} %copy.164), channel_id=1, source_target_pairs={{1,0},{2,1},{3,2},{4,3},{5,4},{6,5},{7,6},{8,7},{9,8},{10,9},{11,1... | collective-permute-start | bytes 184328 | tf_op jit(solution)/shard_map/ppermute | solution.py:32
  13.3 1.6 %copy.29 = bf16[1,16,128,256]{2,3,1,0:T(8,128)(2,1)S(1)} copy(bf16[1,16,128,256]{3,2,1,0:T(8,128)(2,1)} %param.5) | data formatting | bytes 2097152 | tf_op args[1]
  14.9 0.2 constant_dynamic-slice_fusion.1
  15.1 2.1 %fusion.148 = f32[16,128,113]{1,0,2:T(8,128)S(1)} fusion(bf16[16,128,128]{1,2,0:T(8,128)(2,1)S(1)} %bitcast.513, bf16[16,128,128]{2,1,0:T(8,128)(2,1)S(1)} %copy-done.1), kind=kOutput, calls=%fused_computation.337 | convolution fusion | flops 947912704 | bytes 1974272 | tf_op jit(solution)/shard_map/conv_general_dilated | solution.py:36
  17.3 0.4 fusion.140
  17.8 1.9 %collective-permute-start.1 = (f32[16,128,128]{1,0,2:T(8,128)S(1)}, f32[16,128,128]{1,0,2:T(8,128)S(1)}, u32[]{:S(2)}, u32[]{:S(2)}) collective-permute-start(f32[16,128,128]{1,0,2:T(8,128)S(1)} %pad_maximum_fusion), channel_id=1, source_target_pairs={{0,32},{32,0},{1,33},{33,1},{2,34},{34,2},{3,35},{35,3},{4,36},{36... | collective-permute-start | bytes 3145736 | tf_op jit(solution)/shard_map/ppermute | solution.py:72
  19.7 2.1 %fusion.150 = f32[16,128,113]{1,0,2:T(8,128)S(1)} fusion(bf16[16,128,128]{1,2,0:T(8,128)(2,1)S(1)} %bitcast.511, bf16[16,128,128]{2,1,0:T(8,128)(2,1)S(1)} %copy-done.1), kind=kOutput, calls=%fused_computation.339 | convolution fusion | flops 947912704 | bytes 1974272 | tf_op jit(solution)/shard_map/conv_general_dilated | solution.py:36
  21.8 0.4 fusion.141
  22.5 0.4 copy.34
  22.9 1.1 %copy.35 = f32[16,8,16,128]{3,2,0,1:T(8,128)} copy(f32[16,8,16,128]{3,2,1,0:T(8,128)S(1)} %bitcast.509) | data formatting | bytes 2097152 | tf_op jit(solution)/shard_map/reshape | solution.py:73
  24.0 5.8 %all-to-all-start = ((f32[16,8,16,128]{3,2,0,1:T(8,128)}), f32[16,8,16,128]{3,2,0,1:T(8,128)S(1)}, u32[]{:S(2)}, u32[]{:S(2)}) async-start(f32[16,8,16,128]{3,2,0,1:T(8,128)} %copy.35), calls=%async_computation | async-start | bytes 2097152 | tf_op jit(solution)/shard_map/all_to_all | solution.py:74
  29.7 0.6 slice.585
  31.0 0.7 fusion.145
  31.8 13.1 %all-to-all-done = f32[16,8,16,128]{3,2,0,1:T(8,128)S(1)} async-done(((f32[16,8,16,128]{3,2,0,1:T(8,128)}), f32[16,8,16,128]{3,2,0,1:T(8,128)S(1)}, u32[]{:S(2)}, u32[]{:S(2)}) %all-to-all-start) | async-done | bytes 1048608 | tf_op jit(solution)/shard_map/all_to_all | solution.py:74
  45.1 6.5 %collective-permute-start.3 = (f32[17,16,34]{2,1,0:T(8,128)S(1)}, f32[17,16,34]{2,1,0:T(8,128)S(1)}, u32[]{:S(2)}, u32[]{:S(2)}) collective-permute-start(f32[17,16,34]{2,1,0:T(8,128)S(1)} %pad_maximum_fusion.3), channel_id=1, source_target_pairs={{1,0},{2,1},{3,2},{4,3},{5,4},{6,5},{7,6},{8,7},{9,8},{10,9},{11,1... | collective-permute-start | bytes 110984 | tf_op jit(solution)/shard_map/ppermute | solution.py:32
  51.6 2.1 %collective-permute-start.2 = (f32[17,16,34]{2,1,0:T(8,128)S(1)}, f32[17,16,34]{2,1,0:T(8,128)S(1)}, u32[]{:S(2)}, u32[]{:S(2)}) collective-permute-start(f32[17,16,34]{2,1,0:T(8,128)S(1)} %pad_maximum_fusion.2), channel_id=1, source_target_pairs={{0,1},{1,2},{2,3},{3,4},{4,5},{5,6},{6,7},{7,8},{8,9},{9,10},{10,1... | collective-permute-start | bytes 110984 | tf_op jit(solution)/shard_map/ppermute | solution.py:27
  53.7 0.2 copy.44
  53.9 0.5 collective-permute-done.3
  54.4 10.9 %collective-permute-done.2 = f32[17,16,34]{2,1,0:T(8,128)S(1)} collective-permute-done((f32[17,16,34]{2,1,0:T(8,128)S(1)}, f32[17,16,34]{2,1,0:T(8,128)S(1)}, u32[]{:S(2)}, u32[]{:S(2)}) %collective-permute-start.2) | collective-permute-done | bytes 37024 | tf_op jit(solution)/shard_map/ppermute | solution.py:27
  65.5 0.6 gather_fusion
  66.3 0.2 fusion.162
  67.4 0.6 fusion.161
  72.6 1.1 %slice_add_fusion.4 = f32[33,15,8,162]{3,2,1,0:T(8,128)S(1)} fusion(f32[33,15,8,163]{3,2,1,0:T(8,128)S(1)} %fusion.42), kind=kLoop, calls=%fused_computation.5 | loop fusion | flops 641520 | bytes 7698240 | tf_op jit(solution)/shard_map/add | solution.py:20
  73.8 1.1 %slice_add_fusion.3 = f32[33,15,8,160]{3,2,1,0:T(8,128)S(1)} fusion(f32[33,15,8,162]{3,2,1,0:T(8,128)S(1)} %slice_add_fusion.4), kind=kLoop, calls=%fused_computation.4 | loop fusion | flops 633600 | bytes 7603200 | tf_op jit(solution)/shard_map/add | solution.py:20
  74.9 1.1 %slice_add_fusion.2 = f32[33,15,8,156]{3,2,1,0:T(8,128)S(1)} fusion(f32[33,15,8,160]{3,2,1,0:T(8,128)S(1)} %slice_add_fusion.3), kind=kLoop, calls=%fused_computation.3 | loop fusion | flops 617760 | bytes 7413120 | tf_op jit(solution)/shard_map/add | solution.py:20
  76.0 1.1 %slice_add_fusion.1 = f32[33,15,8,148]{3,2,1,0:T(8,128)S(1)} fusion(f32[33,15,8,156]{3,2,1,0:T(8,128)S(1)} %slice_add_fusion.2), kind=kLoop, calls=%fused_computation.2 | loop fusion | flops 586080 | bytes 7032960 | tf_op jit(solution)/shard_map/add | solution.py:20
  77.1 1.1 %slice_add_fusion = f32[33,15,8,132]{3,2,1,0:T(8,128)S(1)} fusion(f32[33,15,8,148]{3,2,1,0:T(8,128)S(1)} %slice_add_fusion.1), kind=kLoop, calls=%fused_computation.1 | loop fusion | flops 522720 | bytes 6272640 | tf_op jit(solution)/shard_map/add | solution.py:20
  78.8 1.5 %add_select_fusion = (f32[15,8,132]{2,1,0:T(8,128)S(1)}, f32[15,8,132]{2,1,0:T(8,128)S(1)}, f32[15,8,132]{2,1,0:T(8,128)S(1)}, f32[15,8,132]{2,1,0:T(8,128)S(1)}...) fusion(f32[15,8,2]{2,1,0:T(8,128)S(1)} %reshape.121, ...), kind=kLoop, calls=%fused_computation.300 | loop fusion | flops 3453120 | bytes 4878852 | tf_op jit(solution)/shard_map/jit(_where)/select_n | solution.py:135
  80.3 0.9 %maximum_maximum_fusion = f32[15,8,132]{2,1,0:T(8,128)S(1)} fusion(f32[15,8,132]{2,1,0:T(8,128)S(1)} %get-tuple-element.11, f32[15,8,164]{2,1,0:T(8,128)S(1)} %fusion.35, f32[33,15,8,132]{3,2,1,0:T(8,128)S(1)} %slice_add_fusion), kind=kLoop, calls=%fused_computation.301 | loop fusion | flops 1267200 | bytes 3548160 | tf_op jit(solution)/shard_map/max | solution.py:125
  81.2 0.7 fusion.142
  81.9 0.8 slice_maximum_fusion
  (89 shorter events, 7.4 us)
Async XLA Ops:
  0.6 14.5 %copy-start.1 = (bf16[16,128,128]{2,1,0:T(8,128)(2,1)S(1)}, bf16[16,128,128]{2,1,0:T(8,128)(2,1)}, u32[]{:S(2)}) copy-start(bf16[16,128,128]{2,1,0:T(8,128)(2,1)} %param.4) | copy-start | bytes 1572868
  1.6 15.6 %collective-permute-start = (bf16[16,15,128]{2,0,1:T(8,128)(2,1)S(1)}, bf16[16,15,128]{2,0,1:T(8,128)(2,1)S(1)}, u32[]{:S(2)}, u32[]{:S(2)}) collective-permute-start(bf16[16,15,128]{2,0,1:T(8,128)(2,1)S(1)} %copy.164), channel_id=1, source_target_pairs={{1,0},{2,1},{3,2},{4,3},{5,4},{6,5},{7,6},{8,7},{9,8},{10,9},{11,1... | collective-permute-start | bytes 184328 | tf_op jit(solution)/shard_map/ppermute | solution.py:32
  17.8 4.6 %collective-permute-start.1 = (f32[16,128,128]{1,0,2:T(8,128)S(1)}, f32[16,128,128]{1,0,2:T(8,128)S(1)}, u32[]{:S(2)}, u32[]{:S(2)}) collective-permute-start(f32[16,128,128]{1,0,2:T(8,128)S(1)} %pad_maximum_fusion), channel_id=1, source_target_pairs={{0,32},{32,0},{1,33},{33,1},{2,34},{34,2},{3,35},{35,3},{4,36},{36... | collective-permute-start | bytes 3145736 | tf_op jit(solution)/shard_map/ppermute | solution.py:72
  22.2 7.5 %copy-start.2 = (s32[15,2]{0,1:T(2,128)S(1)}, s32[15,2]{0,1:T(2,128)}, u32[]{:S(2)}) copy-start(s32[15,2]{0,1:T(2,128)} %param.7) | copy-start | bytes 364
  22.2 8.1 %copy-start = (s32[15,8,16]{2,1,0:T(8,128)S(1)}, s32[15,8,16]{2,1,0:T(8,128)}, u32[]{:S(2)}) copy-start(s32[15,8,16]{2,1,0:T(8,128)} %param.6) | copy-start | bytes 23044
  22.5 8.5 %slice-start = ((s32[15,2]{0,1:T(2,128)}), s32[15,1]{0,1:T(1,128)S(1)}, s32[]{:S(2)}) async-start(s32[15,2]{0,1:T(2,128)} %param.7), calls=%async_computation.1 | async-start | bytes 1024 | tf_op jit(solution)/shard_map/slice | solution.py:93
  24.0 20.9 %all-to-all-start = ((f32[16,8,16,128]{3,2,0,1:T(8,128)}), f32[16,8,16,128]{3,2,0,1:T(8,128)S(1)}, u32[]{:S(2)}, u32[]{:S(2)}) async-start(f32[16,8,16,128]{3,2,0,1:T(8,128)} %copy.35), calls=%async_computation | async-start | bytes 2097152 | tf_op jit(solution)/shard_map/all_to_all | solution.py:74
  45.1 9.3 %collective-permute-start.3 = (f32[17,16,34]{2,1,0:T(8,128)S(1)}, f32[17,16,34]{2,1,0:T(8,128)S(1)}, u32[]{:S(2)}, u32[]{:S(2)}) collective-permute-start(f32[17,16,34]{2,1,0:T(8,128)S(1)} %pad_maximum_fusion.3), channel_id=1, source_target_pairs={{1,0},{2,1},{3,2},{4,3},{5,4},{6,5},{7,6},{8,7},{9,8},{10,9},{11,1... | collective-permute-start | bytes 110984 | tf_op jit(solution)/shard_map/ppermute | solution.py:32
  51.6 13.7 %collective-permute-start.2 = (f32[17,16,34]{2,1,0:T(8,128)S(1)}, f32[17,16,34]{2,1,0:T(8,128)S(1)}, u32[]{:S(2)}, u32[]{:S(2)}) collective-permute-start(f32[17,16,34]{2,1,0:T(8,128)S(1)} %pad_maximum_fusion.2), channel_id=1, source_target_pairs={{0,1},{1,2},{2,3},{3,4},{4,5},{5,6},{6,7},{7,8},{8,9},{9,10},{10,1... | collective-permute-start | bytes 110984 | tf_op jit(solution)/shard_map/ppermute | solution.py:27

commit v16 on v14

--- a/solution.py
+++ b/solution.py
@@ -52,7 +52,7 @@
 
     lag_f = peak_lags.astype(jnp.float32)
     pairs_n, lines_n, _ = peak_lags.shape
-    rim = channel_data[:, : tap_count - 1, :]
+    rim = channel_data[:, :tap_count, :]
     first_lags = peak_lags[:, :, 0].astype(channel_data.dtype).reshape(-1)
     plane = rim.shape[1] * rim.shape[2]
     first_lags = jnp.pad(first_lags, (0, plane - first_lags.size)).reshape((1,) + rim.shape[1:])
@@ -61,7 +61,7 @@
     lag_next = got[frames].reshape(-1)[: pairs_n * lines_n].astype(jnp.float32)
     lag_next = lag_next.reshape(pairs_n, lines_n, 1)
     main_rows = sample_rows - tap_count + 1
-    tail_rows = jnp.concatenate([channel_data[:, main_rows:, :], rim_rows], axis=1)
+    tail_rows = jnp.concatenate([channel_data[:, main_rows:, :], rim_rows[:, : tap_count - 1]], axis=1)
 
     weights = delay_weights[0]
     taps, cin, cols = weights.shape

time: 78.7 us -> 78.9 us (level)
    slice x1, local copies, waits for them, and re-layouts: 0.9 us -> 0.02 us  [shards(): channel_data[:, main_rows:, :]]
    slice x1 -> x2, local copies, waits for them, and re-layouts: 0.01 us -> 0.86 us  [the longest x1 0.85 us: shards(): rim = channel_data[:, :tap_count, :]]
  transfers between devices with their start and end apart: 5 -> 5, of which waited for: 4 -> 5; matrix products, arithmetic and copies ran while one was open for 11% -> 11% of each run, Pallas kernels for 0% -> 0%
where the time goes in v16:
time: 78.9 us; the launch traced here: 78.6 us
  starting transfers between devices  28.2 us (36%)
  waiting for transfers between devices  18.9 us (24%)
  other arithmetic  17 us (22%)
  local copies, waits for them, and re-layouts  8 us (10%)
  matrix products  5.02 us (6%)
  between operations  1.37 us (2%)
    ppermute x2, starting transfers between devices, from_right(): return lax.ppermute(block, axis, [(i + 1, i) for i in range(count - 1)])  20.1 us
    all_to_all x1, waiting for transfers between devices, shards(): vol = lax.all_to_all(vol, ('cx', 'cy'), 1, 1, tiled=True).sum(axis=1)  14 us
    add x13, other arithmetic, window_sum(): values = values[..., :n] + values[..., width:width + n]  6.34 us
    conv_general_dilated x4, matrix products, beamform(): lax.conv_general_dilated(extended, weights, window_strides=(1,), padding=...  5.02 us
    all_to_all x1, starting transfers between devices, shards(): vol = lax.all_to_all(vol, ('cx', 'cy'), 1, 1, tiled=True).sum(axis=1)  4.33 us
    unnamed x32, other arithmetic  4.24 us
    ppermute x1, waiting for transfers between devices, from_left(): return lax.ppermute(block, axis, [(i, i + 1) for i in range(count - 1)])  3.99 us
    ppermute x1, starting transfers between devices, shards(): vol = vol_mine + lax.ppermute(vol_other, 'cc', [(0, 1), (1, 0)])  1.92 us
  transfers between devices with their start and end apart: 5, of which 5 were waited for; matrix products, arithmetic and copies ran while one was open for 11% of the time, Pallas kernels for 0%

profile of v16, /device:TPU:48, one launch (start us, length us, event | category | flops | bytes accessed | tf_op | source)
XLA Modules:
  0.0 78.6 jit_solution(17003052856293361455)
XLA Ops:
  0.6 1.0 %fusion.145 = bf16[15,8]{1,0:T(8,128)(2,1)S(1)} fusion(s32[15,8,16]{2,1,0:T(8,128)} %param.6), kind=kLoop, calls=%fused_computation.327 | loop fusion | flops 120 | bytes 720 | tf_op jit(solution)/shard_map/slice | solution.py:56
  1.8 0.9 %slice.773 = bf16[16,16,128]{2,1,0:T(8,128)(2,1)S(1)} slice(bf16[16,128,128]{2,1,0:T(8,128)(2,1)} %param.4), slice={[0:16], [0:16], [0:128]} | slice | bytes 131072 | tf_op jit(solution)/shard_map/slice | solution.py:55
  2.6 12.5 %collective-permute-start = (bf16[17,16,128]{2,0,1:T(8,128)(2,1)S(1)}, bf16[17,16,128]{2,0,1:T(8,128)(2,1)S(1)}, u32[]{:S(2)}, u32[]{:S(2)}) collective-permute-start(bf16[17,16,128]{2,0,1:T(8,128)(2,1)S(1)} %pad_maximum_fusion.4), channel_id=1, source_target_pairs={{1,0},{2,1},{3,2},{4,3},{5,4},{6,5},{7,6},{8,7},{9,8},{10,9},{11,1... | collective-permute-start | bytes 208904 | tf_op jit(solution)/shard_map/ppermute | solution.py:32
  15.2 1.6 %copy.48 = bf16[1,16,128,256]{2,3,1,0:T(8,128)(2,1)S(1)} copy(bf16[1,16,128,256]{3,2,1,0:T(8,128)(2,1)} %param.5) | data formatting | bytes 2097152 | tf_op args[1]
  16.8 0.2 constant_dynamic-slice_fusion.1
  17.1 2.1 %fusion.149 = f32[16,128,113]{1,0,2:T(8,128)S(1)} fusion(bf16[16,128,128]{1,2,0:T(8,128)(2,1)S(1)} %bitcast.516, bf16[16,128,128]{2,1,0:T(8,128)(2,1)S(1)} %copy-done.1), kind=kOutput, calls=%fused_computation.340 | convolution fusion | flops 947912704 | bytes 1974272 | tf_op jit(solution)/shard_map/conv_general_dilated | solution.py:36
  19.3 0.4 fusion.140
  19.8 1.9 %collective-permute-start.1 = (f32[16,128,128]{1,0,2:T(8,128)S(1)}, f32[16,128,128]{1,0,2:T(8,128)S(1)}, u32[]{:S(2)}, u32[]{:S(2)}) collective-permute-start(f32[16,128,128]{1,0,2:T(8,128)S(1)} %pad_maximum_fusion), channel_id=1, source_target_pairs={{0,32},{32,0},{1,33},{33,1},{2,34},{34,2},{3,35},{35,3},{4,36},{36... | collective-permute-start | bytes 3145736 | tf_op jit(solution)/shard_map/ppermute | solution.py:78
  21.7 2.1 %fusion.151 = f32[16,128,113]{1,0,2:T(8,128)S(1)} fusion(bf16[16,128,128]{1,2,0:T(8,128)(2,1)S(1)} %bitcast.514, bf16[16,128,128]{2,1,0:T(8,128)(2,1)S(1)} %copy-done.1), kind=kOutput, calls=%fused_computation.342 | convolution fusion | flops 947912704 | bytes 1974272 | tf_op jit(solution)/shard_map/conv_general_dilated | solution.py:36
  23.9 0.4 fusion.141
  24.5 0.4 copy.54
  24.9 1.1 %copy.55 = f32[16,8,16,128]{3,2,0,1:T(8,128)} copy(f32[16,8,16,128]{3,2,1,0:T(8,128)S(1)} %bitcast.512) | data formatting | bytes 2097152 | tf_op jit(solution)/shard_map/reshape | solution.py:79
  26.0 4.3 %all-to-all-start = ((f32[16,8,16,128]{3,2,0,1:T(8,128)}), f32[16,8,16,128]{3,2,0,1:T(8,128)S(1)}, u32[]{:S(2)}, u32[]{:S(2)}) async-start(f32[16,8,16,128]{3,2,0,1:T(8,128)} %copy.55), calls=%async_computation | async-start | bytes 2097152 | tf_op jit(solution)/shard_map/all_to_all | solution.py:80
  30.4 0.6 slice.588
  31.7 0.7 fusion.146
  32.7 14.0 %all-to-all-done = f32[16,8,16,128]{3,2,0,1:T(8,128)S(1)} async-done(((f32[16,8,16,128]{3,2,0,1:T(8,128)}), f32[16,8,16,128]{3,2,0,1:T(8,128)S(1)}, u32[]{:S(2)}, u32[]{:S(2)}) %all-to-all-start) | async-done | bytes 1048608 | tf_op jit(solution)/shard_map/all_to_all | solution.py:80
  46.9 1.9 %collective-permute-start.2 = (f32[17,16,34]{2,1,0:T(8,128)S(1)}, f32[17,16,34]{2,1,0:T(8,128)S(1)}, u32[]{:S(2)}, u32[]{:S(2)}) collective-permute-start(f32[17,16,34]{2,1,0:T(8,128)S(1)} %pad_maximum_fusion.2), channel_id=1, source_target_pairs={{0,1},{1,2},{2,3},{3,4},{4,5},{5,6},{6,7},{7,8},{8,9},{9,10},{10,1... | collective-permute-start | bytes 110984 | tf_op jit(solution)/shard_map/ppermute | solution.py:27
  48.8 7.5 %collective-permute-start.3 = (f32[16,16,34]{2,1,0:T(8,128)S(1)}, f32[16,16,34]{2,1,0:T(8,128)S(1)}, u32[]{:S(2)}, u32[]{:S(2)}) collective-permute-start(f32[16,16,34]{2,1,0:T(8,128)S(1)} %get-tuple-element.18), channel_id=1, source_target_pairs={{1,0},{2,1},{3,2},{4,3},{5,4},{6,5},{7,6},{8,7},{9,8},{10,9},{11,1... | collective-permute-start | bytes 104456 | tf_op jit(solution)/shard_map/ppermute | solution.py:32
  56.5 4.0 %collective-permute-done.2 = f32[17,16,34]{2,1,0:T(8,128)S(1)} collective-permute-done((f32[17,16,34]{2,1,0:T(8,128)S(1)}, f32[17,16,34]{2,1,0:T(8,128)S(1)}, u32[]{:S(2)}, u32[]{:S(2)}) %collective-permute-start.2) | collective-permute-done | bytes 37024 | tf_op jit(solution)/shard_map/ppermute | solution.py:27
  60.5 0.8 collective-permute-done.3
  61.4 0.6 gather_fusion
  62.2 0.2 fusion.162
  63.2 0.6 fusion.161
  68.4 1.1 %slice_add_fusion.4 = f32[33,15,8,162]{3,2,1,0:T(8,128)S(1)} fusion(f32[33,15,8,163]{3,2,1,0:T(8,128)S(1)} %fusion.42), kind=kLoop, calls=%fused_computation.5 | loop fusion | flops 641520 | bytes 7698240 | tf_op jit(solution)/shard_map/add | solution.py:20
  69.6 1.1 %slice_add_fusion.3 = f32[33,15,8,160]{3,2,1,0:T(8,128)S(1)} fusion(f32[33,15,8,162]{3,2,1,0:T(8,128)S(1)} %slice_add_fusion.4), kind=kLoop, calls=%fused_computation.4 | loop fusion | flops 633600 | bytes 7603200 | tf_op jit(solution)/shard_map/add | solution.py:20
  70.7 1.1 %slice_add_fusion.2 = f32[33,15,8,156]{3,2,1,0:T(8,128)S(1)} fusion(f32[33,15,8,160]{3,2,1,0:T(8,128)S(1)} %slice_add_fusion.3), kind=kLoop, calls=%fused_computation.3 | loop fusion | flops 617760 | bytes 7413120 | tf_op jit(solution)/shard_map/add | solution.py:20
  71.8 1.1 %slice_add_fusion.1 = f32[33,15,8,148]{3,2,1,0:T(8,128)S(1)} fusion(f32[33,15,8,156]{3,2,1,0:T(8,128)S(1)} %slice_add_fusion.2), kind=kLoop, calls=%fused_computation.2 | loop fusion | flops 586080 | bytes 7032960 | tf_op jit(solution)/shard_map/add | solution.py:20
  72.9 1.1 %slice_add_fusion = f32[33,15,8,132]{3,2,1,0:T(8,128)S(1)} fusion(f32[33,15,8,148]{3,2,1,0:T(8,128)S(1)} %slice_add_fusion.1), kind=kLoop, calls=%fused_computation.1 | loop fusion | flops 522720 | bytes 6272640 | tf_op jit(solution)/shard_map/add | solution.py:20
  74.6 1.5 %add_select_fusion = (f32[15,8,132]{2,1,0:T(8,128)S(1)}, f32[15,8,132]{2,1,0:T(8,128)S(1)}, f32[15,8,132]{2,1,0:T(8,128)S(1)}, f32[15,8,132]{2,1,0:T(8,128)S(1)}...) fusion(f32[15,8,2]{2,1,0:T(8,128)S(1)} %reshape.128, ...), kind=kLoop, calls=%fused_computation.299 | loop fusion | flops 3453120 | bytes 4878852 | tf_op jit(solution)/shard_map/jit(_where)/select_n | solution.py:136
  76.1 0.9 %maximum_maximum_fusion = f32[15,8,132]{2,1,0:T(8,128)S(1)} fusion(f32[15,8,132]{2,1,0:T(8,128)S(1)} %get-tuple-element.9, f32[15,8,164]{2,1,0:T(8,128)S(1)} %fusion.35, f32[33,15,8,132]{3,2,1,0:T(8,128)S(1)} %slice_add_fusion), kind=kLoop, calls=%fused_computation.300 | loop fusion | flops 1267200 | bytes 3548160 | tf_op jit(solution)/shard_map/max | solution.py:126
  77.0 0.7 fusion.142
  77.7 0.8 %slice_maximum_fusion = f32[15,8,128]{2,1,0:T(8,128)} fusion(f32[15,8,132]{2,1,0:T(8,128)S(1)} %get-tuple-element.8, f32[15,8,132]{2,1,0:T(8,128)S(1)} %get-tuple-element.7, f32[15,8,132]{2,1,0:T(8,128)S(1)} %get-tuple-element.6, f32[15,8,132]{2,1,0:T(8,128)S(1)} %get-tuple-element.5, f32[15,8,132]{2,1,0:T(8,128)S(1)} %get-tuple-element.4, ...), kind=kLoop, calls=%fused_computation.319 | loop fusion | flops 92160 | bytes 491520 | tf_op jit(solution)/shard_map/max | solution.py:126
  (94 shorter events, 7.9 us)
Async XLA Ops:
  0.6 16.4 %copy-start.1 = (bf16[16,128,128]{2,1,0:T(8,128)(2,1)S(1)}, bf16[16,128,128]{2,1,0:T(8,128)(2,1)}, u32[]{:S(2)}) copy-start(bf16[16,128,128]{2,1,0:T(8,128)(2,1)} %param.4) | copy-start | bytes 1572868
  2.6 16.7 %collective-permute-start = (bf16[17,16,128]{2,0,1:T(8,128)(2,1)S(1)}, bf16[17,16,128]{2,0,1:T(8,128)(2,1)S(1)}, u32[]{:S(2)}, u32[]{:S(2)}) collective-permute-start(bf16[17,16,128]{2,0,1:T(8,128)(2,1)S(1)} %pad_maximum_fusion.4), channel_id=1, source_target_pairs={{1,0},{2,1},{3,2},{4,3},{5,4},{6,5},{7,6},{8,7},{9,8},{10,9},{11,1... | collective-permute-start | bytes 208904 | tf_op jit(solution)/shard_map/ppermute | solution.py:32
  19.8 4.6 %collective-permute-start.1 = (f32[16,128,128]{1,0,2:T(8,128)S(1)}, f32[16,128,128]{1,0,2:T(8,128)S(1)}, u32[]{:S(2)}, u32[]{:S(2)}) collective-permute-start(f32[16,128,128]{1,0,2:T(8,128)S(1)} %pad_maximum_fusion), channel_id=1, source_target_pairs={{0,32},{32,0},{1,33},{33,1},{2,34},{34,2},{3,35},{35,3},{4,36},{36... | collective-permute-start | bytes 3145736 | tf_op jit(solution)/shard_map/ppermute | solution.py:78
  24.3 6.1 %copy-start = (s32[15,8,16]{2,1,0:T(8,128)S(1)}, s32[15,8,16]{2,1,0:T(8,128)}, u32[]{:S(2)}) copy-start(s32[15,8,16]{2,1,0:T(8,128)} %param.6) | copy-start | bytes 23044
  24.3 6.1 %copy-start.2 = (s32[15,2]{0,1:T(2,128)S(1)}, s32[15,2]{0,1:T(2,128)}, u32[]{:S(2)}) copy-start(s32[15,2]{0,1:T(2,128)} %param.7) | copy-start | bytes 364
  24.5 7.2 %slice-start = ((s32[15,2]{0,1:T(2,128)}), s32[15,1]{0,1:T(1,128)S(1)}, s32[]{:S(2)}) async-start(s32[15,2]{0,1:T(2,128)} %param.7), calls=%async_computation.1 | async-start | bytes 1024 | tf_op jit(solution)/shard_map/slice | solution.py:94
  26.0 20.7 %all-to-all-start = ((f32[16,8,16,128]{3,2,0,1:T(8,128)}), f32[16,8,16,128]{3,2,0,1:T(8,128)S(1)}, u32[]{:S(2)}, u32[]{:S(2)}) async-start(f32[16,8,16,128]{3,2,0,1:T(8,128)} %copy.55), calls=%async_computation | async-start | bytes 2097152 | tf_op jit(solution)/shard_map/all_to_all | solution.py:80
  46.9 13.6 %collective-permute-start.2 = (f32[17,16,34]{2,1,0:T(8,128)S(1)}, f32[17,16,34]{2,1,0:T(8,128)S(1)}, u32[]{:S(2)}, u32[]{:S(2)}) collective-permute-start(f32[17,16,34]{2,1,0:T(8,128)S(1)} %pad_maximum_fusion.2), channel_id=1, source_target_pairs={{0,1},{1,2},{2,3},{3,4},{4,5},{5,6},{6,7},{7,8},{8,9},{9,10},{10,1... | collective-permute-start | bytes 110984 | tf_op jit(solution)/shard_map/ppermute | solution.py:27
  48.8 12.4 %collective-permute-start.3 = (f32[16,16,34]{2,1,0:T(8,128)S(1)}, f32[16,16,34]{2,1,0:T(8,128)S(1)}, u32[]{:S(2)}, u32[]{:S(2)}) collective-permute-start(f32[16,16,34]{2,1,0:T(8,128)S(1)} %get-tuple-element.18), channel_id=1, source_target_pairs={{1,0},{2,1},{3,2},{4,3},{5,4},{6,5},{7,6},{8,7},{9,8},{10,9},{11,1... | collective-permute-start | bytes 104456 | tf_op jit(solution)/shard_map/ppermute | solution.py:32

commit v17 on v14

--- a/solution.py
+++ b/solution.py
@@ -106,9 +106,9 @@
         [xr * yr[..., j : j + prod_len] + xi * yi[..., j : j + prod_len] for j in range(nlag)]
     )
     cross_sum = window_sum(prods)
-    power_a = window_sum(xr * xr + xi * xi) / (2 * WIN)
-    ey = yr * yr + yi * yi
-    power_full = window_sum(ey[..., : out_len + nlag - 1 + WIN - 1]) / (2 * WIN)
+    energy = window_sum(chain[:, :, 0] * chain[:, :, 0] + chain[:, :, 1] * chain[:, :, 1]) / (2 * WIN)
+    power_a = energy[:-1, :, WIN // 2 : WIN // 2 + out_len]
+    power_full = energy[1:, :, : out_len + nlag - 1]
     root_b = jnp.sqrt(power_full + epsilon)
     root_a = 2 * WIN * jnp.sqrt(power_a + epsilon)
 

time: 78.7 us -> 85 us (1.080)
  the two profiles are of different devices: /device:TPU:48 before, /device:TPU:40 now
where the time goes in v17:
time: 85 us; the launch traced here: 84.6 us
  starting transfers between devices  28.9 us (34%)
  waiting for transfers between devices  24.4 us (29%)
  other arithmetic  16.7 us (20%)
  local copies, waits for them, and re-layouts  8.21 us (10%)
  matrix products  5.03 us (6%)
  between operations  1.37 us (2%)
    ppermute x2, starting transfers between devices, from_right(): return lax.ppermute(block, axis, [(i + 1, i) for i in range(count - 1)])  19.1 us
    all_to_all x1, waiting for transfers between devices, shards(): vol = lax.all_to_all(vol, ('cx', 'cy'), 1, 1, tiled=True).sum(axis=1)  12.8 us
    ppermute x1, waiting for transfers between devices, from_left(): return lax.ppermute(block, axis, [(i, i + 1) for i in range(count - 1)])  11.5 us
    add x9, other arithmetic, window_sum(): values = values[..., :n] + values[..., width:width + n]  5.97 us
    all_to_all x1, starting transfers between devices, shards(): vol = lax.all_to_all(vol, ('cx', 'cy'), 1, 1, tiled=True).sum(axis=1)  5.76 us
    conv_general_dilated x4, matrix products, beamform(): lax.conv_general_dilated(extended, weights, window_strides=(1,), padding=...  5.03 us
    unnamed x32, other arithmetic  4.24 us
    ppermute x1, starting transfers between devices, from_left(): return lax.ppermute(block, axis, [(i, i + 1) for i in range(count - 1)])  2.1 us
  transfers between devices with their start and end apart: 5, of which 3 were waited for; matrix products, arithmetic and copies ran while one was open for 10% of the time, Pallas kernels for 0%

profile of v17, /device:TPU:40, one launch (start us, length us, event | category | flops | bytes accessed | tf_op | source)
XLA Modules:
  0.0 84.6 jit_solution(9788898835215551151)
XLA Ops:
  0.6 1.0 %fusion.143 = bf16[15,8]{1,0:T(8,128)(2,1)S(1)} fusion(s32[15,8,16]{2,1,0:T(8,128)} %param.6), kind=kLoop, calls=%fused_computation.322 | loop fusion | flops 120 | bytes 720 | tf_op jit(solution)/shard_map/slice | solution.py:56
  1.8 0.9 %fusion.157 = (bf16[16,15,128]{2,1,0:T(8,128)(2,1)S(1)}, bf16[16,15,128]{2,1,0:T(8,128)(2,1)S(1)}) fusion(bf16[16,128,128]{2,1,0:T(8,128)(2,1)} %param.4), kind=kLoop, calls=%fused_computation.339 | loop fusion | bytes 245760 | tf_op jit(solution)/shard_map/slice | solution.py:64
  2.7 11.6 %collective-permute-start = (bf16[17,15,128]{2,0,1:T(8,128)(2,1)S(1)}, bf16[17,15,128]{2,0,1:T(8,128)(2,1)S(1)}, u32[]{:S(2)}, u32[]{:S(2)}) collective-permute-start(bf16[17,15,128]{2,0,1:T(8,128)(2,1)S(1)} %pad_maximum_fusion.4), channel_id=1, source_target_pairs={{1,0},{2,1},{3,2},{4,3},{5,4},{6,5},{7,6},{8,7},{9,8},{10,9},{11,1... | collective-permute-start | bytes 195848 | tf_op jit(solution)/shard_map/ppermute | solution.py:32
  14.3 1.6 %copy.74 = bf16[1,16,128,256]{2,3,1,0:T(8,128)(2,1)S(1)} copy(bf16[1,16,128,256]{3,2,1,0:T(8,128)(2,1)} %param.5) | data formatting | bytes 2097152 | tf_op args[1]
  16.0 0.2 constant_dynamic-slice_fusion.1
  16.2 2.1 %fusion.147 = f32[16,128,113]{1,0,2:T(8,128)S(1)} fusion(bf16[16,128,128]{1,2,0:T(8,128)(2,1)S(1)} %bitcast.511, bf16[16,128,128]{2,1,0:T(8,128)(2,1)S(1)} %copy-done.1), kind=kOutput, calls=%fused_computation.335 | convolution fusion | flops 947912704 | bytes 1974272 | tf_op jit(solution)/shard_map/conv_general_dilated | solution.py:36
  18.4 0.4 fusion.138
  18.9 1.9 %collective-permute-start.1 = (f32[16,128,128]{1,0,2:T(8,128)S(1)}, f32[16,128,128]{1,0,2:T(8,128)S(1)}, u32[]{:S(2)}, u32[]{:S(2)}) collective-permute-start(f32[16,128,128]{1,0,2:T(8,128)S(1)} %pad_maximum_fusion), channel_id=1, source_target_pairs={{0,32},{32,0},{1,33},{33,1},{2,34},{34,2},{3,35},{35,3},{4,36},{36... | collective-permute-start | bytes 3145736 | tf_op jit(solution)/shard_map/ppermute | solution.py:78
  20.8 2.1 %fusion.149 = f32[16,128,113]{1,0,2:T(8,128)S(1)} fusion(bf16[16,128,128]{1,2,0:T(8,128)(2,1)S(1)} %bitcast.509, bf16[16,128,128]{2,1,0:T(8,128)(2,1)S(1)} %copy-done.1), kind=kOutput, calls=%fused_computation.337 | convolution fusion | flops 947912704 | bytes 1974272 | tf_op jit(solution)/shard_map/conv_general_dilated | solution.py:36
  22.9 0.4 fusion.139
  23.6 0.4 copy.80
  24.0 1.1 %copy.81 = f32[16,8,16,128]{3,2,0,1:T(8,128)} copy(f32[16,8,16,128]{3,2,1,0:T(8,128)S(1)} %bitcast.506) | data formatting | bytes 2097152 | tf_op jit(solution)/shard_map/reshape | solution.py:79
  25.1 5.8 %all-to-all-start = ((f32[16,8,16,128]{3,2,0,1:T(8,128)}), f32[16,8,16,128]{3,2,0,1:T(8,128)S(1)}, u32[]{:S(2)}, u32[]{:S(2)}) async-start(f32[16,8,16,128]{3,2,0,1:T(8,128)} %copy.81), calls=%async_computation | async-start | bytes 2097152 | tf_op jit(solution)/shard_map/all_to_all | solution.py:80
  30.8 0.6 slice.567
  32.0 0.2 copy.93
  32.2 0.7 fusion.144
  33.2 12.8 %all-to-all-done = f32[16,8,16,128]{3,2,0,1:T(8,128)S(1)} async-done(((f32[16,8,16,128]{3,2,0,1:T(8,128)}), f32[16,8,16,128]{3,2,0,1:T(8,128)S(1)}, u32[]{:S(2)}, u32[]{:S(2)}) %all-to-all-start) | async-done | bytes 1048608 | tf_op jit(solution)/shard_map/all_to_all | solution.py:80
  46.1 7.5 %collective-permute-start.3 = (f32[16,16,34]{2,1,0:T(8,128)S(1)}, f32[16,16,34]{2,1,0:T(8,128)S(1)}, u32[]{:S(2)}, u32[]{:S(2)}) collective-permute-start(f32[16,16,34]{2,1,0:T(8,128)S(1)} %get-tuple-element.21), channel_id=1, source_target_pairs={{1,0},{2,1},{3,2},{4,3},{5,4},{6,5},{7,6},{8,7},{9,8},{10,9},{11,1... | collective-permute-start | bytes 104456 | tf_op jit(solution)/shard_map/ppermute | solution.py:32
  53.6 2.1 %collective-permute-start.2 = (f32[17,16,34]{2,1,0:T(8,128)S(1)}, f32[17,16,34]{2,1,0:T(8,128)S(1)}, u32[]{:S(2)}, u32[]{:S(2)}) collective-permute-start(f32[17,16,34]{2,1,0:T(8,128)S(1)} %pad_maximum_fusion.2), channel_id=1, source_target_pairs={{0,1},{1,2},{2,3},{3,4},{4,5},{5,6},{6,7},{7,8},{8,9},{9,10},{10,1... | collective-permute-start | bytes 110984 | tf_op jit(solution)/shard_map/ppermute | solution.py:27
  55.8 11.5 %collective-permute-done.2 = f32[17,16,34]{2,1,0:T(8,128)S(1)} collective-permute-done((f32[17,16,34]{2,1,0:T(8,128)S(1)}, f32[17,16,34]{2,1,0:T(8,128)S(1)}, u32[]{:S(2)}, u32[]{:S(2)}) %collective-permute-start.2) | collective-permute-done | bytes 37024 | tf_op jit(solution)/shard_map/ppermute | solution.py:27
  67.6 0.6 gather_fusion
  69.4 0.6 fusion.160
  70.1 0.2 fusion.161
  74.9 1.1 %slice_add_fusion.4 = f32[33,15,8,162]{3,2,1,0:T(8,128)S(1)} fusion(f32[33,15,8,163]{3,2,1,0:T(8,128)S(1)} %fusion.41), kind=kLoop, calls=%fused_computation.5 | loop fusion | flops 641520 | bytes 7698240 | tf_op jit(solution)/shard_map/add | solution.py:20
  76.1 1.1 %slice_add_fusion.3 = f32[33,15,8,160]{3,2,1,0:T(8,128)S(1)} fusion(f32[33,15,8,162]{3,2,1,0:T(8,128)S(1)} %slice_add_fusion.4), kind=kLoop, calls=%fused_computation.4 | loop fusion | flops 633600 | bytes 7603200 | tf_op jit(solution)/shard_map/add | solution.py:20
  77.2 1.1 %slice_add_fusion.2 = f32[33,15,8,156]{3,2,1,0:T(8,128)S(1)} fusion(f32[33,15,8,160]{3,2,1,0:T(8,128)S(1)} %slice_add_fusion.3), kind=kLoop, calls=%fused_computation.3 | loop fusion | flops 617760 | bytes 7413120 | tf_op jit(solution)/shard_map/add | solution.py:20
  78.3 1.1 %slice_add_fusion.1 = f32[33,15,8,148]{3,2,1,0:T(8,128)S(1)} fusion(f32[33,15,8,156]{3,2,1,0:T(8,128)S(1)} %slice_add_fusion.2), kind=kLoop, calls=%fused_computation.2 | loop fusion | flops 586080 | bytes 7032960 | tf_op jit(solution)/shard_map/add | solution.py:20
  79.4 1.1 %slice_add_fusion = f32[33,15,8,132]{3,2,1,0:T(8,128)S(1)} fusion(f32[33,15,8,148]{3,2,1,0:T(8,128)S(1)} %slice_add_fusion.1), kind=kLoop, calls=%fused_computation.1 | loop fusion | flops 522720 | bytes 6272640 | tf_op jit(solution)/shard_map/add | solution.py:20
  80.6 0.9 %maximum_maximum_fusion = f32[15,8,132]{2,1,0:T(8,128)S(1)} fusion(f32[15,8,164]{2,1,0:T(8,128)S(1)} %fusion.36, f32[33,15,8,132]{3,2,1,0:T(8,128)S(1)} %slice_add_fusion, f32[16,8,165]{2,1,0:T(8,128)S(1)} %fusion), kind=kLoop, calls=%fused_computation.296 | loop fusion | flops 1298880 | bytes 3548160 | tf_op jit(solution)/shard_map/max | solution.py:126
  81.7 1.4 %add_select_fusion = (f32[15,8,132]{2,1,0:T(8,128)S(1)}, f32[15,8,132]{2,1,0:T(8,128)S(1)}, f32[15,8,132]{2,1,0:T(8,128)S(1)}, f32[15,8,132]{2,1,0:T(8,128)S(1)}...) fusion(f32[15,8,2]{2,1,0:T(8,128)S(1)} %reshape.134, ...), kind=kLoop, calls=%fused_computation.295 | loop fusion | flops 3421440 | bytes 4752132 | tf_op jit(solution)/shard_map/jit(_where)/select_n | solution.py:136
  83.1 0.7 fusion.140
  83.8 0.8 slice_maximum_fusion
  (91 shorter events, 7.5 us)
Async XLA Ops:
  0.6 15.6 %copy-start.1 = (bf16[16,128,128]{2,1,0:T(8,128)(2,1)S(1)}, bf16[16,128,128]{2,1,0:T(8,128)(2,1)}, u32[]{:S(2)}) copy-start(bf16[16,128,128]{2,1,0:T(8,128)(2,1)} %param.4) | copy-start | bytes 1572868
  2.7 15.6 %collective-permute-start = (bf16[17,15,128]{2,0,1:T(8,128)(2,1)S(1)}, bf16[17,15,128]{2,0,1:T(8,128)(2,1)S(1)}, u32[]{:S(2)}, u32[]{:S(2)}) collective-permute-start(bf16[17,15,128]{2,0,1:T(8,128)(2,1)S(1)} %pad_maximum_fusion.4), channel_id=1, source_target_pairs={{1,0},{2,1},{3,2},{4,3},{5,4},{6,5},{7,6},{8,7},{9,8},{10,9},{11,1... | collective-permute-start | bytes 195848 | tf_op jit(solution)/shard_map/ppermute | solution.py:32
  18.9 4.6 %collective-permute-start.1 = (f32[16,128,128]{1,0,2:T(8,128)S(1)}, f32[16,128,128]{1,0,2:T(8,128)S(1)}, u32[]{:S(2)}, u32[]{:S(2)}) collective-permute-start(f32[16,128,128]{1,0,2:T(8,128)S(1)} %pad_maximum_fusion), channel_id=1, source_target_pairs={{0,32},{32,0},{1,33},{33,1},{2,34},{34,2},{3,35},{35,3},{4,36},{36... | collective-permute-start | bytes 3145736 | tf_op jit(solution)/shard_map/ppermute | solution.py:78
  23.3 7.5 %copy-start.2 = (s32[15,2]{0,1:T(2,128)S(1)}, s32[15,2]{0,1:T(2,128)}, u32[]{:S(2)}) copy-start(s32[15,2]{0,1:T(2,128)} %param.7) | copy-start | bytes 364
  23.3 8.1 %copy-start = (s32[15,8,16]{2,1,0:T(8,128)S(1)}, s32[15,8,16]{2,1,0:T(8,128)}, u32[]{:S(2)}) copy-start(s32[15,8,16]{2,1,0:T(8,128)} %param.6) | copy-start | bytes 23044
  23.6 8.6 %slice-start = ((s32[15,2]{0,1:T(2,128)}), s32[15,1]{0,1:T(1,128)S(1)}, s32[]{:S(2)}) async-start(s32[15,2]{0,1:T(2,128)} %param.7), calls=%async_computation.1 | async-start | bytes 1024 | tf_op jit(solution)/shard_map/slice | solution.py:94
  25.1 20.9 %all-to-all-start = ((f32[16,8,16,128]{3,2,0,1:T(8,128)}), f32[16,8,16,128]{3,2,0,1:T(8,128)S(1)}, u32[]{:S(2)}, u32[]{:S(2)}) async-start(f32[16,8,16,128]{3,2,0,1:T(8,128)} %copy.81), calls=%async_computation | async-start | bytes 2097152 | tf_op jit(solution)/shard_map/all_to_all | solution.py:80
  46.1 21.2 %collective-permute-start.3 = (f32[16,16,34]{2,1,0:T(8,128)S(1)}, f32[16,16,34]{2,1,0:T(8,128)S(1)}, u32[]{:S(2)}, u32[]{:S(2)}) collective-permute-start(f32[16,16,34]{2,1,0:T(8,128)S(1)} %get-tuple-element.21), channel_id=1, source_target_pairs={{1,0},{2,1},{3,2},{4,3},{5,4},{6,5},{7,6},{8,7},{9,8},{10,9},{11,1... | collective-permute-start | bytes 104456 | tf_op jit(solution)/shard_map/ppermute | solution.py:32
  53.6 13.7 %collective-permute-start.2 = (f32[17,16,34]{2,1,0:T(8,128)S(1)}, f32[17,16,34]{2,1,0:T(8,128)S(1)}, u32[]{:S(2)}, u32[]{:S(2)}) collective-permute-start(f32[17,16,34]{2,1,0:T(8,128)S(1)} %pad_maximum_fusion.2), channel_id=1, source_target_pairs={{0,1},{1,2},{2,3},{3,4},{4,5},{5,6},{6,7},{7,8},{8,9},{9,10},{10,1... | collective-permute-start | bytes 110984 | tf_op jit(solution)/shard_map/ppermute | solution.py:27
